TPU v7x, 32 devices: a whole 2x2x4 slice. The times are simulated.
32 devices in a mesh: row: 4 (over z), col: 8 (over y, x, core).
Axes of the slice: x: 2, y: 2, z: 4, core: 2. Of those that a mesh axis runs over, the one named last changes fastest.
Arguments:
- positions: float32 [3, 4, 8, 64], P(None, 'row', 'col'), may hold values from 0 to 32, as said below
- species: int32 [4, 8, 64], P('row', 'col'), may hold values from 0 to 3
- descriptors: float32 [128, 4, 8, 64], P(None, 'row', 'col'), may hold values from -6 to 6
- readout: float32 [4, 128], replicated, may hold values from -0.5 to 0.5
- hardness: float32 [4], replicated, may hold values from 1 to 4
- widths: float32 [4], replicated, may hold values from 0.5 to 1.5
Outputs:
- charges: float32 [4, 8, 64], P('row', 'col')
- forces: float32 [3, 4, 8, 64], P(None, 'row', 'col')
Inputs may be any that keep to these rules, and one draw needn't show every extreme that they name: `positions`: the atoms of brick (b, c) lie in [4 b, 4 b + 4) x [4 c, 4 c + 4) x [0, 4); no two atoms are closer than 0.4.
All inputs are finite; a program needn't handle non-finite values.
Results may differ from a plain program's by a relative error of at most 0.0003.
Values sent between devices are 32-bit elements; how exact they have to be, the bound alone decides.
No kernel may reach another device: no remote copies, remote signals or barrier semaphores. Data moves between devices by JAX's collectives and lax.ppermute only.
A program may use at most 64 MiB of HBM per device.

v0:
```python
import jax
import jax.numpy as jnp
from jax import lax
from jax.sharding import PartitionSpec as P

ITERS = 3


ROOT_PI = 1.7724538509055159
TWO_ROOT = 1.1283791670955126


def screened(row_geometry, col_geometry, self_pair):
    squared = jnp.zeros(self_pair.shape, row_geometry.dtype)
    for axis_id in range(3):
        separation = row_geometry[axis_id][:, None] - col_geometry[axis_id][None, :]
        squared = squared + separation * separation
    squared = jnp.where(self_pair, 1.0, squared)
    inverse = lax.rsqrt(squared)
    screening = lax.rsqrt(2.0 * (row_geometry[3][:, None] + col_geometry[3][None, :]))
    return jnp.where(self_pair, 0.0, lax.erf(screening * squared * inverse) * inverse)


def pulling(row_geometry, col_geometry, self_pair, col_charges):
    separations = []
    squared = jnp.zeros(self_pair.shape, row_geometry.dtype)
    for axis_id in range(3):
        separation = row_geometry[axis_id][:, None] - col_geometry[axis_id][None, :]
        separations.append(separation)
        squared = squared + separation * separation
    squared = jnp.where(self_pair, 1.0, squared)
    inverse = lax.rsqrt(squared)
    screening = lax.rsqrt(2.0 * (row_geometry[3][:, None] + col_geometry[3][None, :]))
    slope = (
        (
            lax.erf(screening * squared * inverse) * inverse
            - TWO_ROOT * screening * jnp.exp(-screening * screening * squared)
        )
        * inverse
        * inverse
    )
    slope = jnp.where(self_pair, 0.0, slope) * col_charges[None, :]
    return jnp.stack(
        [
            jnp.sum(slope * separations[0], 1),
            jnp.sum(slope * separations[1], 1),
            jnp.sum(slope * separations[2], 1),
        ]
    )


def apply_kernel(row_geometry, col_geometry, self_pair, vectors):
    kernel = screened(row_geometry, col_geometry, self_pair)
    return jnp.sum(kernel[None, :, :] * vectors[:, None, :], 2)


def shards(positions, species, descriptors, readout, hardness, widths):
    per_brick = species.shape[-1]
    row_at = lax.axis_index("row")
    col_at = lax.axis_index("col")
    kind_range = jnp.arange(hardness.shape[0], dtype=jnp.int32)
    onehot = (kind_range[:, None] == species.reshape(1, per_brick)).astype(jnp.float32)
    hard_atom = jnp.sum(onehot * hardness[:, None], 0)
    width_atom = jnp.sum(onehot * widths[:, None], 0)
    features = descriptors.reshape(descriptors.shape[0], per_brick)
    atom_weights = jnp.zeros(features.shape, jnp.float32)
    for kind in range(hardness.shape[0]):
        atom_weights = atom_weights + onehot[kind][None, :] * readout[kind][:, None]
    negativity = jnp.sum(features * atom_weights, 0)
    self_term = hard_atom + 1.0 / (width_atom * ROOT_PI)
    own_geometry = jnp.concatenate(
        [positions, (width_atom * width_atom).reshape(1, 1, 1, per_brick)], 0
    )
    row_geometry = lax.all_gather(own_geometry, "col", axis=2, tiled=True).reshape(4, -1)
    col_geometry = lax.all_gather(own_geometry, "row", axis=1, tiled=True).reshape(4, -1)
    row_total = row_geometry.shape[1]
    block_rows = 512
    block_count = row_total // block_rows

    def pair_mask(row_index, col_index):
        same_slot = (
            row_index[:, None] - col_at * per_brick == col_index[None, :] - row_at * per_brick
        )
        return same_slot & (row_index[:, None] // per_brick == col_at)

    def sweep(segment, block_fn, rows_out):
        columns = segment.shape[-1]
        col_index = jnp.arange(columns, dtype=jnp.int32)

        def one_block(block):
            first_row = block * block_rows
            row_part = lax.dynamic_slice_in_dim(row_geometry, first_row, block_rows, 1)
            row_index = first_row + jnp.arange(block_rows, dtype=jnp.int32)
            return block_fn(row_part, col_geometry, pair_mask(row_index, col_index), segment)

        blocks = lax.map(one_block, jnp.arange(block_count, dtype=jnp.int32))
        return jnp.moveaxis(blocks, 0, 1).reshape(rows_out, row_total)

    def squares(resid):
        return lax.psum(jnp.sum(resid * resid, 1), ("row", "col"))

    rhs = jnp.stack([-negativity, jnp.ones((per_brick,), jnp.float32)])
    solution = jnp.zeros_like(rhs)
    resid = rhs
    direction = rhs
    norm_now = squares(resid)
    for iteration in range(ITERS):
        partial_value = sweep(lax.all_gather(direction, "row", axis=1, tiled=True), apply_kernel, 2)
        whole = lax.psum(partial_value, "col")
        mine = lax.dynamic_slice_in_dim(whole, col_at * per_brick, per_brick, 1)
        image = mine + self_term[None, :] * direction
        curvature = lax.psum(jnp.sum(direction * image, 1), ("row", "col"))
        step_size = norm_now / curvature
        solution = solution + step_size[:, None] * direction
        if iteration + 1 < ITERS:
            resid = resid - step_size[:, None] * image
            norm_next = squares(resid)
            direction = resid + (norm_next / norm_now)[:, None] * direction
            norm_now = norm_next
    totals = lax.psum(jnp.sum(solution, 1), ("row", "col"))
    lagrange = totals[0] / totals[1]
    charges = solution[0] - lagrange * solution[1]
    field_sums = jnp.zeros((3, row_total), jnp.float32) + sweep(
        lax.all_gather(charges, "row", axis=0, tiled=True), pulling, 3
    )
    whole_pull = lax.psum(field_sums, "col")
    mine_pull = lax.dynamic_slice_in_dim(whole_pull, col_at * per_brick, per_brick, 1)
    forces = (charges[None, :] * mine_pull).reshape(3, 1, 1, per_brick)
    return (charges.reshape(1, 1, per_brick), forces)


def solution(mesh):
    in_specs = (
        P(None, "row", "col", None),
        P("row", "col", None),
        P(None, "row", "col", None),
        P(),
        P(),
        P(),
    )
    out_specs = (P("row", "col", None), P(None, "row", "col", None))
    return jax.shard_map(shards, mesh=mesh, in_specs=in_specs, out_specs=out_specs, check_vma=False)
```

profile of v0, /device:TPU:0, one launch (start us, length us, event | category | flops | bytes accessed | tf_op | source)
XLA Modules:
  0.0 359.4 jit_solution(654294700805835680)
XLA Ops:
  0.7 0.6 copy-done.1
  1.4 0.7 copy-done.4
  2.1 10.4 %all_gather.18 = f32[4,1,8,64]{3,0,1,2:T(4,128)S(1)} all-gather(f32[4,1,1,64]{3,0,1,2:T(4,128)S(1)} %pad_maximum_fusion.1), channel_id=1, replica_groups=mesh['row'=4,'col'=8] {'col'}, dimensions={2}, use_global_device_ids=true | all-gather | bytes 9216 | tf_op jit(solution)/shard_map/all_gather | solution.py:74
  12.8 12.1 %all_gather.19 = f32[4,4,1,64]{3,0,2,1:T(4,128)S(1)} all-gather(f32[4,1,1,64]{3,0,2,1:T(4,128)S(1)} %fusion.29), channel_id=1, replica_groups=mesh['row'=4,'col'=8] {'row'}, dimensions={1}, use_global_device_ids=true | all-gather | bytes 5120 | tf_op jit(solution)/shard_map/all_gather | solution.py:75
  25.9 0.7 copy-done.2
  26.7 9.7 %all-gather.1 = f32[4,64,2]{1,2,0:T(2,128)S(1)} all-gather(f32[1,64,2]{1,2,0:T(2,128)S(1)} %pad_bitcast_fusion), channel_id=1, replica_groups=mesh['row'=4,'col'=8] {'row'}, dimensions={0}, use_global_device_ids=true | all-gather | bytes 2560 | tf_op jit(solution)/shard_map/all_gather | solution.py:108
  36.7 11.8 %psum.78 = f32[2,512]{1,0:T(2,128)S(1)} all-reduce(f32[2,512]{1,0:T(2,128)S(1)} %multiply_reduce_fusion.2), channel_id=1, replica_groups=mesh['row'=4,'col'=8] {'col'}, use_global_device_ids=true, to_apply=%region_5.6 | all-reduce | flops 1024 | bytes 8192 | tf_op jit(solution)/shard_map/psum | solution.py:109
  48.8 37.6 %all-reduce.2 = (f32[2]{0:T(128)S(1)}, f32[2]{0:T(128)S(1)}) all-reduce(f32[2]{0:T(128)S(1)} %get-tuple-element.86, f32[2]{0:T(128)S(1)} %get-tuple-element.85), channel_id=1, replica_groups=mesh['row'=4,'col'=8] {'row','col'}, use_global_device_ids=true, to_apply=%region_2.0 | all-reduce | flops 4 | bytes 32 | tf_op jit(solution)/shard_map/psum | solution.py:100
  86.6 41.6 %psum.80 = f32[2]{0:T(128)S(1)} all-reduce(f32[2]{0:T(128)S(1)} %get-tuple-element.113), channel_id=1, replica_groups=mesh['row'=4,'col'=8] {'row','col'}, use_global_device_ids=true, to_apply=%region_10.11 | all-reduce | flops 2 | bytes 16 | tf_op jit(solution)/shard_map/psum | solution.py:100
  128.3 9.1 %all-gather.2 = f32[4,64,2]{1,2,0:T(2,128)S(1)} all-gather(f32[1,64,2]{1,2,0:T(2,128)S(1)} %fusion.28), channel_id=1, replica_groups=mesh['row'=4,'col'=8] {'row'}, dimensions={0}, use_global_device_ids=true | all-gather | bytes 2560 | tf_op jit(solution)/shard_map/all_gather | solution.py:108
  137.7 11.8 %psum.81 = f32[2,512]{1,0:T(2,128)S(1)} all-reduce(f32[2,512]{1,0:T(2,128)S(1)} %multiply_reduce_fusion.1), channel_id=1, replica_groups=mesh['row'=4,'col'=8] {'col'}, use_global_device_ids=true, to_apply=%region_12.13 | all-reduce | flops 1024 | bytes 8192 | tf_op jit(solution)/shard_map/psum | solution.py:109
  149.7 38.5 %psum.82 = f32[2]{0:T(128)S(1)} all-reduce(f32[2]{0:T(128)S(1)} %multiply_reduce_fusion.5), channel_id=1, replica_groups=mesh['row'=4,'col'=8] {'row','col'}, use_global_device_ids=true, to_apply=%region_14.15 | all-reduce | flops 2 | bytes 16 | tf_op jit(solution)/shard_map/psum | solution.py:112
  188.4 41.5 %psum.83 = f32[2]{0:T(128)S(1)} all-reduce(f32[2]{0:T(128)S(1)} %get-tuple-element.103), channel_id=1, replica_groups=mesh['row'=4,'col'=8] {'row','col'}, use_global_device_ids=true, to_apply=%region_16.17 | all-reduce | flops 2 | bytes 16 | tf_op jit(solution)/shard_map/psum | solution.py:100
  230.0 9.1 %all-gather.3 = f32[4,64,2]{1,2,0:T(2,128)S(1)} all-gather(f32[1,64,2]{1,2,0:T(2,128)S(1)} %bitcast.57), channel_id=1, replica_groups=mesh['row'=4,'col'=8] {'row'}, dimensions={0}, use_global_device_ids=true | all-gather | bytes 2560 | tf_op jit(solution)/shard_map/all_gather | solution.py:108
  239.4 11.8 %psum.84 = f32[2,512]{1,0:T(2,128)S(1)} all-reduce(f32[2,512]{1,0:T(2,128)S(1)} %multiply_reduce_fusion), channel_id=1, replica_groups=mesh['row'=4,'col'=8] {'col'}, use_global_device_ids=true, to_apply=%region_18.19 | all-reduce | flops 1024 | bytes 8192 | tf_op jit(solution)/shard_map/psum | solution.py:109
  251.4 38.5 %psum.85 = f32[2]{0:T(128)S(1)} all-reduce(f32[2]{0:T(128)S(1)} %multiply_reduce_fusion.3), channel_id=1, replica_groups=mesh['row'=4,'col'=8] {'row','col'}, use_global_device_ids=true, to_apply=%region_20.21 | all-reduce | flops 2 | bytes 16 | tf_op jit(solution)/shard_map/psum | solution.py:112
  290.1 41.5 %psum.86 = f32[2]{0:T(128)S(1)} all-reduce(f32[2]{0:T(128)S(1)} %get-tuple-element.101), channel_id=1, replica_groups=mesh['row'=4,'col'=8] {'row','col'}, use_global_device_ids=true, to_apply=%region_22.23 | all-reduce | flops 2 | bytes 16 | tf_op jit(solution)/shard_map/psum | solution.py:120
  331.7 0.6 fusion.27
  333.6 0.6 copy-done.7
  334.2 0.6 dynamic-slice
  335.6 9.9 %all-reduce.1 = f32[256]{0:T(256)S(1)} all-reduce(f32[256]{0:T(256)S(1)} %get-tuple-element.99), channel_id=2, replica_groups=mesh['row'=4,'col'=8] {'row'}, use_global_device_ids=true, to_apply=%add.1 | all-reduce | flops 256 | bytes 2048
  345.5 1.2 fusion.3
  346.7 12.0 %psum.87 = f32[3,512]{1,0:T(4,128)S(1)} all-reduce(f32[3,512]{1,0:T(4,128)S(1)} %pad_maximum_fusion), channel_id=1, replica_groups=mesh['row'=4,'col'=8] {'col'}, use_global_device_ids=true, to_apply=%region_26.27 | all-reduce | flops 1536 | bytes 12288 | tf_op jit(solution)/shard_map/psum | solution.py:126
  358.8 0.6 reshape.327
  (63 shorter events, 4.0 us)
Async XLA Ops:
  0.6 0.7 copy-start.1
  0.6 0.7 copy-start.6
  0.7 0.7 copy-start.5
  1.4 0.7 copy-start.4
  25.3 1.2 copy-start
  25.8 0.7 copy-start.2
  333.6 0.7 copy-start.7
  335.6 23.2 %copy-start.3 = (f32[1,64]{1,0:T(1,128)}, f32[1,64]{1,0:T(1,128)S(1)}, u32[]{:S(2)}) copy-start(f32[1,64]{1,0:T(1,128)S(1)} %get-tuple-element.100) | copy-start | bytes 772
where the time goes:
time: 361 us; the launch traced here: 359 us
  blocking collectives  347 us (96%)
  local copies, waits for them, and re-layouts  5.38 us (1%)
  other arithmetic  4.18 us (1%)
    psum x3, blocking collectives, squares(): return lax.psum(jnp.sum(resid * resid, 1), ('row', 'col'))  121 us
    psum x2, blocking collectives, shards(): curvature = lax.psum(jnp.sum(direction * image, 1), ('row', 'col'))  77.1 us
    psum x1, blocking collectives, shards(): totals = lax.psum(jnp.sum(solution, 1), ('row', 'col'))  41.5 us
    psum x3, blocking collectives, shards(): whole = lax.psum(partial_value, 'col')  35.4 us
    all_gather x3, blocking collectives, shards(): lax.all_gather(direction, 'row', axis=1, tiled=True)  27.9 us
    all_gather x1, blocking collectives, shards(): lax.all_gather(own_geometry, 'row', axis=1, tiled=True).reshape(4, -1)  12.1 us
    psum x1, blocking collectives, shards(): whole_pull = lax.psum(field_sums, 'col')  12 us
    all_gather x1, blocking collectives, shards(): lax.all_gather(own_geometry, 'col', axis=2, tiled=True).reshape(4, -1)  10.4 us

commit v1 on v0

v1 whole, which is shorter than its diff:
```python
import jax
import jax.numpy as jnp
from jax import lax
from jax.sharding import PartitionSpec as P

ITERS = 3


ROOT_PI = 1.7724538509055159
TWO_ROOT = 1.1283791670955126

PAIR_LIMIT = 16 * 1024 * 1024


def screened(row_geometry, col_geometry, self_pair):
    squared = jnp.zeros(self_pair.shape, row_geometry.dtype)
    for axis_id in range(3):
        separation = row_geometry[axis_id][:, None] - col_geometry[axis_id][None, :]
        squared = squared + separation * separation
    squared = jnp.where(self_pair, 1.0, squared)
    inverse = lax.rsqrt(squared)
    screening = lax.rsqrt(2.0 * (row_geometry[3][:, None] + col_geometry[3][None, :]))
    off = lax.erf(screening * squared * inverse) * inverse
    return jnp.where(self_pair, row_geometry[5][:, None], off)


def pulling(row_geometry, col_geometry, self_pair, col_charges):
    separations = []
    squared = jnp.zeros(self_pair.shape, row_geometry.dtype)
    for axis_id in range(3):
        separation = row_geometry[axis_id][:, None] - col_geometry[axis_id][None, :]
        separations.append(separation)
        squared = squared + separation * separation
    squared = jnp.where(self_pair, 1.0, squared)
    inverse = lax.rsqrt(squared)
    screening = lax.rsqrt(2.0 * (row_geometry[3][:, None] + col_geometry[3][None, :]))
    slope = (
        (
            lax.erf(screening * squared * inverse) * inverse
            - TWO_ROOT * screening * jnp.exp(-screening * screening * squared)
        )
        * inverse
        * inverse
    )
    slope = jnp.where(self_pair, 0.0, slope) * col_charges[None, :]
    return jnp.stack(
        [
            jnp.sum(slope * separations[0], 1),
            jnp.sum(slope * separations[1], 1),
            jnp.sum(slope * separations[2], 1),
        ]
    )


def make_shards(rows, cols):
    devices = rows * cols
    everyone = ("row", "col")

    def gather_all(piece):
        spread = jnp.broadcast_to(piece[None], (devices,) + piece.shape)
        got = lax.all_to_all(spread, everyone, 0, 0, tiled=True)
        return jnp.moveaxis(got, 0, 1).reshape(piece.shape[0], -1)

    def shards(positions, species, descriptors, readout, hardness, widths):
        per_brick = species.shape[-1]
        atoms = devices * per_brick
        me = lax.axis_index("row") * cols + lax.axis_index("col")
        kind_range = jnp.arange(hardness.shape[0], dtype=jnp.int32)
        onehot = (kind_range[:, None] == species.reshape(1, per_brick)).astype(jnp.float32)
        hard_atom = jnp.sum(onehot * hardness[:, None], 0)
        width_atom = jnp.sum(onehot * widths[:, None], 0)
        features = descriptors.reshape(descriptors.shape[0], per_brick)
        atom_weights = jnp.zeros(features.shape, jnp.float32)
        for kind in range(hardness.shape[0]):
            atom_weights = atom_weights + onehot[kind][None, :] * readout[kind][:, None]
        negativity = jnp.sum(features * atom_weights, 0)
        self_term = hard_atom + 1.0 / (width_atom * ROOT_PI)
        own = jnp.concatenate(
            [
                positions.reshape(3, per_brick),
                (width_atom * width_atom)[None],
                negativity[None],
                self_term[None],
            ],
            0,
        )
        geometry = gather_all(own)
        col_index = jnp.arange(atoms, dtype=jnp.int32)

        pair = devices % 2 == 0 and (atoms // 2) * atoms * 4 <= PAIR_LIMIT
        if pair:
            parity = me % 2
            halves = devices // 2
            row_geometry = lax.dynamic_index_in_dim(
                geometry.reshape(6, halves, 2, per_brick), parity, 2, keepdims=False
            ).reshape(6, -1)
            brick_of = 2 * jnp.arange(halves, dtype=jnp.int32) + parity
            row_index = (brick_of[:, None] * per_brick + jnp.arange(per_brick, dtype=jnp.int32)[None]).reshape(-1)
            partner = [(i, i ^ 1) for i in range(devices)]

            def pick_rows(vectors):
                return lax.dynamic_index_in_dim(
                    vectors.reshape(2, halves, 2, per_brick), parity, 2, keepdims=False
                ).reshape(2, -1)

            def assemble(mine):
                theirs = lax.ppermute(mine, everyone, partner)
                first = jnp.where(parity == 0, mine, theirs).reshape(2, halves, per_brick)
                second = jnp.where(parity == 0, theirs, mine).reshape(2, halves, per_brick)
                return jnp.stack([first, second], 2).reshape(2, atoms)
        else:
            row_geometry = own
            row_index = me * per_brick + jnp.arange(per_brick, dtype=jnp.int32)

            def assemble(mine):
                return gather_all(mine.reshape(2, per_brick))

        matrix = screened(row_geometry, geometry, row_index[:, None] == col_index[None, :])

        def operate(vectors):
            return assemble(jnp.sum(matrix[None, :, :] * vectors[:, None, :], 2))

        rhs = jnp.stack([-geometry[4], jnp.ones((atoms,), jnp.float32)])
        solution = jnp.zeros_like(rhs)
        resid = rhs
        direction = rhs
        norm_now = jnp.sum(resid * resid, 1)
        for iteration in range(ITERS):
            image = operate(direction)
            step_size = norm_now / jnp.sum(direction * image, 1)
            solution = solution + step_size[:, None] * direction
            if iteration + 1 < ITERS:
                resid = resid - step_size[:, None] * image
                norm_next = jnp.sum(resid * resid, 1)
                direction = resid + (norm_next / norm_now)[:, None] * direction
                norm_now = norm_next
        totals = jnp.sum(solution, 1)
        lagrange = totals[0] / totals[1]
        charges = solution[0] - lagrange * solution[1]
        own_index = me * per_brick + jnp.arange(per_brick, dtype=jnp.int32)
        own_charges = lax.dynamic_slice_in_dim(charges, me * per_brick, per_brick, 0)
        field = pulling(own, geometry, own_index[:, None] == col_index[None, :], charges)
        forces = (own_charges[None, :] * field).reshape(3, 1, 1, per_brick)
        return (own_charges.reshape(1, 1, per_brick), forces)

    return shards


def solution(mesh):
    in_specs = (
        P(None, "row", "col", None),
        P("row", "col", None),
        P(None, "row", "col", None),
        P(),
        P(),
        P(),
    )
    out_specs = (P("row", "col", None), P(None, "row", "col", None))
    shards = make_shards(mesh.shape["row"], mesh.shape["col"])
    return jax.shard_map(shards, mesh=mesh, in_specs=in_specs, out_specs=out_specs, check_vma=False)
```

time: 361 us -> 55.6 us (0.15)
  blocking collectives: 347 us -> 0 us
  other arithmetic: 4.18 us -> 25.8 us
  waiting for transfers between devices: 0 us -> 10.2 us
  starting transfers between devices: 0 us -> 7.93 us
  local copies, waits for them, and re-layouts: 5.38 us -> 9.06 us
    psum x10 -> x0, blocking collectives: 287 us -> none  [the longest x3 121 us: squares(): return lax.psum(jnp.sum(resid * resid, 1), ('row', 'col'))]
    all_gather x5 -> x0, blocking collectives: 50.3 us -> none  [the longest x3 27.9 us: shards(): lax.all_gather(direction, 'row', axis=1, tiled=True)]
    unnamed x1 -> x0, blocking collectives: 9.88 us -> none
    reduce_sum x9, other arithmetic: 1.8 us -> 11.7 us  [the longest x3 10.5 us: operate(): return assemble(jnp.sum(matrix[None, :, :] * vectors[:, None, :], 2))]
    select_n x1 -> x4, other arithmetic: 0.49 us -> 9.03 us  [the longest x1 9.01 us: screened(): return jnp.where(self_pair, row_geometry[5][:, None], off)]
    all_to_all x0 -> x1, starting transfers between devices: none -> 7.3 us  [gather_all(): got = lax.all_to_all(spread, everyone, 0, 0, tiled=True)]
    all_to_all x0 -> x1, waiting for transfers between devices: none -> 7.16 us  [gather_all(): got = lax.all_to_all(spread, everyone, 0, 0, tiled=True)]
  transfers between devices with their start and end apart: 0 -> 4, of which waited for: 0 -> 4; matrix products, arithmetic and copies ran while one was open for 0% -> 0% of each run, Pallas kernels for 0% -> 0%
where the time goes in v1:
time: 55.6 us; the launch traced here: 55.2 us
  other arithmetic  25.8 us (46%)
  waiting for transfers between devices  10.2 us (18%)
  local copies, waits for them, and re-layouts  9.06 us (16%)
  starting transfers between devices  7.93 us (14%)
  between operations  2.15 us (4%)
    reduce_sum x3, other arithmetic, operate(): return assemble(jnp.sum(matrix[None, :, :] * vectors[:, None, :], 2))  10.5 us
    select_n x1, other arithmetic, screened(): return jnp.where(self_pair, row_geometry[5][:, None], off)  9.01 us
    all_to_all x1, starting transfers between devices, gather_all(): got = lax.all_to_all(spread, everyone, 0, 0, tiled=True)  7.3 us
    all_to_all x1, waiting for transfers between devices, gather_all(): got = lax.all_to_all(spread, everyone, 0, 0, tiled=True)  7.16 us
    unnamed x7, local copies, waits for them, and re-layouts  4.71 us
    ppermute x3, waiting for transfers between devices, assemble(): theirs = lax.ppermute(mine, everyone, partner)  3.06 us
  transfers between devices with their start and end apart: 4, of which 4 were waited for; matrix products, arithmetic and copies ran while one was open for 0% of the time, Pallas kernels for 0%

profile of v1, /device:TPU:0, one launch (start us, length us, event | category | flops | bytes accessed | tf_op | source)
XLA Modules:
  0.0 55.2 jit_solution(17840544865066839076)
XLA Ops:
  0.6 0.7 %fusion.14 = f32[4,64]{1,0:T(4,128)S(1)} fusion(s32[64]{0:T(128)} %bitcast.52), kind=kLoop, calls=%fused_computation.68 | loop fusion | flops 512 | bytes 1280 | tf_op jit(solution)/shard_map/convert_element_type | solution.py:69
  1.3 0.8 %slice_bitcast_fusion.9 = (f32[128]{0:T(128)S(1)}, f32[128]{0:T(128)S(1)}, f32[128]{0:T(128)S(1)}, f32[128]{0:T(128)S(1)}) fusion(f32[4,128]{1,0:T(4,128)} %param.9), kind=kLoop, calls=%fused_computation.83 | loop fusion | bytes 4096 | tf_op jit(solution)/shard_map/mul | solution.py:75
  2.1 0.7 %copy.13 = f32[3,1,1,64]{3,0,1,2:T(4,128)S(1)} copy(f32[3,1,1,64]{3,2,1,0:T(1,128)} %param.6) | data formatting | bytes 1536
  2.8 0.8 %select_reduce_fusion.1 = (f32[64]{0:T(128)S(1)}, f32[64]{0:T(128)S(1)}) fusion(f32[4]{0:T(128)} %param.11, s32[64]{0:T(128)} %bitcast.53, f32[4]{0:T(128)} %param.10), kind=kLoop, calls=%fused_computation.66 | loop fusion | flops 1152 | bytes 800 | tf_op jit(solution)/shard_map/reduce_sum | solution.py:71
  3.6 1.0 %fusion.11 = f32[64]{0:T(128)S(1)} fusion(f32[128,1,1,64]{0,3,2,1:T(8,128)} %param.8, f32[128]{0:T(128)S(1)} %get-tuple-element.39, f32[64]{0:T(128)S(1)} %get-tuple-element.34, f32[128]{0:T(128)S(1)} %get-tuple-element.40, f32[64]{0:T(128)S(1)} %get-tuple-element.35, f32[128]{0:T(128)S(1)} %get-tuple-element.38, f32[64]{0:T(128)S(1)} %get-tuple-element.36, ...), kind=kLoop, calls=%fused_computation.31 | loop fusion | flops 73664 | bytes 36096 | tf_op jit(solution)/shard_map/reduce_sum | solution.py:76
  4.6 0.7 %reshape.463 = f32[32,1,384]{2,1,0:T(1,128)} reshape(f32[32,6,64]{2,1,0:T(8,128)S(1)} %broadcast_in_dim.25) | data formatting | bytes 98304
  5.3 7.3 %all-to-all-start = ((f32[32,1,384]{2,1,0:T(1,128)}), f32[32,1,384]{2,1,0:T(1,128)S(1)}, u32[]{:S(2)}, u32[]{:S(2)}) async-start(f32[32,1,384]{2,1,0:T(1,128)} %reshape.463), calls=%async_computation | async-start | bytes 98304 | tf_op jit(solution)/shard_map/all_to_all | solution.py:61
  12.8 7.2 %all-to-all-done = f32[32,1,384]{2,1,0:T(1,128)S(1)} async-done(((f32[32,1,384]{2,1,0:T(1,128)}), f32[32,1,384]{2,1,0:T(1,128)S(1)}, u32[]{:S(2)}, u32[]{:S(2)}) %all-to-all-start) | async-done | bytes 49184 | tf_op jit(solution)/shard_map/all_to_all | solution.py:61
  20.0 0.5 broadcast.205
  20.5 0.8 %reduce.40 = f32[32,384]{1,0:T(8,128)S(1)} reduce(f32[32,1,384]{2,1,0:T(1,128)S(1)} %all-to-all-done, f32[]{:T(128)} %broadcast.205), dimensions={1}, to_apply=%all_to_all.3.reduce_sub_computation | reduce | bytes 98308 | tf_op jit(solution)/shard_map/all_to_all | solution.py:61
  21.8 0.2 slice_reduce_fusion.3
  22.4 9.0 %fusion = f32[1024,2048]{1,0:T(8,128)S(1)} fusion(f32[2048]{0:T(1024)S(1)} %sub.134, f32[1024]{0:T(1024)S(1)} %sub.132, f32[2048]{0:T(1024)S(1)} %sub.129, f32[1024]{0:T(1024)S(1)} %sub.127, f32[2048]{0:T(1024)S(1)} %sub.124, f32[1024]{0:T(1024)S(1)} %sub.122, f32[2048]{0:T(1024)S(1)} %add.160, f32[1024]{0:T(1024)S(1)} %add.158, ...), kind=kLoop, calls=%fused_computation.4 | loop fusion | flops 33554432 | bytes 8445952 | tf_op jit(solution)/shard_map/jit(_where)/select_n | solution.py:24
  31.5 3.2 %copy-done = f32[1024,2048]{1,0:T(8,128)} copy-done((f32[1024,2048]{1,0:T(8,128)}, f32[1024,2048]{1,0:T(8,128)S(1)}, u32[]{:S(2)}) %copy-start) | copy-done | bytes 8388632
  34.7 1.2 %multiply_reduce_fusion.2 = f32[2,1024]{1,0:T(2,128)S(1)} fusion(f32[2,2048]{1,0:T(2,128)S(1)} %stack.25, f32[1024,2048]{1,0:T(8,128)S(1)} %fusion), kind=kLoop, calls=%fused_computation.2 | loop fusion | flops 8386560 | bytes 8413184 | tf_op jit(solution)/shard_map/reduce_sum | solution.py:121
  36.1 1.1 %collective-permute-done = f32[2,1024]{1,0:T(2,128)S(1)} collective-permute-done((f32[2,1024]{1,0:T(2,128)S(1)}, f32[2,1024]{1,0:T(2,128)S(1)}, u32[]{:S(2)}, u32[]{:S(2)}) %collective-permute-start) | collective-permute-done | bytes 8224 | tf_op jit(solution)/shard_map/ppermute | solution.py:107
  37.9 4.6 %multiply_reduce_fusion.1 = f32[2,1024]{1,0:T(2,128)S(1)} fusion(f32[2,2048]{1,0:T(2,128)S(1)} %multiply_add_fusion.2, f32[1024,2048]{1,0:T(8,128)} %copy-done), kind=kLoop, calls=%fused_computation.1 | loop fusion | flops 8386560 | bytes 8413184 | tf_op jit(solution)/shard_map/reduce_sum | solution.py:121
  42.6 0.2 collective-permute-start.1
  42.8 1.0 %collective-permute-done.1 = f32[2,1024]{1,0:T(2,128)S(1)} collective-permute-done((f32[2,1024]{1,0:T(2,128)S(1)}, f32[2,1024]{1,0:T(2,128)S(1)}, u32[]{:S(2)}, u32[]{:S(2)}) %collective-permute-start.1) | collective-permute-done | bytes 8224 | tf_op jit(solution)/shard_map/ppermute | solution.py:107
  44.6 4.7 %multiply_reduce_fusion = f32[2,1024]{1,0:T(2,128)S(1)} fusion(f32[2,2048]{1,0:T(2,128)S(1)} %multiply_add_fusion.1, f32[1024,2048]{1,0:T(8,128)} %copy-done), kind=kLoop, calls=%fused_computation | loop fusion | flops 8386560 | bytes 8413184 | tf_op jit(solution)/shard_map/reduce_sum | solution.py:121
  49.6 1.0 %collective-permute-done.2 = f32[2,1024]{1,0:T(2,128)S(1)} collective-permute-done((f32[2,1024]{1,0:T(2,128)S(1)}, f32[2,1024]{1,0:T(2,128)S(1)}, u32[]{:S(2)}, u32[]{:S(2)}) %collective-permute-start.2) | collective-permute-done | bytes 8224 | tf_op jit(solution)/shard_map/ppermute | solution.py:107
  51.2 0.6 %fusion.19 = (f32[1]{0:T(128)}, f32[1]{0:T(128)}) fusion(f32[2]{0:T(128)S(1)} %get-tuple-element.19), kind=kLoop, calls=%fused_computation.90 | loop fusion | bytes 16 | tf_op jit(solution)/shard_map/slice | solution.py:138
  53.2 0.6 %fusion.16 = (f32[64]{0:T(128)S(1)}, f32[1,1,64]{2,1,0:T(1,128)}) fusion(f32[1,2048]{1,0:T(1,128)S(1)} %fusion.13, s32[]{:T(128)S(6)} %select_n.76), kind=kLoop, calls=%fused_computation.86 | loop fusion | bytes 772 | tf_op jit(solution)/shard_map/dynamic_slice | solution.py:141
  53.8 0.8 %fusion.5 = (f32[64]{0:T(128)S(1)}, f32[64]{0:T(128)S(1)}, f32[64]{0:T(128)S(1)}) fusion(f32[2048]{0:T(1024)S(1)} %sub.124, f32[64]{0:T(128)S(1)} %get-tuple-element.42, f32[2048]{0:T(1024)S(1)} %bitcast.49, f32[2048]{0:T(1024)S(1)} %sub.134, f32[64]{0:T(128)S(1)} %get-tuple-element.43, f32[2048]{0:T(1024)S(1)} %sub.129, f32[64]{0:T(128)S(1)} %get-tuple-element.41, ...), kind=kLoop, calls=%fused_computation.19 | loop fusion | flops 4063040 | bytes 43008 | tf_op jit(solution)/shard_map/reduce_sum | solution.py:48
  54.6 0.6 %maximum_multiply_fusion = f32[3,1,1,64]{3,2,1,0:T(1,128)} fusion(f32[1,1,1,64]{3,2,1,0:T(1,128)S(1)} %bitcast.55, f32[1,1,1,64]{3,2,1,0:T(1,128)S(1)} %bitcast.56, f32[1,1,1,64]{3,2,1,0:T(1,128)S(1)} %bitcast.54, f32[64]{0:T(128)S(1)} %get-tuple-element.31), kind=kLoop, calls=%fused_computation.69 | loop fusion | flops 576 | bytes 1792 | tf_op jit(solution)/shard_map/mul | solution.py:143
  (59 shorter events, 3.8 us)
Async XLA Ops:
  5.3 14.6 %all-to-all-start = ((f32[32,1,384]{2,1,0:T(1,128)}), f32[32,1,384]{2,1,0:T(1,128)S(1)}, u32[]{:S(2)}, u32[]{:S(2)}) async-start(f32[32,1,384]{2,1,0:T(1,128)} %reshape.463), calls=%async_computation | async-start | bytes 98304 | tf_op jit(solution)/shard_map/all_to_all | solution.py:61
  31.5 3.2 %copy-start = (f32[1024,2048]{1,0:T(8,128)}, f32[1024,2048]{1,0:T(8,128)S(1)}, u32[]{:S(2)}) copy-start(f32[1024,2048]{1,0:T(8,128)S(1)} %fusion) | copy-start | bytes 25165828
  34.7 8.1 %copy-start.1 = (f32[3,1,1,64]{3,2,1,0:T(1,128)S(1)}, f32[3,1,1,64]{3,2,1,0:T(1,128)}, u32[]{:S(2)}) copy-start(f32[3,1,1,64]{3,2,1,0:T(1,128)} %param.6) | copy-start | bytes 2308
  35.9 1.2 %collective-permute-start = (f32[2,1024]{1,0:T(2,128)S(1)}, f32[2,1024]{1,0:T(2,128)S(1)}, u32[]{:S(2)}, u32[]{:S(2)}) collective-permute-start(f32[2,1024]{1,0:T(2,128)S(1)} %multiply_reduce_fusion.2), channel_id=1, source_target_pairs={{0,1},{1,0},{2,3},{3,2},{4,5},{5,4},{6,7},{7,6},{8,9},{9,8},{10,11... | collective-permute-start | bytes 24584 | tf_op jit(solution)/shard_map/ppermute | solution.py:107
  42.6 1.2 %collective-permute-start.1 = (f32[2,1024]{1,0:T(2,128)S(1)}, f32[2,1024]{1,0:T(2,128)S(1)}, u32[]{:S(2)}, u32[]{:S(2)}) collective-permute-start(f32[2,1024]{1,0:T(2,128)S(1)} %multiply_reduce_fusion.1), channel_id=1, source_target_pairs={{0,1},{1,0},{2,3},{3,2},{4,5},{5,4},{6,7},{7,6},{8,9},{9,8},{10,11... | collective-permute-start | bytes 24584 | tf_op jit(solution)/shard_map/ppermute | solution.py:107
  49.3 1.2 %collective-permute-start.2 = (f32[2,1024]{1,0:T(2,128)S(1)}, f32[2,1024]{1,0:T(2,128)S(1)}, u32[]{:S(2)}, u32[]{:S(2)}) collective-permute-start(f32[2,1024]{1,0:T(2,128)S(1)} %multiply_reduce_fusion), channel_id=1, source_target_pairs={{0,1},{1,0},{2,3},{3,2},{4,5},{5,4},{6,7},{7,6},{8,9},{9,8},{10,11... | collective-permute-start | bytes 24584 | tf_op jit(solution)/shard_map/ppermute | solution.py:107

commit v2 on v1

--- a/solution.py
+++ b/solution.py
@@ -10,6 +10,7 @@
 TWO_ROOT = 1.1283791670955126
 
 PAIR_LIMIT = 16 * 1024 * 1024
+CHUNKS = 4
 
 
 def screened(row_geometry, col_geometry, self_pair):
@@ -115,10 +116,23 @@
             def assemble(mine):
                 return gather_all(mine.reshape(2, per_brick))
 
-        matrix = screened(row_geometry, geometry, row_index[:, None] == col_index[None, :])
+        chunks = CHUNKS if pair and atoms % CHUNKS == 0 else 1
+        width = atoms // chunks
+        matrices = [
+            screened(
+                row_geometry,
+                geometry[:, c * width : (c + 1) * width],
+                row_index[:, None] == col_index[None, c * width : (c + 1) * width],
+            )
+            for c in range(chunks)
+        ]
 
         def operate(vectors):
-            return assemble(jnp.sum(matrix[None, :, :] * vectors[:, None, :], 2))
+            total = 0.0
+            for c, matrix in enumerate(matrices):
+                part = vectors[:, c * width : (c + 1) * width]
+                total = total + jnp.sum(matrix[None, :, :] * part[:, None, :], 2)
+            return assemble(total)
 
         rhs = jnp.stack([-geometry[4], jnp.ones((atoms,), jnp.float32)])
         solution = jnp.zeros_like(rhs)

time: 55.6 us -> 50 us (0.90)
  other arithmetic: 25.8 us -> 20.6 us
    reduce_sum x3 -> x10, other arithmetic: 10.5 us -> 7.82 us  [operate(): total = total + jnp.sum(matrix[None, :, :] * part[:, None, :], 2)]
    select_n x1 -> x2, other arithmetic: 9.01 us -> 6.46 us  [screened(): return jnp.where(self_pair, row_geometry[5][:, None], off)]
    unnamed x7 -> x19, local copies, waits for them, and re-layouts: 4.71 us -> 4.4 us
  transfers between devices with their start and end apart: 4 -> 4, of which waited for: 4 -> 4; matrix products, arithmetic and copies ran while one was open for 0% -> 1% of each run, Pallas kernels for 0% -> 0%
where the time goes in v2:
time: 50 us; the launch traced here: 49.6 us
  other arithmetic  20.6 us (41%)
  waiting for transfers between devices  9.9 us (20%)
  local copies, waits for them, and re-layouts  8.89 us (18%)
  starting transfers between devices  7.94 us (16%)
  between operations  2.3 us (5%)
    reduce_sum x10, other arithmetic, operate(): total = total + jnp.sum(matrix[None, :, :] * part[:, None, :], 2)  7.82 us
    all_to_all x1, starting transfers between devices, gather_all(): got = lax.all_to_all(spread, everyone, 0, 0, tiled=True)  7.3 us
    all_to_all x1, waiting for transfers between devices, gather_all(): got = lax.all_to_all(spread, everyone, 0, 0, tiled=True)  7.12 us
    select_n x2, other arithmetic, screened(): return jnp.where(self_pair, row_geometry[5][:, None], off)  6.46 us
    unnamed x19, local copies, waits for them, and re-layouts  4.4 us
    ppermute x3, waiting for transfers between devices, assemble(): theirs = lax.ppermute(mine, everyone, partner)  2.78 us
  transfers between devices with their start and end apart: 4, of which 4 were waited for; matrix products, arithmetic and copies ran while one was open for 1% of the time, Pallas kernels for 0%

profile of v2, /device:TPU:0, one launch (start us, length us, event | category | flops | bytes accessed | tf_op | source)
XLA Modules:
  0.0 49.6 jit_solution(1643245436793629708)
XLA Ops:
  0.6 0.7 %fusion.18 = f32[4,64]{1,0:T(4,128)S(1)} fusion(s32[64]{0:T(128)} %bitcast.85), kind=kLoop, calls=%fused_computation.102 | loop fusion | flops 512 | bytes 1280 | tf_op jit(solution)/shard_map/convert_element_type | solution.py:70
  1.3 0.7 %copy.15 = f32[3,1,1,64]{3,0,1,2:T(4,128)S(1)} copy(f32[3,1,1,64]{3,2,1,0:T(1,128)} %param.6) | data formatting | bytes 1536
  2.0 0.8 %slice_bitcast_fusion.9 = (f32[128]{0:T(128)S(1)}, f32[128]{0:T(128)S(1)}, f32[128]{0:T(128)S(1)}, f32[128]{0:T(128)S(1)}) fusion(f32[4,128]{1,0:T(4,128)} %param.9), kind=kLoop, calls=%fused_computation.117 | loop fusion | bytes 4096 | tf_op jit(solution)/shard_map/mul | solution.py:76
  2.8 0.8 %select_reduce_fusion.1 = (f32[64]{0:T(128)S(1)}, f32[64]{0:T(128)S(1)}) fusion(f32[4]{0:T(128)} %param.11, s32[64]{0:T(128)} %bitcast.86, f32[4]{0:T(128)} %param.10), kind=kLoop, calls=%fused_computation.100 | loop fusion | flops 1152 | bytes 800 | tf_op jit(solution)/shard_map/reduce_sum | solution.py:72
  3.6 1.0 %fusion.10 = f32[64]{0:T(128)S(1)} fusion(f32[128,1,1,64]{0,3,2,1:T(8,128)} %param.8, f32[128]{0:T(128)S(1)} %get-tuple-element.71, f32[64]{0:T(128)S(1)} %get-tuple-element.66, f32[128]{0:T(128)S(1)} %get-tuple-element.72, f32[64]{0:T(128)S(1)} %get-tuple-element.67, f32[128]{0:T(128)S(1)} %get-tuple-element.70, f32[64]{0:T(128)S(1)} %get-tuple-element.68, ...), kind=kLoop, calls=%fused_computation.49 | loop fusion | flops 73664 | bytes 36096 | tf_op jit(solution)/shard_map/reduce_sum | solution.py:77
  4.6 0.7 %reshape.1005 = f32[32,1,384]{2,1,0:T(1,128)} reshape(f32[32,6,64]{2,1,0:T(8,128)S(1)} %broadcast_in_dim.37) | data formatting | bytes 98304
  5.3 7.3 %all-to-all-start = ((f32[32,1,384]{2,1,0:T(1,128)}), f32[32,1,384]{2,1,0:T(1,128)S(1)}, u32[]{:S(2)}, u32[]{:S(2)}) async-start(f32[32,1,384]{2,1,0:T(1,128)} %reshape.1005), calls=%async_computation | async-start | bytes 98304 | tf_op jit(solution)/shard_map/all_to_all | solution.py:62
  12.8 7.1 %all-to-all-done = f32[32,1,384]{2,1,0:T(1,128)S(1)} async-done(((f32[32,1,384]{2,1,0:T(1,128)}), f32[32,1,384]{2,1,0:T(1,128)S(1)}, u32[]{:S(2)}, u32[]{:S(2)}) %all-to-all-start) | async-done | bytes 49184 | tf_op jit(solution)/shard_map/all_to_all | solution.py:62
  20.5 0.8 %reduce.40 = f32[32,384]{1,0:T(8,128)S(1)} reduce(f32[32,1,384]{2,1,0:T(1,128)S(1)} %all-to-all-done, f32[]{:T(128)} %broadcast.558), dimensions={1}, to_apply=%all_to_all.3.reduce_sub_computation | reduce | bytes 98308 | tf_op jit(solution)/shard_map/all_to_all | solution.py:62
  22.3 3.2 %compare_select_fusion.6 = (f32[1024,512]{1,0:T(8,128)S(1)}, f32[1024,512]{1,0:T(8,128)S(1)}) fusion(f32[512]{0:T(512)S(1)} %bitcast.81, f32[1024]{0:T(1024)S(1)} %sub.265, f32[512]{0:T(512)S(1)} %bitcast.82, f32[1024]{0:T(1024)S(1)} %sub.261, f32[512]{0:T(512)S(1)} %bitcast.83, f32[1024]{0:T(1024)S(1)} %sub.257, f32[512]{0:T(512)S(1)} %bitcast.84, ...), kind=kLoop, calls=%fused_computation.18 | loop fusion | flops 16777216 | bytes 4239360 | tf_op jit(solution)/shard_map/jit(_where)/select_n | solution.py:25
  25.6 3.2 %compare_select_fusion.4 = (f32[1024,512]{1,0:T(8,128)S(1)}, f32[1024,512]{1,0:T(8,128)S(1)}) fusion(f32[512]{0:T(512)S(1)} %bitcast.74, f32[512]{0:T(512)S(1)} %bitcast.75, f32[512]{0:T(512)S(1)} %bitcast.76, f32[512]{0:T(512)S(1)} %bitcast.69, s32[512]{0:T(512)S(1)} %iota_add_fusion.3, f32[1024]{0:T(1024)S(1)} %sub.265, f32[1024]{0:T(1024)S(1)} %sub.261, ...), kind=kLoop, calls=%fused_computation.16 | loop fusion | flops 16777216 | bytes 4239360 | tf_op jit(solution)/shard_map/jit(_where)/select_n | solution.py:25
  28.8 0.7 %multiply_reduce_fusion.10 = (f32[2,1024]{1,0:T(2,128)S(1)}, f32[2,1024]{1,0:T(2,128)S(1)}) fusion(f32[2,512]{1,0:T(2,128)S(1)} %get-tuple-element.61, f32[1024,512]{1,0:T(8,128)S(1)} %get-tuple-element.41, f32[2,512]{1,0:T(2,128)S(1)} %get-tuple-element.64, f32[1024,512]{1,0:T(8,128)S(1)} %get-tuple-element.43), kind=kLoop, calls=%fused_computation.10 | loop fusion | flops 4190208 | bytes 4218880 | tf_op jit(solution)/shard_map/reduce_sum | solution.py:134
  29.5 0.7 %copy-done.2 = f32[1024,512]{1,0:T(8,128)} copy-done((f32[1024,512]{1,0:T(8,128)}, f32[1024,512]{1,0:T(8,128)S(1)}, u32[]{:S(2)}) %copy-start.2) | copy-done | bytes 2097176
  30.2 0.6 %copy-done.4 = f32[1024,512]{1,0:T(8,128)} copy-done((f32[1024,512]{1,0:T(8,128)}, f32[1024,512]{1,0:T(8,128)S(1)}, u32[]{:S(2)}) %copy-start.4) | copy-done | bytes 2097176
  30.8 0.7 %multiply_reduce_fusion.8 = (f32[2,1024]{1,0:T(2,128)S(1)}, f32[2,1024]{1,0:T(2,128)S(1)}) fusion(f32[2,512]{1,0:T(2,128)S(1)} %get-tuple-element.63, f32[1024,512]{1,0:T(8,128)S(1)} %get-tuple-element.44, f32[2,512]{1,0:T(2,128)S(1)} %get-tuple-element.62, f32[1024,512]{1,0:T(8,128)S(1)} %get-tuple-element.42), kind=kLoop, calls=%fused_computation.8 | loop fusion | flops 4190208 | bytes 4218880 | tf_op jit(solution)/shard_map/reduce_sum | solution.py:134
  31.6 1.1 %collective-permute-done = f32[2,1024]{1,0:T(2,128)S(1)} collective-permute-done((f32[2,1024]{1,0:T(2,128)S(1)}, f32[2,1024]{1,0:T(2,128)S(1)}, u32[]{:S(2)}, u32[]{:S(2)}) %collective-permute-start) | collective-permute-done | bytes 8224 | tf_op jit(solution)/shard_map/ppermute | solution.py:108
  33.5 2.1 %multiply_reduce_fusion.6 = f32[2,1024]{1,0:T(2,128)S(1)} fusion(f32[2,512]{1,0:T(2,128)S(1)} %get-tuple-element.53, f32[1024,512]{1,0:T(8,128)} %copy-done.2), kind=kLoop, calls=%fused_computation.6 | loop fusion | flops 2095104 | bytes 2109440 | tf_op jit(solution)/shard_map/reduce_sum | solution.py:134
  36.4 0.8 %copy-done.1 = f32[1024,512]{1,0:T(8,128)S(1)} copy-done((f32[1024,512]{1,0:T(8,128)S(1)}, f32[1024,512]{1,0:T(8,128)}, u32[]{:S(2)}) %copy-start.1) | copy-done | bytes 2097176
  37.9 1.0 %collective-permute-done.1 = f32[2,1024]{1,0:T(2,128)S(1)} collective-permute-done((f32[2,1024]{1,0:T(2,128)S(1)}, f32[2,1024]{1,0:T(2,128)S(1)}, u32[]{:S(2)}, u32[]{:S(2)}) %collective-permute-start.1) | collective-permute-done | bytes 8224 | tf_op jit(solution)/shard_map/ppermute | solution.py:108
  39.7 2.1 %multiply_reduce_fusion.3 = f32[2,1024]{1,0:T(2,128)S(1)} fusion(f32[2,512]{1,0:T(2,128)S(1)} %get-tuple-element.50, f32[1024,512]{1,0:T(8,128)} %copy-done), kind=kLoop, calls=%fused_computation.3 | loop fusion | flops 2095104 | bytes 2109440 | tf_op jit(solution)/shard_map/reduce_sum | solution.py:134
  42.6 0.8 %copy-done.3 = f32[1024,512]{1,0:T(8,128)S(1)} copy-done((f32[1024,512]{1,0:T(8,128)S(1)}, f32[1024,512]{1,0:T(8,128)}, u32[]{:S(2)}) %copy-start.3) | copy-done | bytes 2097176
  44.3 0.7 %collective-permute-done.2 = f32[2,1024]{1,0:T(2,128)S(1)} collective-permute-done((f32[2,1024]{1,0:T(2,128)S(1)}, f32[2,1024]{1,0:T(2,128)S(1)}, u32[]{:S(2)}, u32[]{:S(2)}) %collective-permute-start.2) | collective-permute-done | bytes 8224 | tf_op jit(solution)/shard_map/ppermute | solution.py:108
  45.7 0.6 %fusion.27 = (f32[1]{0:T(128)}, f32[1]{0:T(128)}) fusion(f32[2]{0:T(128)S(1)} %get-tuple-element.19), kind=kLoop, calls=%fused_computation.127 | loop fusion | bytes 16 | tf_op jit(solution)/shard_map/slice | solution.py:152
  48.2 0.8 %fusion.4 = (f32[64]{0:T(128)S(1)}, f32[64]{0:T(128)S(1)}, f32[64]{0:T(128)S(1)}) fusion(f32[2048]{0:T(1024)S(1)} %sub.292, f32[64]{0:T(128)S(1)} %get-tuple-element.74, f32[2048]{0:T(1024)S(1)} %bitcast.66, f32[2048]{0:T(1024)S(1)} %sub.302, f32[64]{0:T(128)S(1)} %get-tuple-element.75, f32[2048]{0:T(1024)S(1)} %sub.297, f32[64]{0:T(128)S(1)} %get-tuple-element.73, ...), kind=kLoop, calls=%fused_computation.37 | loop fusion | flops 4063040 | bytes 43008 | tf_op jit(solution)/shard_map/reduce_sum | solution.py:49
  (91 shorter events, 8.5 us)
Async XLA Ops:
  5.3 14.6 %all-to-all-start = ((f32[32,1,384]{2,1,0:T(1,128)}), f32[32,1,384]{2,1,0:T(1,128)S(1)}, u32[]{:S(2)}, u32[]{:S(2)}) async-start(f32[32,1,384]{2,1,0:T(1,128)} %reshape.1005), calls=%async_computation | async-start | bytes 98304 | tf_op jit(solution)/shard_map/all_to_all | solution.py:62
  25.6 3.3 %copy-start = (f32[1024,512]{1,0:T(8,128)}, f32[1024,512]{1,0:T(8,128)S(1)}, u32[]{:S(2)}) copy-start(f32[1024,512]{1,0:T(8,128)S(1)} %get-tuple-element.43) | copy-start | bytes 6291460
  28.8 1.4 %copy-start.2 = (f32[1024,512]{1,0:T(8,128)}, f32[1024,512]{1,0:T(8,128)S(1)}, u32[]{:S(2)}) copy-start(f32[1024,512]{1,0:T(8,128)S(1)} %get-tuple-element.41) | copy-start | bytes 6291460
  28.8 1.9 %copy-start.4 = (f32[1024,512]{1,0:T(8,128)}, f32[1024,512]{1,0:T(8,128)S(1)}, u32[]{:S(2)}) copy-start(f32[1024,512]{1,0:T(8,128)S(1)} %get-tuple-element.42) | copy-start | bytes 6291460
  31.4 1.2 %collective-permute-start = (f32[2,1024]{1,0:T(2,128)S(1)}, f32[2,1024]{1,0:T(2,128)S(1)}, u32[]{:S(2)}, u32[]{:S(2)}) collective-permute-start(f32[2,1024]{1,0:T(2,128)S(1)} %add_add_fusion.2), channel_id=1, source_target_pairs={{0,1},{1,0},{2,3},{3,2},{4,5},{5,4},{6,7},{7,6},{8,9},{9,8},{10,11... | collective-permute-start | bytes 24584 | tf_op jit(solution)/shard_map/ppermute | solution.py:108
  33.5 2.5 %copy-start.5 = (f32[1024,512]{1,0:T(8,128)S(1)}, f32[1024,512]{1,0:T(8,128)}, u32[]{:S(2)}) copy-start(f32[1024,512]{1,0:T(8,128)} %copy-done.4) | copy-start | bytes 6291460
  35.6 1.6 %copy-start.1 = (f32[1024,512]{1,0:T(8,128)S(1)}, f32[1024,512]{1,0:T(8,128)}, u32[]{:S(2)}) copy-start(f32[1024,512]{1,0:T(8,128)} %copy-done) | copy-start | bytes 6291460
  36.0 1.8 %copy-start.7 = (f32[3,1,1,64]{3,2,1,0:T(1,128)S(1)}, f32[3,1,1,64]{3,2,1,0:T(1,128)}, u32[]{:S(2)}) copy-start(f32[3,1,1,64]{3,2,1,0:T(1,128)} %param.6) | copy-start | bytes 2308
  37.6 1.2 %collective-permute-start.1 = (f32[2,1024]{1,0:T(2,128)S(1)}, f32[2,1024]{1,0:T(2,128)S(1)}, u32[]{:S(2)}, u32[]{:S(2)}) collective-permute-start(f32[2,1024]{1,0:T(2,128)S(1)} %add_add_fusion.1), channel_id=1, source_target_pairs={{0,1},{1,0},{2,3},{3,2},{4,5},{5,4},{6,7},{7,6},{8,9},{9,8},{10,11... | collective-permute-start | bytes 24584 | tf_op jit(solution)/shard_map/ppermute | solution.py:108
  39.2 2.6 %copy-start.6 = (f32[1024,512]{1,0:T(8,128)S(1)}, f32[1024,512]{1,0:T(8,128)}, u32[]{:S(2)}) copy-start(f32[1024,512]{1,0:T(8,128)} %copy-done.4) | copy-start | bytes 6291460
  41.8 1.6 %copy-start.3 = (f32[1024,512]{1,0:T(8,128)S(1)}, f32[1024,512]{1,0:T(8,128)}, u32[]{:S(2)}) copy-start(f32[1024,512]{1,0:T(8,128)} %copy-done.2) | copy-start | bytes 6291460
  43.8 1.2 %collective-permute-start.2 = (f32[2,1024]{1,0:T(2,128)S(1)}, f32[2,1024]{1,0:T(2,128)S(1)}, u32[]{:S(2)}, u32[]{:S(2)}) collective-permute-start(f32[2,1024]{1,0:T(2,128)S(1)} %add_add_fusion), channel_id=1, source_target_pairs={{0,1},{1,0},{2,3},{3,2},{4,5},{5,4},{6,7},{7,6},{8,9},{9,8},{10,11... | collective-permute-start | bytes 24584 | tf_op jit(solution)/shard_map/ppermute | solution.py:108

commit v3 on v1

--- a/solution.py
+++ b/solution.py
@@ -10,6 +10,10 @@
 TWO_ROOT = 1.1283791670955126
 
 PAIR_LIMIT = 16 * 1024 * 1024
+BLOCKS = (
+    ((0, 0), (1, 1), (0, 1), (0, 2), (1, 2)),
+    ((2, 2), (3, 3), (2, 3), (0, 3), (1, 3)),
+)
 
 
 def screened(row_geometry, col_geometry, self_pair):
@@ -115,10 +119,43 @@
             def assemble(mine):
                 return gather_all(mine.reshape(2, per_brick))
 
-        matrix = screened(row_geometry, geometry, row_index[:, None] == col_index[None, :])
+        if pair and atoms % 4 == 0:
+            group = atoms // 4
+            starts = []
+            matrices = []
+            for k, ((row_a, col_a), (row_b, col_b)) in enumerate(zip(BLOCKS[0], BLOCKS[1])):
+                row_at = jnp.where(parity == 0, row_a, row_b) * group
+                col_at = jnp.where(parity == 0, col_a, col_b) * group
+                starts.append((row_at, col_at))
+                local = jnp.arange(group, dtype=jnp.int32)
+                matrices.append(
+                    screened(
+                        lax.dynamic_slice_in_dim(geometry, row_at, group, 1),
+                        lax.dynamic_slice_in_dim(geometry, col_at, group, 1),
+                        (row_at + local)[:, None] == (col_at + local)[None, :],
+                    )
+                )
 
-        def operate(vectors):
-            return assemble(jnp.sum(matrix[None, :, :] * vectors[:, None, :], 2))
+            def operate(vectors):
+                partial = jnp.zeros_like(vectors)
+                for k, (matrix, (row_at, col_at)) in enumerate(zip(matrices, starts)):
+                    col_part = lax.dynamic_slice_in_dim(vectors, col_at, group, 1)
+                    forward = jnp.sum(matrix[None, :, :] * col_part[:, None, :], 2)
+                    partial = lax.dynamic_update_slice_in_dim(
+                        partial, lax.dynamic_slice_in_dim(partial, row_at, group, 1) + forward, row_at, 1
+                    )
+                    if k >= 2:
+                        row_part = lax.dynamic_slice_in_dim(vectors, row_at, group, 1)
+                        backward = jnp.sum(matrix[None, :, :] * row_part[:, :, None], 1)
+                        partial = lax.dynamic_update_slice_in_dim(
+                            partial, lax.dynamic_slice_in_dim(partial, col_at, group, 1) + backward, col_at, 1
+                        )
+                return partial + lax.ppermute(partial, everyone, partner)
+        else:
+            matrix = screened(row_geometry, geometry, row_index[:, None] == col_index[None, :])
+
+            def operate(vectors):
+                return assemble(jnp.sum(matrix[None, :, :] * vectors[:, None, :], 2))
 
         rhs = jnp.stack([-geometry[4], jnp.ones((atoms,), jnp.float32)])
         solution = jnp.zeros_like(rhs)

time: 55.6 us -> 41.7 us (0.75)
  other arithmetic: 25.8 us -> 16.2 us
  local copies, waits for them, and re-layouts: 9.06 us -> 4.76 us
    select_n x1 -> x2, other arithmetic: 9.01 us -> 3.76 us  [screened(): return jnp.where(self_pair, row_geometry[5][:, None], off)]
    reduce_sum x3 -> x5, other arithmetic: 10.5 us -> 5.98 us  [operate(): backward = jnp.sum(matrix[None, :, :] * row_part[:, :, None], 1)]
    unnamed x7 -> x9, local copies, waits for them, and re-layouts: 4.71 us -> 1.51 us
    another operation x10 -> x3, local copies, waits for them, and re-layouts: 0.59 us -> 0.02 us  [the longest x9 0.58 us: assemble(): return jnp.stack([first, second], 2).reshape(2, atoms)]
  transfers between devices with their start and end apart: 4 -> 4, of which waited for: 4 -> 4; matrix products, arithmetic and copies ran while one was open for 0% -> 1% of each run, Pallas kernels for 0% -> 0%
where the time goes in v3:
time: 41.7 us; the launch traced here: 41.3 us
  other arithmetic  16.2 us (39%)
  waiting for transfers between devices  10.1 us (24%)
  starting transfers between devices  7.94 us (19%)
  local copies, waits for them, and re-layouts  4.76 us (11%)
  between operations  2.3 us (6%)
    all_to_all x1, starting transfers between devices, gather_all(): got = lax.all_to_all(spread, everyone, 0, 0, tiled=True)  7.3 us
    all_to_all x1, waiting for transfers between devices, gather_all(): got = lax.all_to_all(spread, everyone, 0, 0, tiled=True)  7.26 us
    reduce_sum x5, other arithmetic, operate(): backward = jnp.sum(matrix[None, :, :] * row_part[:, :, None], 1)  5.98 us
    select_n x2, other arithmetic, screened(): return jnp.where(self_pair, row_geometry[5][:, None], off)  3.76 us
    ppermute x3, waiting for transfers between devices, operate(): return partial + lax.ppermute(partial, everyone, partner)  2.82 us
    unnamed x9, local copies, waits for them, and re-layouts  1.51 us
    reduce_sum x1, other arithmetic, shards(): negativity = jnp.sum(features * atom_weights, 0)  0.96 us
    mul x2, local copies, waits for them, and re-layouts, shards(): atom_weights = atom_weights + onehot[kind][None, :] * readout[kind][:, None]  0.84 us
  transfers between devices with their start and end apart: 4, of which 4 were waited for; matrix products, arithmetic and copies ran while one was open for 1% of the time, Pallas kernels for 0%

profile of v3, /device:TPU:0, one launch (start us, length us, event | category | flops | bytes accessed | tf_op | source)
XLA Modules:
  0.0 41.3 jit_solution(3852837080739691471)
XLA Ops:
  0.6 0.7 %fusion.34 = f32[4,64]{1,0:T(4,128)S(1)} fusion(s32[64]{0:T(128)} %bitcast.98), kind=kLoop, calls=%fused_computation.170 | loop fusion | flops 512 | bytes 1280 | tf_op jit(solution)/shard_map/convert_element_type | solution.py:73
  1.3 0.7 %copy.12 = f32[3,1,1,64]{3,0,1,2:T(4,128)S(1)} copy(f32[3,1,1,64]{3,2,1,0:T(1,128)} %param.6) | data formatting | bytes 1536
  2.0 0.8 %slice_bitcast_fusion.9 = (f32[128]{0:T(128)S(1)}, f32[128]{0:T(128)S(1)}, f32[128]{0:T(128)S(1)}, f32[128]{0:T(128)S(1)}) fusion(f32[4,128]{1,0:T(4,128)} %param.9), kind=kLoop, calls=%fused_computation.183 | loop fusion | bytes 4096 | tf_op jit(solution)/shard_map/mul | solution.py:79
  2.8 0.8 %select_reduce_fusion.1 = (f32[64]{0:T(128)S(1)}, f32[64]{0:T(128)S(1)}) fusion(f32[4]{0:T(128)} %param.11, s32[64]{0:T(128)} %bitcast.99, f32[4]{0:T(128)} %param.10), kind=kLoop, calls=%fused_computation.168 | loop fusion | flops 1152 | bytes 800 | tf_op jit(solution)/shard_map/reduce_sum | solution.py:75
  3.6 1.0 %fusion.11 = f32[64]{0:T(128)S(1)} fusion(f32[128,1,1,64]{0,3,2,1:T(8,128)} %param.8, f32[128]{0:T(128)S(1)} %get-tuple-element.105, f32[64]{0:T(128)S(1)} %get-tuple-element.100, f32[128]{0:T(128)S(1)} %get-tuple-element.106, f32[64]{0:T(128)S(1)} %get-tuple-element.101, f32[128]{0:T(128)S(1)} %get-tuple-element.104, f32[64]{0:T(128)S(1)} %get-tuple-element.102, ...), kind=kLoop, calls=%fused_computation.61 | loop fusion | flops 73664 | bytes 36096 | tf_op jit(solution)/shard_map/reduce_sum | solution.py:80
  4.6 0.7 %reshape.1118 = f32[32,1,384]{2,1,0:T(1,128)} reshape(f32[32,6,64]{2,1,0:T(8,128)S(1)} %broadcast_in_dim.53) | data formatting | bytes 98304
  5.3 7.3 %all-to-all-start = ((f32[32,1,384]{2,1,0:T(1,128)}), f32[32,1,384]{2,1,0:T(1,128)S(1)}, u32[]{:S(2)}, u32[]{:S(2)}) async-start(f32[32,1,384]{2,1,0:T(1,128)} %reshape.1118), calls=%async_computation | async-start | bytes 98304 | tf_op jit(solution)/shard_map/all_to_all | solution.py:65
  12.7 7.3 %all-to-all-done = f32[32,1,384]{2,1,0:T(1,128)S(1)} async-done(((f32[32,1,384]{2,1,0:T(1,128)}), f32[32,1,384]{2,1,0:T(1,128)S(1)}, u32[]{:S(2)}, u32[]{:S(2)}) %all-to-all-start) | async-done | bytes 49184 | tf_op jit(solution)/shard_map/all_to_all | solution.py:65
  20.0 0.5 %broadcast.663 = f32[]{:T(128)} broadcast(f32[]{:T(128)} %constant.171), dimensions={} | broadcast | bytes 8 | tf_op jit(solution)/shard_map/all_to_all | solution.py:65
  20.5 0.8 %reduce.20 = f32[32,384]{1,0:T(8,128)S(1)} reduce(f32[32,1,384]{2,1,0:T(1,128)S(1)} %all-to-all-done, f32[]{:T(128)} %broadcast.663), dimensions={1}, to_apply=%all_to_all.3.reduce_sub_computation | reduce | bytes 98308 | tf_op jit(solution)/shard_map/all_to_all | solution.py:65
  21.9 2.2 %compare_select_fusion.6 = (f32[512,512]{1,0:T(8,128)S(1)}, f32[512,512]{1,0:T(8,128)S(1)}, f32[512,512]{1,0:T(8,128)S(1)}) fusion(f32[512]{0:T(512)S(1)} %bitcast.97, f32[512]{0:T(512)S(1)} %bitcast.92, f32[512]{0:T(512)S(1)} %bitcast.93, f32[512]{0:T(512)S(1)} %bitcast.94, f32[512]{0:T(512)S(1)} %bitcast.95, s32[512]{0:T(512)S(1)} %iota_add_fusion.3, ...), kind=kLoop, calls=%fused_computation.30 | loop fusion | flops 12582912 | bytes 3170304 | tf_op jit(solution)/shard_map/jit(_where)/select_n | solution.py:28
  24.2 1.5 %compare_select_fusion = (f32[512,512]{1,0:T(8,128)S(1)}, f32[512,512]{1,0:T(8,128)S(1)}) fusion(f32[512]{0:T(512)S(1)} %bitcast.78, f32[512]{0:T(512)S(1)} %bitcast.79, f32[512]{0:T(512)S(1)} %bitcast.80, f32[512]{0:T(512)S(1)} %bitcast.81, f32[512]{0:T(512)S(1)} %bitcast.74, f32[512]{0:T(512)S(1)} %bitcast.85, f32[512]{0:T(512)S(1)} %bitcast.75, ...), kind=kLoop, calls=%fused_computation.24 | loop fusion | flops 8388608 | bytes 2129920 | tf_op jit(solution)/shard_map/jit(_where)/select_n | solution.py:28
  25.7 1.5 %multiply_reduce_fusion.16 = (f32[2,512]{1,0:T(2,128)S(1)}, f32[2,512]{1,0:T(2,128)S(1)}, f32[2,512]{1,0:T(2,128)S(1)}, f32[2,512]{1,0:T(2,128)S(1)}, f32[2,512]...) fusion(f32[2,512]{1,0:T(2,128)S(1)} %get-tuple-element.88, ...), kind=kLoop, calls=%fused_computation.16 | loop fusion | flops 8380416 | bytes 5296128 | tf_op jit(solution)/shard_map/reduce_sum | solution.py:149
  27.6 1.1 %collective-permute-done = f32[2,2048]{1,0:T(2,128)S(1)} collective-permute-done((f32[2,2048]{1,0:T(2,128)S(1)}, f32[2,2048]{1,0:T(2,128)S(1)}, u32[]{:S(2)}, u32[]{:S(2)}) %collective-permute-start) | collective-permute-done | bytes 16416 | tf_op jit(solution)/shard_map/ppermute | solution.py:153
  29.2 0.7 %multiply_reduce_fusion.12 = (f32[2,512]{1,0:T(2,128)S(1)}, f32[2,512]{1,0:T(2,128)S(1)}, f32[2,512]{1,0:T(2,128)S(1)}, f32[2,512]{1,0:T(2,128)S(1)}) fusion(f32[2,512]{1,0:T(2,128)S(1)} %get-tuple-element.80, f32[512,512]{1,0:T(8,128)S(1)} %get-tuple-element.82, f32[2,512]{1,0:T(2,128)S(1)} %get-tuple-element.79, f32[512,512]{1,0:T(8,128)S(1)} %get-tuple-element.83, ...), kind=kLoop, calls=%fused_computation.12 | loop fusion | flops 4190208 | bytes 3170304 | tf_op jit(solution)/shard_map/reduce_sum | solution.py:149
  30.1 0.7 %multiply_reduce_fusion.8 = (f32[2,512]{1,0:T(2,128)S(1)}, f32[2,512]{1,0:T(2,128)S(1)}, f32[2,512]{1,0:T(2,128)S(1)}, f32[2,512]{1,0:T(2,128)S(1)}) fusion(f32[2,512]{1,0:T(2,128)S(1)} %get-tuple-element.76, f32[512,512]{1,0:T(8,128)S(1)} %get-tuple-element.84, f32[2,512]{1,0:T(2,128)S(1)} %get-tuple-element.78, f32[2,512]{1,0:T(2,128)S(1)} %get-tuple-element.77, ...), kind=kLoop, calls=%fused_computation.8 | loop fusion | flops 4190208 | bytes 2125824 | tf_op jit(solution)/shard_map/reduce_sum | solution.py:149
  31.1 1.0 %collective-permute-done.1 = f32[2,2048]{1,0:T(2,128)S(1)} collective-permute-done((f32[2,2048]{1,0:T(2,128)S(1)}, f32[2,2048]{1,0:T(2,128)S(1)}, u32[]{:S(2)}, u32[]{:S(2)}) %collective-permute-start.1) | collective-permute-done | bytes 16416 | tf_op jit(solution)/shard_map/ppermute | solution.py:153
  32.6 2.3 %multiply_reduce_fusion.4 = (f32[2,512]{1,0:T(2,128)S(1)}, f32[2,512]{1,0:T(2,128)S(1)}, f32[2,512]{1,0:T(2,128)S(1)}, f32[2,512]{1,0:T(2,128)S(1)}) fusion(f32[2,512]{1,0:T(2,128)S(1)} %get-tuple-element.75, f32[512,512]{1,0:T(8,128)} %copy-done, f32[2,512]{1,0:T(2,128)S(1)} %get-tuple-element.74, f32[512,512]{1,0:T(8,128)} %copy-done.1, ...), kind=kLoop, calls=%fused_computation.4 | loop fusion | flops 4190208 | bytes 3170304 | tf_op jit(solution)/shard_map/reduce_sum | solution.py:149
  35.0 0.7 %multiply_reduce_fusion = (f32[2,512]{1,0:T(2,128)S(1)}, f32[2,512]{1,0:T(2,128)S(1)}, f32[2,512]{1,0:T(2,128)S(1)}, f32[2,512]{1,0:T(2,128)S(1)}) fusion(f32[2,512]{1,0:T(2,128)S(1)} %get-tuple-element.71, f32[512,512]{1,0:T(8,128)S(1)} %get-tuple-element.84, f32[2,512]{1,0:T(2,128)S(1)} %get-tuple-element.73, f32[2,512]{1,0:T(2,128)S(1)} %get-tuple-element.72, ...), kind=kLoop, calls=%fused_computation | loop fusion | flops 4190208 | bytes 2125824 | tf_op jit(solution)/shard_map/reduce_sum | solution.py:149
  36.3 0.7 %collective-permute-done.2 = f32[2,2048]{1,0:T(2,128)S(1)} collective-permute-done((f32[2,2048]{1,0:T(2,128)S(1)}, f32[2,2048]{1,0:T(2,128)S(1)}, u32[]{:S(2)}, u32[]{:S(2)}) %collective-permute-start.2) | collective-permute-done | bytes 16416 | tf_op jit(solution)/shard_map/ppermute | solution.py:153
  37.4 0.6 %fusion.43 = (f32[1]{0:T(128)}, f32[1]{0:T(128)}) fusion(f32[2]{0:T(128)S(1)} %get-tuple-element.38), kind=kLoop, calls=%fused_computation.193 | loop fusion | bytes 16 | tf_op jit(solution)/shard_map/slice | solution.py:175
  39.3 0.6 %fusion.36 = (f32[64]{0:T(128)S(1)}, f32[1,1,64]{2,1,0:T(1,128)}) fusion(f32[1,2048]{1,0:T(1,128)S(1)} %fusion.18, s32[]{:T(128)S(6)} %select_n.208), kind=kLoop, calls=%fused_computation.186 | loop fusion | bytes 772 | tf_op jit(solution)/shard_map/dynamic_slice | solution.py:178
  39.9 0.8 %fusion.5 = (f32[64]{0:T(128)S(1)}, f32[64]{0:T(128)S(1)}, f32[64]{0:T(128)S(1)}) fusion(f32[2048]{0:T(1024)S(1)} %sub.379, f32[64]{0:T(128)S(1)} %get-tuple-element.108, f32[2048]{0:T(1024)S(1)} %bitcast.71, f32[2048]{0:T(1024)S(1)} %sub.389, f32[64]{0:T(128)S(1)} %get-tuple-element.109, f32[2048]{0:T(1024)S(1)} %sub.384, f32[64]{0:T(128)S(1)} %get-tuple-element.107, ...), kind=kLoop, calls=%fused_computation.52 | loop fusion | flops 4063040 | bytes 43008 | tf_op jit(solution)/shard_map/reduce_sum | solution.py:52
  40.7 0.6 %maximum_multiply_fusion = f32[3,1,1,64]{3,2,1,0:T(1,128)} fusion(f32[1,1,1,64]{3,2,1,0:T(1,128)S(1)} %bitcast.101, f32[1,1,1,64]{3,2,1,0:T(1,128)S(1)} %bitcast.102, f32[1,1,1,64]{3,2,1,0:T(1,128)S(1)} %bitcast.100, f32[64]{0:T(128)S(1)} %get-tuple-element.86), kind=kLoop, calls=%fused_computation.171 | loop fusion | flops 576 | bytes 1792 | tf_op jit(solution)/shard_map/mul | solution.py:180
  (73 shorter events, 3.4 us)
Async XLA Ops:
  5.3 14.6 %all-to-all-start = ((f32[32,1,384]{2,1,0:T(1,128)}), f32[32,1,384]{2,1,0:T(1,128)S(1)}, u32[]{:S(2)}, u32[]{:S(2)}) async-start(f32[32,1,384]{2,1,0:T(1,128)} %reshape.1118), calls=%async_computation | async-start | bytes 98304 | tf_op jit(solution)/shard_map/all_to_all | solution.py:65
  24.2 5.0 %copy-start = (f32[512,512]{1,0:T(8,128)}, f32[512,512]{1,0:T(8,128)S(1)}, u32[]{:S(2)}) copy-start(f32[512,512]{1,0:T(8,128)S(1)} %get-tuple-element.82) | copy-start | bytes 3145732
  24.2 5.0 %copy-start.1 = (f32[512,512]{1,0:T(8,128)}, f32[512,512]{1,0:T(8,128)S(1)}, u32[]{:S(2)}) copy-start(f32[512,512]{1,0:T(8,128)S(1)} %get-tuple-element.83) | copy-start | bytes 3145732
  27.5 1.2 %collective-permute-start = (f32[2,2048]{1,0:T(2,128)S(1)}, f32[2,2048]{1,0:T(2,128)S(1)}, u32[]{:S(2)}, u32[]{:S(2)}) collective-permute-start(f32[2,2048]{1,0:T(2,128)S(1)} %constant_dynamic-update-slice_fusion.16), channel_id=1, source_target_pairs={{0,1},{1,0},{2,3},{3,2},{4,5},{5,4},{6,7},{7,6},{8,9},{9,8},{10,11... | collective-permute-start | bytes 49160 | tf_op jit(solution)/shard_map/ppermute | solution.py:153
  30.0 1.0 %copy-start.2 = (f32[3,1,1,64]{3,2,1,0:T(1,128)S(1)}, f32[3,1,1,64]{3,2,1,0:T(1,128)}, u32[]{:S(2)}) copy-start(f32[3,1,1,64]{3,2,1,0:T(1,128)} %param.6) | copy-start | bytes 2308
  30.9 1.2 %collective-permute-start.1 = (f32[2,2048]{1,0:T(2,128)S(1)}, f32[2,2048]{1,0:T(2,128)S(1)}, u32[]{:S(2)}, u32[]{:S(2)}) collective-permute-start(f32[2,2048]{1,0:T(2,128)S(1)} %constant_dynamic-update-slice_fusion.8), channel_id=1, source_target_pairs={{0,1},{1,0},{2,3},{3,2},{4,5},{5,4},{6,7},{7,6},{8,9},{9,8},{10,11... | collective-permute-start | bytes 49160 | tf_op jit(solution)/shard_map/ppermute | solution.py:153
  35.8 1.2 %collective-permute-start.2 = (f32[2,2048]{1,0:T(2,128)S(1)}, f32[2,2048]{1,0:T(2,128)S(1)}, u32[]{:S(2)}, u32[]{:S(2)}) collective-permute-start(f32[2,2048]{1,0:T(2,128)S(1)} %constant_dynamic-update-slice_fusion), channel_id=1, source_target_pairs={{0,1},{1,0},{2,3},{3,2},{4,5},{5,4},{6,7},{7,6},{8,9},{9,8},{10,11... | collective-permute-start | bytes 49160 | tf_op jit(solution)/shard_map/ppermute | solution.py:153

commit v4 on v3

--- a/solution.py
+++ b/solution.py
@@ -2,6 +2,8 @@
 import jax.numpy as jnp
 from jax import lax
 from jax.sharding import PartitionSpec as P
+from jax.experimental import pallas as pl
+from jax.experimental.pallas import tpu as pltpu
 
 ITERS = 3
 
@@ -56,6 +58,56 @@
     )
 
 
+def prep_kernel(hard_ref, width_ref, pos_ref, species_ref, desc_ref, readout_ref, out_ref):
+    kinds = species_ref[...]
+    hard = jnp.zeros(kinds.shape, jnp.float32)
+    width = jnp.zeros(kinds.shape, jnp.float32)
+    for kind in range(hard_ref.shape[0]):
+        hard = jnp.where(kinds == kind, hard_ref[kind], hard)
+        width = jnp.where(kinds == kind, width_ref[kind], width)
+    scores = lax.dot_general(
+        readout_ref[...],
+        desc_ref[...],
+        (((1,), (1,)), ((), ())),
+        precision=lax.Precision.HIGHEST,
+        preferred_element_type=jnp.float32,
+    )
+    negativity = jnp.zeros(kinds.shape, jnp.float32)
+    for kind in range(hard_ref.shape[0]):
+        negativity = jnp.where(kinds == kind, scores[kind : kind + 1, :], negativity)
+    self_term = hard + 1.0 / (width * ROOT_PI)
+    block = jnp.concatenate(
+        [pos_ref[...], width * width, negativity, self_term, jnp.zeros((2,) + kinds.shape[1:], jnp.float32)], 0
+    )
+    for slot in range(out_ref.shape[0]):
+        out_ref[slot] = block
+
+
+def prep(positions, species, descriptors, readout, hardness, widths, devices):
+    per_brick = species.shape[-1]
+    smem = pltpu.MemorySpace.SMEM if hasattr(pltpu, "MemorySpace") else pltpu.SMEM
+    return pl.pallas_call(
+        prep_kernel,
+        in_specs=[
+            pl.BlockSpec(memory_space=smem),
+            pl.BlockSpec(memory_space=smem),
+            pl.BlockSpec(memory_space=pltpu.VMEM),
+            pl.BlockSpec(memory_space=pltpu.VMEM),
+            pl.BlockSpec(memory_space=pltpu.VMEM),
+            pl.BlockSpec(memory_space=pltpu.VMEM),
+        ],
+        out_specs=pl.BlockSpec(memory_space=pltpu.VMEM),
+        out_shape=jax.ShapeDtypeStruct((devices, 8, per_brick), jnp.float32),
+    )(
+        hardness,
+        widths,
+        positions.reshape(3, per_brick),
+        species.reshape(1, per_brick),
+        descriptors.reshape(descriptors.shape[0], per_brick).T,
+        readout,
+    )
+
+
 def make_shards(rows, cols):
     devices = rows * cols
     everyone = ("row", "col")
@@ -69,26 +121,9 @@
         per_brick = species.shape[-1]
         atoms = devices * per_brick
         me = lax.axis_index("row") * cols + lax.axis_index("col")
-        kind_range = jnp.arange(hardness.shape[0], dtype=jnp.int32)
-        onehot = (kind_range[:, None] == species.reshape(1, per_brick)).astype(jnp.float32)
-        hard_atom = jnp.sum(onehot * hardness[:, None], 0)
-        width_atom = jnp.sum(onehot * widths[:, None], 0)
-        features = descriptors.reshape(descriptors.shape[0], per_brick)
-        atom_weights = jnp.zeros(features.shape, jnp.float32)
-        for kind in range(hardness.shape[0]):
-            atom_weights = atom_weights + onehot[kind][None, :] * readout[kind][:, None]
-        negativity = jnp.sum(features * atom_weights, 0)
-        self_term = hard_atom + 1.0 / (width_atom * ROOT_PI)
-        own = jnp.concatenate(
-            [
-                positions.reshape(3, per_brick),
-                (width_atom * width_atom)[None],
-                negativity[None],
-                self_term[None],
-            ],
-            0,
-        )
-        geometry = gather_all(own)
+        payload = prep(positions, species, descriptors, readout, hardness, widths, devices)
+        geometry = lax.all_to_all(payload, everyone, 0, 2, tiled=True)[0]
+        own = lax.dynamic_slice_in_dim(geometry, me * per_brick, per_brick, 1)
         col_index = jnp.arange(atoms, dtype=jnp.int32)
 
         pair = devices % 2 == 0 and (atoms // 2) * atoms * 4 <= PAIR_LIMIT
@@ -96,8 +131,8 @@
             parity = me % 2
             halves = devices // 2
             row_geometry = lax.dynamic_index_in_dim(
-                geometry.reshape(6, halves, 2, per_brick), parity, 2, keepdims=False
-            ).reshape(6, -1)
+                geometry.reshape(geometry.shape[0], halves, 2, per_brick), parity, 2, keepdims=False
+            ).reshape(geometry.shape[0], -1)
             brick_of = 2 * jnp.arange(halves, dtype=jnp.int32) + parity
             row_index = (brick_of[:, None] * per_brick + jnp.arange(per_brick, dtype=jnp.int32)[None]).reshape(-1)
             partner = [(i, i ^ 1) for i in range(devices)]

time: 41.7 us -> 41.6 us (level)
  other arithmetic: 16.2 us -> 13.8 us
  Pallas kernels: 0 us -> 1.63 us
  local copies, waits for them, and re-layouts: 4.76 us -> 5.51 us
    reduce_sum x2 -> x0, other arithmetic: 1.74 us -> none  [the longest x1 0.96 us: shards(): negativity = jnp.sum(features * atom_weights, 0)]
    pallas_call x0 -> x1, Pallas kernels: none -> 1.63 us  [prep(): pl.pallas_call(prep_kernel, in_specs=[pl.BlockSpec(memory_space=smem), pl...]
    unnamed x9 -> x11, local copies, waits for them, and re-layouts: 1.51 us -> 3.02 us
    mul x2 -> x0, local copies, waits for them, and re-layouts: 0.84 us -> none  [shards(): atom_weights = atom_weights + onehot[kind][None, :] * readout[kind][:, None]]
    convert_element_type x1 -> x0, other arithmetic: 0.66 us -> none  [shards(): (kind_range[:, None] == species.reshape(1, per_brick)).astype(jnp.float32)]
where the time goes in v4:
time: 41.6 us; the launch traced here: 41.3 us
  other arithmetic  13.8 us (33%)
  waiting for transfers between devices  10.1 us (24%)
  starting transfers between devices  7.94 us (19%)
  local copies, waits for them, and re-layouts  5.51 us (13%)
  between operations  2.3 us (6%)
  Pallas kernels  1.63 us (4%)
    all_to_all x1, waiting for transfers between devices, shards(): geometry = lax.all_to_all(payload, everyone, 0, 2, tiled=True)[0]  7.34 us
    all_to_all x1, starting transfers between devices, shards(): geometry = lax.all_to_all(payload, everyone, 0, 2, tiled=True)[0]  7.3 us
    reduce_sum x5, other arithmetic, operate(): backward = jnp.sum(matrix[None, :, :] * row_part[:, :, None], 1)  5.99 us
    select_n x2, other arithmetic, screened(): return jnp.where(self_pair, row_geometry[5][:, None], off)  3.74 us
    unnamed x11, local copies, waits for them, and re-layouts  3.02 us
    ppermute x3, waiting for transfers between devices, operate(): return partial + lax.ppermute(partial, everyone, partner)  2.74 us
    pallas_call x1, Pallas kernels, prep(): pl.pallas_call(prep_kernel, in_specs=[pl.BlockSpec(memory_space=smem), pl...  1.63 us
  transfers between devices with their start and end apart: 4, of which 4 were waited for; matrix products, arithmetic and copies ran while one was open for 1% of the time, Pallas kernels for 0%

profile of v4, /device:TPU:0, one launch (start us, length us, event | category | flops | bytes accessed | tf_op | source)
XLA Modules:
  0.0 41.3 jit_solution(10758897714231511343)
XLA Ops:
  0.6 1.3 %copy.12 = f32[3,1,1,64]{3,0,1,2:T(4,128)} copy(f32[3,1,1,64]{3,2,1,0:T(1,128)} %param.6) | data formatting | bytes 1536
  1.9 1.6 %shard_map.77 = f32[32,8,64]{2,1,0:T(8,128)} custom-call(f32[4]{0:T(128)} %hard_ref.1, f32[4]{0:T(128)} %width_ref.1, f32[3,64]{1,0:T(4,128)} %bitcast.57, s32[1,64]{1,0:T(1,128)} %bitcast.82, f32[64,128]{1,0:T(8,128)} %bitcast.55, f32[4,128]{1,0:T(4,128)} %readout_ref.1), custom_call_target="tpu_custom_call" | custom-call | tf_op jit(solution)/shard_map/pallas_call | solution.py:89
  3.5 1.6 %reshape.1072 = f32[32,1,512]{2,1,0:T(1,128)} reshape(f32[32,8,64]{2,1,0:T(8,128)} %shard_map.77) | data formatting | bytes 131072
  5.2 7.3 %all-to-all-start = ((f32[32,1,512]{2,1,0:T(1,128)}), f32[32,1,512]{2,1,0:T(1,128)S(1)}, u32[]{:S(2)}, u32[]{:S(2)}) async-start(f32[32,1,512]{2,1,0:T(1,128)} %reshape.1072), calls=%async_computation | async-start | bytes 131072 | tf_op jit(solution)/shard_map/all_to_all | solution.py:125
  12.6 7.3 %all-to-all-done = f32[32,1,512]{2,1,0:T(1,128)S(1)} async-done(((f32[32,1,512]{2,1,0:T(1,128)}), f32[32,1,512]{2,1,0:T(1,128)S(1)}, u32[]{:S(2)}, u32[]{:S(2)}) %all-to-all-start) | async-done | bytes 65568 | tf_op jit(solution)/shard_map/all_to_all | solution.py:125
  19.9 0.5 %broadcast.635 = f32[]{:T(128)} broadcast(f32[]{:T(128)} %constant.159), dimensions={} | broadcast | bytes 8 | tf_op jit(solution)/shard_map/all_to_all | solution.py:125
  20.4 0.8 %reduce.20 = f32[32,512]{1,0:T(8,128)S(1)} reduce(f32[32,1,512]{2,1,0:T(1,128)S(1)} %all-to-all-done, f32[]{:T(128)} %broadcast.635), dimensions={1}, to_apply=%all_to_all.11.reduce_sub_computation | reduce | bytes 131076 | tf_op jit(solution)/shard_map/all_to_all | solution.py:125
  21.3 0.2 slice_reduce_fusion.3
  21.9 2.2 %compare_select_fusion.6 = (f32[512,512]{1,0:T(8,128)S(1)}, f32[512,512]{1,0:T(8,128)S(1)}, f32[512,512]{1,0:T(8,128)S(1)}) fusion(f32[512]{0:T(512)S(1)} %bitcast.81, f32[512]{0:T(512)S(1)} %bitcast.76, f32[512]{0:T(512)S(1)} %bitcast.77, f32[512]{0:T(512)S(1)} %bitcast.78, f32[512]{0:T(512)S(1)} %bitcast.79, s32[512]{0:T(512)S(1)} %iota_add_fusion.3, ...), kind=kLoop, calls=%fused_computation.30 | loop fusion | flops 12582912 | bytes 3170304 | tf_op jit(solution)/shard_map/jit(_where)/select_n | solution.py:30
  24.1 1.5 %compare_select_fusion = (f32[512,512]{1,0:T(8,128)S(1)}, f32[512,512]{1,0:T(8,128)S(1)}) fusion(f32[512]{0:T(512)S(1)} %bitcast.62, f32[512]{0:T(512)S(1)} %bitcast.63, f32[512]{0:T(512)S(1)} %bitcast.64, f32[512]{0:T(512)S(1)} %bitcast.65, f32[512]{0:T(512)S(1)} %bitcast.58, f32[512]{0:T(512)S(1)} %bitcast.69, f32[512]{0:T(512)S(1)} %bitcast.59, ...), kind=kLoop, calls=%fused_computation.24 | loop fusion | flops 8388608 | bytes 2129920 | tf_op jit(solution)/shard_map/jit(_where)/select_n | solution.py:30
  25.7 1.5 %multiply_reduce_fusion.16 = (f32[2,512]{1,0:T(2,128)S(1)}, f32[2,512]{1,0:T(2,128)S(1)}, f32[2,512]{1,0:T(2,128)S(1)}, f32[2,512]{1,0:T(2,128)S(1)}, f32[2,512]...) fusion(f32[2,512]{1,0:T(2,128)S(1)} %get-tuple-element.86, ...), kind=kLoop, calls=%fused_computation.16 | loop fusion | flops 8380416 | bytes 5296128 | tf_op jit(solution)/shard_map/reduce_sum | solution.py:184
  27.6 1.1 %collective-permute-done = f32[2,2048]{1,0:T(2,128)S(1)} collective-permute-done((f32[2,2048]{1,0:T(2,128)S(1)}, f32[2,2048]{1,0:T(2,128)S(1)}, u32[]{:S(2)}, u32[]{:S(2)}) %collective-permute-start) | collective-permute-done | bytes 16416 | tf_op jit(solution)/shard_map/ppermute | solution.py:188
  29.1 2.3 %multiply_reduce_fusion.12 = (f32[2,512]{1,0:T(2,128)S(1)}, f32[2,512]{1,0:T(2,128)S(1)}, f32[2,512]{1,0:T(2,128)S(1)}, f32[2,512]{1,0:T(2,128)S(1)}) fusion(f32[2,512]{1,0:T(2,128)S(1)} %get-tuple-element.78, f32[512,512]{1,0:T(8,128)} %copy-done, f32[2,512]{1,0:T(2,128)S(1)} %get-tuple-element.77, f32[512,512]{1,0:T(8,128)} %copy-done.2, ...), kind=kLoop, calls=%fused_computation.12 | loop fusion | flops 4190208 | bytes 3170304 | tf_op jit(solution)/shard_map/reduce_sum | solution.py:184
  31.5 0.7 %multiply_reduce_fusion.8 = (f32[2,512]{1,0:T(2,128)S(1)}, f32[2,512]{1,0:T(2,128)S(1)}, f32[2,512]{1,0:T(2,128)S(1)}, f32[2,512]{1,0:T(2,128)S(1)}) fusion(f32[2,512]{1,0:T(2,128)S(1)} %get-tuple-element.74, f32[512,512]{1,0:T(8,128)S(1)} %get-tuple-element.82, f32[2,512]{1,0:T(2,128)S(1)} %get-tuple-element.76, f32[2,512]{1,0:T(2,128)S(1)} %get-tuple-element.75, ...), kind=kLoop, calls=%fused_computation.8 | loop fusion | flops 4190208 | bytes 2125824 | tf_op jit(solution)/shard_map/reduce_sum | solution.py:184
  32.3 0.2 collective-permute-start.1
  32.6 0.9 %collective-permute-done.1 = f32[2,2048]{1,0:T(2,128)S(1)} collective-permute-done((f32[2,2048]{1,0:T(2,128)S(1)}, f32[2,2048]{1,0:T(2,128)S(1)}, u32[]{:S(2)}, u32[]{:S(2)}) %collective-permute-start.1) | collective-permute-done | bytes 16416 | tf_op jit(solution)/shard_map/ppermute | solution.py:188
  34.1 0.7 %multiply_reduce_fusion.4 = (f32[2,512]{1,0:T(2,128)S(1)}, f32[2,512]{1,0:T(2,128)S(1)}, f32[2,512]{1,0:T(2,128)S(1)}, f32[2,512]{1,0:T(2,128)S(1)}) fusion(f32[2,512]{1,0:T(2,128)S(1)} %get-tuple-element.73, f32[512,512]{1,0:T(8,128)S(1)} %copy-done.1, f32[2,512]{1,0:T(2,128)S(1)} %get-tuple-element.72, f32[512,512]{1,0:T(8,128)S(1)} %copy-done.3, ...), kind=kLoop, calls=%fused_computation.4 | loop fusion | flops 4190208 | bytes 3170304 | tf_op jit(solution)/shard_map/reduce_sum | solution.py:184
  35.0 0.7 %multiply_reduce_fusion = (f32[2,512]{1,0:T(2,128)S(1)}, f32[2,512]{1,0:T(2,128)S(1)}, f32[2,512]{1,0:T(2,128)S(1)}, f32[2,512]{1,0:T(2,128)S(1)}) fusion(f32[2,512]{1,0:T(2,128)S(1)} %get-tuple-element.69, f32[512,512]{1,0:T(8,128)S(1)} %get-tuple-element.82, f32[2,512]{1,0:T(2,128)S(1)} %get-tuple-element.71, f32[2,512]{1,0:T(2,128)S(1)} %get-tuple-element.70, ...), kind=kLoop, calls=%fused_computation | loop fusion | flops 4190208 | bytes 2125824 | tf_op jit(solution)/shard_map/reduce_sum | solution.py:184
  35.8 0.2 collective-permute-start.2
  36.3 0.7 %collective-permute-done.2 = f32[2,2048]{1,0:T(2,128)S(1)} collective-permute-done((f32[2,2048]{1,0:T(2,128)S(1)}, f32[2,2048]{1,0:T(2,128)S(1)}, u32[]{:S(2)}, u32[]{:S(2)}) %collective-permute-start.2) | collective-permute-done | bytes 16416 | tf_op jit(solution)/shard_map/ppermute | solution.py:188
  37.4 0.6 %fusion.40 = (f32[1]{0:T(128)}, f32[1]{0:T(128)}) fusion(f32[2]{0:T(128)S(1)} %get-tuple-element.36), kind=kLoop, calls=%fused_computation.177 | loop fusion | bytes 16 | tf_op jit(solution)/shard_map/slice | solution.py:210
  39.3 0.6 %fusion.33 = (f32[64]{0:T(128)S(1)}, f32[1,1,64]{2,1,0:T(1,128)}) fusion(f32[1,2048]{1,0:T(1,128)S(1)} %fusion.17, s32[]{:T(128)S(6)} %select_n.209), kind=kLoop, calls=%fused_computation.171 | loop fusion | bytes 772 | tf_op jit(solution)/shard_map/dynamic_slice | solution.py:213
  39.9 0.8 %fusion.5 = (f32[64]{0:T(128)S(1)}, f32[64]{0:T(128)S(1)}, f32[64]{0:T(128)S(1)}) fusion(f32[2048]{0:T(1024)S(1)} %sub.379, f32[64]{0:T(128)S(1)} %get-tuple-element.94, f32[2048]{0:T(1024)S(1)} %bitcast.56, f32[2048]{0:T(1024)S(1)} %sub.389, f32[64]{0:T(128)S(1)} %get-tuple-element.92, f32[2048]{0:T(1024)S(1)} %sub.384, f32[64]{0:T(128)S(1)} %get-tuple-element.93, ...), kind=kLoop, calls=%fused_computation.52 | loop fusion | flops 4063040 | bytes 43008 | tf_op jit(solution)/shard_map/reduce_sum | solution.py:54
  40.7 0.6 %maximum_multiply_fusion = f32[3,1,1,64]{3,2,1,0:T(1,128)} fusion(f32[1,1,1,64]{3,2,1,0:T(1,128)S(1)} %bitcast.84, f32[1,1,1,64]{3,2,1,0:T(1,128)S(1)} %bitcast.85, f32[1,1,1,64]{3,2,1,0:T(1,128)S(1)} %bitcast.83, f32[64]{0:T(128)S(1)} %get-tuple-element.84), kind=kLoop, calls=%fused_computation.165 | loop fusion | flops 576 | bytes 1792 | tf_op jit(solution)/shard_map/mul | solution.py:215
  (69 shorter events, 2.8 us)
Async XLA Ops:
  5.2 14.7 %all-to-all-start = ((f32[32,1,512]{2,1,0:T(1,128)}), f32[32,1,512]{2,1,0:T(1,128)S(1)}, u32[]{:S(2)}, u32[]{:S(2)}) async-start(f32[32,1,512]{2,1,0:T(1,128)} %reshape.1072), calls=%async_computation | async-start | bytes 131072 | tf_op jit(solution)/shard_map/all_to_all | solution.py:125
  24.1 1.6 %copy-start = (f32[512,512]{1,0:T(8,128)}, f32[512,512]{1,0:T(8,128)S(1)}, u32[]{:S(2)}) copy-start(f32[512,512]{1,0:T(8,128)S(1)} %get-tuple-element.80) | copy-start | bytes 3145732
  24.1 1.6 %copy-start.2 = (f32[512,512]{1,0:T(8,128)}, f32[512,512]{1,0:T(8,128)S(1)}, u32[]{:S(2)}) copy-start(f32[512,512]{1,0:T(8,128)S(1)} %get-tuple-element.81) | copy-start | bytes 3145732
  27.4 1.2 %collective-permute-start = (f32[2,2048]{1,0:T(2,128)S(1)}, f32[2,2048]{1,0:T(2,128)S(1)}, u32[]{:S(2)}, u32[]{:S(2)}) collective-permute-start(f32[2,2048]{1,0:T(2,128)S(1)} %constant_dynamic-update-slice_fusion.16), channel_id=1, source_target_pairs={{0,1},{1,0},{2,3},{3,2},{4,5},{5,4},{6,7},{7,6},{8,9},{9,8},{10,11... | collective-permute-start | bytes 49160 | tf_op jit(solution)/shard_map/ppermute | solution.py:188
  31.5 2.6 %copy-start.1 = (f32[512,512]{1,0:T(8,128)S(1)}, f32[512,512]{1,0:T(8,128)}, u32[]{:S(2)}) copy-start(f32[512,512]{1,0:T(8,128)} %copy-done) | copy-start | bytes 3145732
  31.5 2.6 %copy-start.3 = (f32[512,512]{1,0:T(8,128)S(1)}, f32[512,512]{1,0:T(8,128)}, u32[]{:S(2)}) copy-start(f32[512,512]{1,0:T(8,128)} %copy-done.2) | copy-start | bytes 3145732
  32.3 1.2 %collective-permute-start.1 = (f32[2,2048]{1,0:T(2,128)S(1)}, f32[2,2048]{1,0:T(2,128)S(1)}, u32[]{:S(2)}, u32[]{:S(2)}) collective-permute-start(f32[2,2048]{1,0:T(2,128)S(1)} %constant_dynamic-update-slice_fusion.8), channel_id=1, source_target_pairs={{0,1},{1,0},{2,3},{3,2},{4,5},{5,4},{6,7},{7,6},{8,9},{9,8},{10,11... | collective-permute-start | bytes 49160 | tf_op jit(solution)/shard_map/ppermute | solution.py:188
  35.8 1.2 %collective-permute-start.2 = (f32[2,2048]{1,0:T(2,128)S(1)}, f32[2,2048]{1,0:T(2,128)S(1)}, u32[]{:S(2)}, u32[]{:S(2)}) collective-permute-start(f32[2,2048]{1,0:T(2,128)S(1)} %constant_dynamic-update-slice_fusion), channel_id=1, source_target_pairs={{0,1},{1,0},{2,3},{3,2},{4,5},{5,4},{6,7},{7,6},{8,9},{9,8},{10,11... | collective-permute-start | bytes 49160 | tf_op jit(solution)/shard_map/ppermute | solution.py:188

commit v5 on v4

--- a/solution.py
+++ b/solution.py
@@ -76,9 +76,10 @@
     for kind in range(hard_ref.shape[0]):
         negativity = jnp.where(kinds == kind, scores[kind : kind + 1, :], negativity)
     self_term = hard + 1.0 / (width * ROOT_PI)
-    block = jnp.concatenate(
-        [pos_ref[...], width * width, negativity, self_term, jnp.zeros((2,) + kinds.shape[1:], jnp.float32)], 0
-    )
+    per_brick = kinds.shape[-1]
+    features = [pos_ref[0], pos_ref[1], pos_ref[2], width * width, negativity, self_term]
+    features = features + [jnp.zeros(kinds.shape, jnp.float32)] * (out_ref.shape[-1] // per_brick - len(features))
+    block = jnp.concatenate(features, 1)
     for slot in range(out_ref.shape[0]):
         out_ref[slot] = block
 
@@ -97,11 +98,11 @@
             pl.BlockSpec(memory_space=pltpu.VMEM),
         ],
         out_specs=pl.BlockSpec(memory_space=pltpu.VMEM),
-        out_shape=jax.ShapeDtypeStruct((devices, 8, per_brick), jnp.float32),
+        out_shape=jax.ShapeDtypeStruct((devices, 1, 8 * per_brick), jnp.float32),
     )(
         hardness,
         widths,
-        positions.reshape(3, per_brick),
+        positions.reshape(3, 1, per_brick),
         species.reshape(1, per_brick),
         descriptors.reshape(descriptors.shape[0], per_brick).T,
         readout,
@@ -122,7 +123,8 @@
         atoms = devices * per_brick
         me = lax.axis_index("row") * cols + lax.axis_index("col")
         payload = prep(positions, species, descriptors, readout, hardness, widths, devices)
-        geometry = lax.all_to_all(payload, everyone, 0, 2, tiled=True)[0]
+        got = lax.all_to_all(payload, everyone, 0, 0, tiled=True)
+        geometry = jnp.moveaxis(got.reshape(devices, 8, per_brick), 0, 1).reshape(8, atoms)
         own = lax.dynamic_slice_in_dim(geometry, me * per_brick, per_brick, 1)
         col_index = jnp.arange(atoms, dtype=jnp.int32)
 

time: 41.6 us -> 37.6 us (0.904)
  local copies, waits for them, and re-layouts: 5.51 us -> 2.08 us
  other arithmetic: 13.8 us -> 13.3 us
    unnamed x11 -> x8, local copies, waits for them, and re-layouts: 3.02 us -> 0.02 us
    all_to_all x1, other arithmetic: 0.8 us -> 0.15 us  [shards(): got = lax.all_to_all(payload, everyone, 0, 0, tiled=True)]
    all_to_all x2 -> x0, local copies, waits for them, and re-layouts: 0.54 us -> none  [shards(): geometry = lax.all_to_all(payload, everyone, 0, 2, tiled=True)[0]]
where the time goes in v5:
time: 37.6 us; the launch traced here: 37.3 us
  other arithmetic  13.3 us (35%)
  waiting for transfers between devices  10.1 us (27%)
  starting transfers between devices  7.94 us (21%)
  between operations  2.3 us (6%)
  local copies, waits for them, and re-layouts  2.08 us (6%)
  Pallas kernels  1.61 us (4%)
    all_to_all x1, waiting for transfers between devices, shards(): got = lax.all_to_all(payload, everyone, 0, 0, tiled=True)  7.34 us
    all_to_all x1, starting transfers between devices, shards(): got = lax.all_to_all(payload, everyone, 0, 0, tiled=True)  7.3 us
    reduce_sum x5, other arithmetic, operate(): backward = jnp.sum(matrix[None, :, :] * row_part[:, :, None], 1)  5.99 us
    select_n x2, other arithmetic, screened(): return jnp.where(self_pair, row_geometry[5][:, None], off)  3.81 us
    ppermute x3, waiting for transfers between devices, operate(): return partial + lax.ppermute(partial, everyone, partner)  2.74 us
    pallas_call x1, Pallas kernels, prep(): pl.pallas_call(prep_kernel, in_specs=[pl.BlockSpec(memory_space=smem), pl...  1.61 us
    reduce_sum x1, other arithmetic, pulling(): jnp.sum(slope * separations[0], 1)  0.81 us
  transfers between devices with their start and end apart: 4, of which 4 were waited for; matrix products, arithmetic and copies ran while one was open for 1% of the time, Pallas kernels for 0%

profile of v5, /device:TPU:0, one launch (start us, length us, event | category | flops | bytes accessed | tf_op | source)
XLA Modules:
  0.0 37.3 jit_solution(3742795961779992043)
XLA Ops:
  0.6 1.6 %shard_map.77 = f32[32,1,512]{2,1,0:T(1,128)} custom-call(f32[4]{0:T(128)} %hard_ref.1, f32[4]{0:T(128)} %width_ref.1, f32[3,1,64]{2,1,0:T(1,128)} %bitcast.75, s32[1,64]{1,0:T(1,128)} %bitcast.76, f32[64,128]{1,0:T(8,128)} %bitcast.49, f32[4,128]{1,0:T(4,128)} %readout_ref.1), custom_call_target="tpu_custom_call" | custom-call | tf_op jit(solution)/shard_map/pallas_call | solution.py:90
  2.2 7.3 %all-to-all-start = ((f32[32,1,512]{2,1,0:T(1,128)}), f32[32,1,512]{2,1,0:T(1,128)S(1)}, u32[]{:S(2)}, u32[]{:S(2)}) async-start(f32[32,1,512]{2,1,0:T(1,128)} %shard_map.77), calls=%async_computation | async-start | bytes 131072 | tf_op jit(solution)/shard_map/all_to_all | solution.py:126
  9.6 7.3 %all-to-all-done = f32[32,1,512]{2,1,0:T(1,128)S(1)} async-done(((f32[32,1,512]{2,1,0:T(1,128)}), f32[32,1,512]{2,1,0:T(1,128)S(1)}, u32[]{:S(2)}, u32[]{:S(2)}) %all-to-all-start) | async-done | bytes 65568 | tf_op jit(solution)/shard_map/all_to_all | solution.py:126
  17.2 0.2 slice_reduce_fusion.3
  17.8 2.3 %compare_select_fusion.6 = (f32[512,512]{1,0:T(8,128)S(1)}, f32[512,512]{1,0:T(8,128)S(1)}, f32[512,512]{1,0:T(8,128)S(1)}) fusion(f32[512]{0:T(512)S(1)} %bitcast.74, f32[512]{0:T(512)S(1)} %bitcast.69, f32[512]{0:T(512)S(1)} %bitcast.70, f32[512]{0:T(512)S(1)} %bitcast.71, f32[512]{0:T(512)S(1)} %bitcast.72, s32[512]{0:T(512)S(1)} %iota_add_fusion.3, ...), kind=kLoop, calls=%fused_computation.30 | loop fusion | flops 12582912 | bytes 3170304 | tf_op jit(solution)/shard_map/jit(_where)/select_n | solution.py:30
  20.1 1.5 %compare_select_fusion = (f32[512,512]{1,0:T(8,128)S(1)}, f32[512,512]{1,0:T(8,128)S(1)}) fusion(f32[512]{0:T(512)S(1)} %bitcast.55, f32[512]{0:T(512)S(1)} %bitcast.56, f32[512]{0:T(512)S(1)} %bitcast.57, f32[512]{0:T(512)S(1)} %bitcast.58, f32[512]{0:T(512)S(1)} %bitcast.51, f32[512]{0:T(512)S(1)} %bitcast.62, f32[512]{0:T(512)S(1)} %bitcast.52, ...), kind=kLoop, calls=%fused_computation.24 | loop fusion | flops 8388608 | bytes 2129920 | tf_op jit(solution)/shard_map/jit(_where)/select_n | solution.py:30
  21.7 1.5 %multiply_reduce_fusion.16 = (f32[2,512]{1,0:T(2,128)S(1)}, f32[2,512]{1,0:T(2,128)S(1)}, f32[2,512]{1,0:T(2,128)S(1)}, f32[2,512]{1,0:T(2,128)S(1)}, f32[2,512]...) fusion(f32[2,512]{1,0:T(2,128)S(1)} %get-tuple-element.86, ...), kind=kLoop, calls=%fused_computation.16 | loop fusion | flops 8380416 | bytes 5296128 | tf_op jit(solution)/shard_map/reduce_sum | solution.py:186
  23.6 1.1 %collective-permute-done = f32[2,2048]{1,0:T(2,128)S(1)} collective-permute-done((f32[2,2048]{1,0:T(2,128)S(1)}, f32[2,2048]{1,0:T(2,128)S(1)}, u32[]{:S(2)}, u32[]{:S(2)}) %collective-permute-start) | collective-permute-done | bytes 16416 | tf_op jit(solution)/shard_map/ppermute | solution.py:190
  24.8 0.2 multiply_reduce_fusion.27
  25.1 2.3 %multiply_reduce_fusion.12 = (f32[2,512]{1,0:T(2,128)S(1)}, f32[2,512]{1,0:T(2,128)S(1)}, f32[2,512]{1,0:T(2,128)S(1)}, f32[2,512]{1,0:T(2,128)S(1)}) fusion(f32[2,512]{1,0:T(2,128)S(1)} %get-tuple-element.78, f32[512,512]{1,0:T(8,128)} %copy-done, f32[2,512]{1,0:T(2,128)S(1)} %get-tuple-element.77, f32[512,512]{1,0:T(8,128)} %copy-done.2, ...), kind=kLoop, calls=%fused_computation.12 | loop fusion | flops 4190208 | bytes 3170304 | tf_op jit(solution)/shard_map/reduce_sum | solution.py:186
  27.5 0.7 %multiply_reduce_fusion.8 = (f32[2,512]{1,0:T(2,128)S(1)}, f32[2,512]{1,0:T(2,128)S(1)}, f32[2,512]{1,0:T(2,128)S(1)}, f32[2,512]{1,0:T(2,128)S(1)}) fusion(f32[2,512]{1,0:T(2,128)S(1)} %get-tuple-element.74, f32[512,512]{1,0:T(8,128)S(1)} %get-tuple-element.82, f32[2,512]{1,0:T(2,128)S(1)} %get-tuple-element.76, f32[2,512]{1,0:T(2,128)S(1)} %get-tuple-element.75, ...), kind=kLoop, calls=%fused_computation.8 | loop fusion | flops 4190208 | bytes 2125824 | tf_op jit(solution)/shard_map/reduce_sum | solution.py:186
  28.3 0.2 collective-permute-start.1
  28.6 0.9 %collective-permute-done.1 = f32[2,2048]{1,0:T(2,128)S(1)} collective-permute-done((f32[2,2048]{1,0:T(2,128)S(1)}, f32[2,2048]{1,0:T(2,128)S(1)}, u32[]{:S(2)}, u32[]{:S(2)}) %collective-permute-start.1) | collective-permute-done | bytes 16416 | tf_op jit(solution)/shard_map/ppermute | solution.py:190
  29.6 0.2 multiply_reduce_fusion.26
  29.8 0.2 multiply_reduce_fusion.25
  30.1 0.7 %multiply_reduce_fusion.4 = (f32[2,512]{1,0:T(2,128)S(1)}, f32[2,512]{1,0:T(2,128)S(1)}, f32[2,512]{1,0:T(2,128)S(1)}, f32[2,512]{1,0:T(2,128)S(1)}) fusion(f32[2,512]{1,0:T(2,128)S(1)} %get-tuple-element.73, f32[512,512]{1,0:T(8,128)S(1)} %copy-done.1, f32[2,512]{1,0:T(2,128)S(1)} %get-tuple-element.72, f32[512,512]{1,0:T(8,128)S(1)} %copy-done.3, ...), kind=kLoop, calls=%fused_computation.4 | loop fusion | flops 4190208 | bytes 3170304 | tf_op jit(solution)/shard_map/reduce_sum | solution.py:186
  31.0 0.7 %multiply_reduce_fusion = (f32[2,512]{1,0:T(2,128)S(1)}, f32[2,512]{1,0:T(2,128)S(1)}, f32[2,512]{1,0:T(2,128)S(1)}, f32[2,512]{1,0:T(2,128)S(1)}) fusion(f32[2,512]{1,0:T(2,128)S(1)} %get-tuple-element.69, f32[512,512]{1,0:T(8,128)S(1)} %get-tuple-element.82, f32[2,512]{1,0:T(2,128)S(1)} %get-tuple-element.71, f32[2,512]{1,0:T(2,128)S(1)} %get-tuple-element.70, ...), kind=kLoop, calls=%fused_computation | loop fusion | flops 4190208 | bytes 2125824 | tf_op jit(solution)/shard_map/reduce_sum | solution.py:186
  31.8 0.2 collective-permute-start.2
  32.3 0.7 %collective-permute-done.2 = f32[2,2048]{1,0:T(2,128)S(1)} collective-permute-done((f32[2,2048]{1,0:T(2,128)S(1)}, f32[2,2048]{1,0:T(2,128)S(1)}, u32[]{:S(2)}, u32[]{:S(2)}) %collective-permute-start.2) | collective-permute-done | bytes 16416 | tf_op jit(solution)/shard_map/ppermute | solution.py:190
  33.1 0.2 fusion.35
  33.4 0.6 %fusion.40 = (f32[1]{0:T(128)}, f32[1]{0:T(128)}) fusion(f32[2]{0:T(128)S(1)} %get-tuple-element.36), kind=kLoop, calls=%fused_computation.176 | loop fusion | bytes 16 | tf_op jit(solution)/shard_map/slice | solution.py:212
  35.3 0.6 %fusion.33 = (f32[64]{0:T(128)S(1)}, f32[1,1,64]{2,1,0:T(1,128)}) fusion(f32[1,2048]{1,0:T(1,128)S(1)} %fusion.17, s32[]{:T(128)S(6)} %select_n.209), kind=kLoop, calls=%fused_computation.170 | loop fusion | bytes 772 | tf_op jit(solution)/shard_map/dynamic_slice | solution.py:215
  35.9 0.8 %fusion.5 = (f32[64]{0:T(128)S(1)}, f32[64]{0:T(128)S(1)}, f32[64]{0:T(128)S(1)}) fusion(f32[2048]{0:T(1024)S(1)} %sub.379, f32[64]{0:T(128)S(1)} %get-tuple-element.94, f32[2048]{0:T(1024)S(1)} %bitcast.50, f32[2048]{0:T(1024)S(1)} %sub.389, f32[64]{0:T(128)S(1)} %get-tuple-element.92, f32[2048]{0:T(1024)S(1)} %sub.384, f32[64]{0:T(128)S(1)} %get-tuple-element.93, ...), kind=kLoop, calls=%fused_computation.52 | loop fusion | flops 4063040 | bytes 43008 | tf_op jit(solution)/shard_map/reduce_sum | solution.py:54
  36.7 0.6 %maximum_multiply_fusion = f32[3,1,1,64]{3,2,1,0:T(1,128)} fusion(f32[1,1,1,64]{3,2,1,0:T(1,128)S(1)} %bitcast.78, f32[1,1,1,64]{3,2,1,0:T(1,128)S(1)} %bitcast.79, f32[1,1,1,64]{3,2,1,0:T(1,128)S(1)} %bitcast.77, f32[64]{0:T(128)S(1)} %get-tuple-element.84), kind=kLoop, calls=%fused_computation.164 | loop fusion | flops 576 | bytes 1792 | tf_op jit(solution)/shard_map/mul | solution.py:217
  (66 shorter events, 2.1 us)
Async XLA Ops:
  2.2 14.7 %all-to-all-start = ((f32[32,1,512]{2,1,0:T(1,128)}), f32[32,1,512]{2,1,0:T(1,128)S(1)}, u32[]{:S(2)}, u32[]{:S(2)}) async-start(f32[32,1,512]{2,1,0:T(1,128)} %shard_map.77), calls=%async_computation | async-start | bytes 131072 | tf_op jit(solution)/shard_map/all_to_all | solution.py:126
  20.1 1.6 %copy-start = (f32[512,512]{1,0:T(8,128)}, f32[512,512]{1,0:T(8,128)S(1)}, u32[]{:S(2)}) copy-start(f32[512,512]{1,0:T(8,128)S(1)} %get-tuple-element.80) | copy-start | bytes 3145732
  20.1 1.6 %copy-start.2 = (f32[512,512]{1,0:T(8,128)}, f32[512,512]{1,0:T(8,128)S(1)}, u32[]{:S(2)}) copy-start(f32[512,512]{1,0:T(8,128)S(1)} %get-tuple-element.81) | copy-start | bytes 3145732
  23.4 1.2 %collective-permute-start = (f32[2,2048]{1,0:T(2,128)S(1)}, f32[2,2048]{1,0:T(2,128)S(1)}, u32[]{:S(2)}, u32[]{:S(2)}) collective-permute-start(f32[2,2048]{1,0:T(2,128)S(1)} %constant_dynamic-update-slice_fusion.16), channel_id=1, source_target_pairs={{0,1},{1,0},{2,3},{3,2},{4,5},{5,4},{6,7},{7,6},{8,9},{9,8},{10,11... | collective-permute-start | bytes 49160 | tf_op jit(solution)/shard_map/ppermute | solution.py:190
  27.5 2.6 %copy-start.1 = (f32[512,512]{1,0:T(8,128)S(1)}, f32[512,512]{1,0:T(8,128)}, u32[]{:S(2)}) copy-start(f32[512,512]{1,0:T(8,128)} %copy-done) | copy-start | bytes 3145732
  27.5 2.6 %copy-start.3 = (f32[512,512]{1,0:T(8,128)S(1)}, f32[512,512]{1,0:T(8,128)}, u32[]{:S(2)}) copy-start(f32[512,512]{1,0:T(8,128)} %copy-done.2) | copy-start | bytes 3145732
  28.3 1.2 %collective-permute-start.1 = (f32[2,2048]{1,0:T(2,128)S(1)}, f32[2,2048]{1,0:T(2,128)S(1)}, u32[]{:S(2)}, u32[]{:S(2)}) collective-permute-start(f32[2,2048]{1,0:T(2,128)S(1)} %constant_dynamic-update-slice_fusion.8), channel_id=1, source_target_pairs={{0,1},{1,0},{2,3},{3,2},{4,5},{5,4},{6,7},{7,6},{8,9},{9,8},{10,11... | collective-permute-start | bytes 49160 | tf_op jit(solution)/shard_map/ppermute | solution.py:190
  31.8 1.2 %collective-permute-start.2 = (f32[2,2048]{1,0:T(2,128)S(1)}, f32[2,2048]{1,0:T(2,128)S(1)}, u32[]{:S(2)}, u32[]{:S(2)}) collective-permute-start(f32[2,2048]{1,0:T(2,128)S(1)} %constant_dynamic-update-slice_fusion), channel_id=1, source_target_pairs={{0,1},{1,0},{2,3},{3,2},{4,5},{5,4},{6,7},{7,6},{8,9},{9,8},{10,11... | collective-permute-start | bytes 49160 | tf_op jit(solution)/shard_map/ppermute | solution.py:190

commit v6 on v5

--- a/solution.py
+++ b/solution.py
@@ -109,6 +109,28 @@
     )
 
 
+def pulling_matrices(row_geometry, col_geometry, self_pair):
+    separations = []
+    squared = jnp.zeros(self_pair.shape, row_geometry.dtype)
+    for axis_id in range(3):
+        separation = row_geometry[axis_id][:, None] - col_geometry[axis_id][None, :]
+        separations.append(separation)
+        squared = squared + separation * separation
+    squared = jnp.where(self_pair, 1.0, squared)
+    inverse = lax.rsqrt(squared)
+    screening = lax.rsqrt(2.0 * (row_geometry[3][:, None] + col_geometry[3][None, :]))
+    slope = (
+        (
+            lax.erf(screening * squared * inverse) * inverse
+            - TWO_ROOT * screening * jnp.exp(-screening * screening * squared)
+        )
+        * inverse
+        * inverse
+    )
+    slope = jnp.where(self_pair, 0.0, slope)
+    return [slope * separation for separation in separations]
+
+
 def make_shards(rows, cols):
     devices = rows * cols
     everyone = ("row", "col")
@@ -164,16 +186,16 @@
                 row_at = jnp.where(parity == 0, row_a, row_b) * group
                 col_at = jnp.where(parity == 0, col_a, col_b) * group
                 starts.append((row_at, col_at))
-                local = jnp.arange(group, dtype=jnp.int32)
+                offsets = jnp.arange(group, dtype=jnp.int32)
                 matrices.append(
                     screened(
                         lax.dynamic_slice_in_dim(geometry, row_at, group, 1),
                         lax.dynamic_slice_in_dim(geometry, col_at, group, 1),
-                        (row_at + local)[:, None] == (col_at + local)[None, :],
+                        (row_at + offsets)[:, None] == (col_at + offsets)[None, :],
                     )
                 )
 
-            def operate(vectors):
+            def partial_image(vectors):
                 partial = jnp.zeros_like(vectors)
                 for k, (matrix, (row_at, col_at)) in enumerate(zip(matrices, starts)):
                     col_part = lax.dynamic_slice_in_dim(vectors, col_at, group, 1)
@@ -187,33 +209,47 @@
                         partial = lax.dynamic_update_slice_in_dim(
                             partial, lax.dynamic_slice_in_dim(partial, col_at, group, 1) + backward, col_at, 1
                         )
+                return partial
+
+            def operate(vectors):
+                partial = partial_image(vectors)
                 return partial + lax.ppermute(partial, everyone, partner)
+
+            def curvature(vectors, ready):
+                mine, ready = lax.optimization_barrier((jnp.sum(vectors * partial_image(vectors), 1), ready))
+                return mine + lax.ppermute(mine, everyone, partner), ready
         else:
             matrix = screened(row_geometry, geometry, row_index[:, None] == col_index[None, :])
 
             def operate(vectors):
                 return assemble(jnp.sum(matrix[None, :, :] * vectors[:, None, :], 2))
+
+            def curvature(vectors, ready):
+                return jnp.sum(vectors * operate(vectors), 1), ready
 
         rhs = jnp.stack([-geometry[4], jnp.ones((atoms,), jnp.float32)])
         solution = jnp.zeros_like(rhs)
         resid = rhs
         direction = rhs
         norm_now = jnp.sum(resid * resid, 1)
-        for iteration in range(ITERS):
+        own_index = me * per_brick + jnp.arange(per_brick, dtype=jnp.int32)
+        for iteration in range(ITERS - 1):
             image = operate(direction)
             step_size = norm_now / jnp.sum(direction * image, 1)
             solution = solution + step_size[:, None] * direction
-            if iteration + 1 < ITERS:
-                resid = resid - step_size[:, None] * image
-                norm_next = jnp.sum(resid * resid, 1)
-                direction = resid + (norm_next / norm_now)[:, None] * direction
-                norm_now = norm_next
+            resid = resid - step_size[:, None] * image
+            norm_next = jnp.sum(resid * resid, 1)
+            direction = resid + (norm_next / norm_now)[:, None] * direction
+            norm_now = norm_next
+        pull = pulling_matrices(own, geometry, own_index[:, None] == col_index[None, :])
+        last_curvature, pull = curvature(direction, pull)
+        step_size = norm_now / last_curvature
+        solution = solution + step_size[:, None] * direction
         totals = jnp.sum(solution, 1)
-        lagrange = totals[0] / totals[1]
-        charges = solution[0] - lagrange * solution[1]
-        own_index = me * per_brick + jnp.arange(per_brick, dtype=jnp.int32)
+        weights = jnp.where(jnp.arange(2) == 0, 1.0, -(totals[::-1] / totals))
+        charges = jnp.sum(weights[:, None] * solution, 0)
         own_charges = lax.dynamic_slice_in_dim(charges, me * per_brick, per_brick, 0)
-        field = pulling(own, geometry, own_index[:, None] == col_index[None, :], charges)
+        field = jnp.stack([jnp.sum(part * charges[None, :], 1) for part in pull])
         forces = (own_charges[None, :] * field).reshape(3, 1, 1, per_brick)
         return (own_charges.reshape(1, 1, per_brick), forces)
 

time: 37.6 us -> 37.2 us (0.989)
  other arithmetic: 13.3 us -> 15.7 us
  between operations: 2.3 us -> 1 us
  waiting for transfers between devices: 10.1 us -> 8.84 us
  local copies, waits for them, and re-layouts: 2.08 us -> 1.68 us
    ppermute x3 -> x2, waiting for transfers between devices: 2.74 us -> 0.71 us  [operate(): return partial + lax.ppermute(partial, everyone, partner)]
    mul x0 -> x1, other arithmetic: none -> 1.85 us  [pulling_matrices(): return [slope * separation for separation in separations]]
    ppermute x0 -> x1, waiting for transfers between devices: none -> 0.82 us  [curvature(): return (mine + lax.ppermute(mine, everyone, partner), ready)]
    reduce_sum x6 -> x8, other arithmetic: 6.81 us -> 7.52 us  [the longest x5 5.99 us: partial_image(): backward = jnp.sum(matrix[None, :, :] * row_part[:, :, None], 1)]
    slice x1 -> x0, local copies, waits for them, and re-layouts: 0.59 us -> none  [shards(): lagrange = totals[0] / totals[1]]
    reshape x0 -> x1, local copies, waits for them, and re-layouts: none -> 0.59 us  [shards(): return (own_charges.reshape(1, 1, per_brick), forces)]
    dynamic_slice x1, local copies, waits for them, and re-layouts: 0.59 us -> 0.07 us  [shards(): lax.dynamic_slice_in_dim(charges, me * per_brick, per_brick, 0)]
    ppermute x0 -> x1, starting transfers between devices: none -> 0.4 us  [curvature(): return (mine + lax.ppermute(mine, everyone, partner), ready)]
  transfers between devices with their start and end apart: 4 -> 4, of which waited for: 4 -> 3; matrix products, arithmetic and copies ran while one was open for 1% -> 6% of each run, Pallas kernels for 0% -> 0%
where the time goes in v6:
time: 37.2 us; the launch traced here: 36.9 us
  other arithmetic  15.7 us (42%)
  waiting for transfers between devices  8.84 us (24%)
  starting transfers between devices  8.11 us (22%)
  local copies, waits for them, and re-layouts  1.68 us (5%)
  Pallas kernels  1.61 us (4%)
  between operations  1 us (3%)
    all_to_all x1, waiting for transfers between devices, shards(): got = lax.all_to_all(payload, everyone, 0, 0, tiled=True)  7.31 us
    all_to_all x1, starting transfers between devices, shards(): got = lax.all_to_all(payload, everyone, 0, 0, tiled=True)  7.3 us
    reduce_sum x5, other arithmetic, partial_image(): backward = jnp.sum(matrix[None, :, :] * row_part[:, :, None], 1)  5.99 us
    select_n x2, other arithmetic, screened(): return jnp.where(self_pair, row_geometry[5][:, None], off)  3.81 us
    mul x1, other arithmetic, pulling_matrices(): return [slope * separation for separation in separations]  1.85 us
    pallas_call x1, Pallas kernels, prep(): pl.pallas_call(prep_kernel, in_specs=[pl.BlockSpec(memory_space=smem), pl...  1.61 us
    reduce_sum x1, other arithmetic, shards(): field = jnp.stack([jnp.sum(part * charges[None, :], 1) for part in pull])  1.3 us
    ppermute x1, waiting for transfers between devices, curvature(): return (mine + lax.ppermute(mine, everyone, partner), ready)  0.82 us
  transfers between devices with their start and end apart: 4, of which 3 were waited for; matrix products, arithmetic and copies ran while one was open for 6% of the time, Pallas kernels for 0%

profile of v6, /device:TPU:0, one launch (start us, length us, event | category | flops | bytes accessed | tf_op | source)
XLA Modules:
  0.0 36.9 jit_solution(2643887565772116076)
XLA Ops:
  0.6 1.6 %shard_map.77 = f32[32,1,512]{2,1,0:T(1,128)} custom-call(f32[4]{0:T(128)} %hard_ref.1, f32[4]{0:T(128)} %width_ref.1, f32[3,1,64]{2,1,0:T(1,128)} %bitcast.73, s32[1,64]{1,0:T(1,128)} %bitcast.74, f32[64,128]{1,0:T(8,128)} %bitcast.45, f32[4,128]{1,0:T(4,128)} %readout_ref.1), custom_call_target="tpu_custom_call" | custom-call | tf_op jit(solution)/shard_map/pallas_call | solution.py:90
  2.2 7.3 %all-to-all-start = ((f32[32,1,512]{2,1,0:T(1,128)}), f32[32,1,512]{2,1,0:T(1,128)S(1)}, u32[]{:S(2)}, u32[]{:S(2)}) async-start(f32[32,1,512]{2,1,0:T(1,128)} %shard_map.77), calls=%async_computation | async-start | bytes 131072 | tf_op jit(solution)/shard_map/all_to_all | solution.py:148
  9.6 7.3 %all-to-all-done = f32[32,1,512]{2,1,0:T(1,128)S(1)} async-done(((f32[32,1,512]{2,1,0:T(1,128)}), f32[32,1,512]{2,1,0:T(1,128)S(1)}, u32[]{:S(2)}, u32[]{:S(2)}) %all-to-all-start) | async-done | bytes 65568 | tf_op jit(solution)/shard_map/all_to_all | solution.py:148
  17.2 0.2 slice_reduce_fusion.3
  17.8 2.3 %compare_select_fusion.6 = (f32[512,512]{1,0:T(8,128)S(1)}, f32[512,512]{1,0:T(8,128)S(1)}, f32[512,512]{1,0:T(8,128)S(1)}) fusion(f32[512]{0:T(512)S(1)} %bitcast.72, f32[512]{0:T(512)S(1)} %bitcast.67, f32[512]{0:T(512)S(1)} %bitcast.68, f32[512]{0:T(512)S(1)} %bitcast.69, f32[512]{0:T(512)S(1)} %bitcast.70, s32[512]{0:T(512)S(1)} %iota_add_fusion.3, ...), kind=kLoop, calls=%fused_computation.30 | loop fusion | flops 12582912 | bytes 3170304 | tf_op jit(solution)/shard_map/jit(_where)/select_n | solution.py:30
  20.1 1.5 %compare_select_fusion = (f32[512,512]{1,0:T(8,128)S(1)}, f32[512,512]{1,0:T(8,128)S(1)}) fusion(f32[512]{0:T(512)S(1)} %bitcast.53, f32[512]{0:T(512)S(1)} %bitcast.54, f32[512]{0:T(512)S(1)} %bitcast.55, f32[512]{0:T(512)S(1)} %bitcast.56, f32[512]{0:T(512)S(1)} %bitcast.49, f32[512]{0:T(512)S(1)} %bitcast.60, f32[512]{0:T(512)S(1)} %bitcast.50, ...), kind=kLoop, calls=%fused_computation.24 | loop fusion | flops 8388608 | bytes 2129920 | tf_op jit(solution)/shard_map/jit(_where)/select_n | solution.py:30
  21.7 1.5 %multiply_reduce_fusion.16 = (f32[2,512]{1,0:T(2,128)S(1)}, f32[2,512]{1,0:T(2,128)S(1)}, f32[2,512]{1,0:T(2,128)S(1)}, f32[2,512]{1,0:T(2,128)S(1)}, f32[2,512]...) fusion(f32[2,512]{1,0:T(2,128)S(1)} %get-tuple-element.95, ...), kind=kLoop, calls=%fused_computation.16 | loop fusion | flops 8380416 | bytes 5296128 | tf_op jit(solution)/shard_map/reduce_sum | solution.py:208
  23.4 0.2 collective-permute-start
  23.9 0.7 %collective-permute-done = f32[2,2048]{1,0:T(2,128)S(1)} collective-permute-done((f32[2,2048]{1,0:T(2,128)S(1)}, f32[2,2048]{1,0:T(2,128)S(1)}, u32[]{:S(2)}, u32[]{:S(2)}) %collective-permute-start) | collective-permute-done | bytes 16416 | tf_op jit(solution)/shard_map/ppermute | solution.py:216
  24.8 0.2 multiply_reduce_fusion.31
  25.1 2.3 %multiply_reduce_fusion.12 = (f32[2,512]{1,0:T(2,128)S(1)}, f32[2,512]{1,0:T(2,128)S(1)}, f32[2,512]{1,0:T(2,128)S(1)}, f32[2,512]{1,0:T(2,128)S(1)}) fusion(f32[2,512]{1,0:T(2,128)S(1)} %get-tuple-element.89, f32[512,512]{1,0:T(8,128)} %copy-done, f32[2,512]{1,0:T(2,128)S(1)} %get-tuple-element.88, f32[512,512]{1,0:T(8,128)} %copy-done.2, ...), kind=kLoop, calls=%fused_computation.12 | loop fusion | flops 4190208 | bytes 3170304 | tf_op jit(solution)/shard_map/reduce_sum | solution.py:208
  27.5 0.7 %multiply_reduce_fusion.8 = (f32[2,512]{1,0:T(2,128)S(1)}, f32[2,512]{1,0:T(2,128)S(1)}, f32[2,512]{1,0:T(2,128)S(1)}, f32[2,512]{1,0:T(2,128)S(1)}) fusion(f32[2,512]{1,0:T(2,128)S(1)} %get-tuple-element.85, f32[512,512]{1,0:T(8,128)S(1)} %get-tuple-element.93, f32[2,512]{1,0:T(2,128)S(1)} %get-tuple-element.87, f32[2,512]{1,0:T(2,128)S(1)} %get-tuple-element.86, ...), kind=kLoop, calls=%fused_computation.8 | loop fusion | flops 4190208 | bytes 2125824 | tf_op jit(solution)/shard_map/reduce_sum | solution.py:208
  28.3 0.2 collective-permute-start.1
  28.5 1.8 %subtract_multiply_fusion = (f32[64,2048]{1,0:T(8,128)}, f32[64,2048]{1,0:T(8,128)}, f32[64,2048]{1,0:T(8,128)}) fusion(f32[2048]{0:T(1024)S(1)} %sub.383, f32[64]{0:T(128)S(1)} %get-tuple-element.101, f32[2048]{0:T(1024)S(1)} %sub.378, f32[64]{0:T(128)S(1)} %get-tuple-element.102, f32[2048]{0:T(1024)S(1)} %sub.373, f32[64]{0:T(128)S(1)} %get-tuple-element.103, ...), kind=kLoop, calls=%fused_computation.41 | loop fusion | flops 3538944 | bytes 1606912 | tf_op jit(solution)/shard_map/mul | solution.py:131
  30.4 0.2 multiply_reduce_fusion.30
  30.6 0.2 multiply_reduce_fusion.29
  31.0 0.7 %multiply_reduce_fusion.4 = (f32[2,512]{1,0:T(2,128)S(1)}, f32[2,512]{1,0:T(2,128)S(1)}, f32[2,512]{1,0:T(2,128)S(1)}, f32[2,512]{1,0:T(2,128)S(1)}) fusion(f32[2,512]{1,0:T(2,128)S(1)} %get-tuple-element.84, f32[512,512]{1,0:T(8,128)S(1)} %copy-done.1, f32[2,512]{1,0:T(2,128)S(1)} %get-tuple-element.83, f32[512,512]{1,0:T(8,128)S(1)} %copy-done.3, ...), kind=kLoop, calls=%fused_computation.4 | loop fusion | flops 4190208 | bytes 3170304 | tf_op jit(solution)/shard_map/reduce_sum | solution.py:208
  31.8 0.7 %multiply_reduce_fusion = (f32[2,512]{1,0:T(2,128)S(1)}, f32[2,512]{1,0:T(2,128)S(1)}, f32[2,512]{1,0:T(2,128)S(1)}, f32[2,512]{1,0:T(2,128)S(1)}) fusion(f32[2,512]{1,0:T(2,128)S(1)} %get-tuple-element.80, f32[512,512]{1,0:T(8,128)S(1)} %get-tuple-element.93, f32[2,512]{1,0:T(2,128)S(1)} %get-tuple-element.82, f32[2,512]{1,0:T(2,128)S(1)} %get-tuple-element.81, ...), kind=kLoop, calls=%fused_computation | loop fusion | flops 4190208 | bytes 2125824 | tf_op jit(solution)/shard_map/reduce_sum | solution.py:208
  32.7 0.4 %collective-permute-start.2 = (f32[2]{0:T(128)S(1)}, f32[2]{0:T(128)S(1)}, u32[]{:S(2)}, u32[]{:S(2)}) collective-permute-start(f32[2]{0:T(128)S(1)} %multiply_reduce_fusion.28), channel_id=1, source_target_pairs={{0,1},{1,0},{2,3},{3,2},{4,5},{5,4},{6,7},{7,6},{8,9},{9,8},{10,11... | collective-permute-start | bytes 32 | tf_op jit(solution)/shard_map/ppermute | solution.py:220
  33.1 0.8 %collective-permute-done.2 = f32[2]{0:T(128)S(1)} collective-permute-done((f32[2]{0:T(128)S(1)}, f32[2]{0:T(128)S(1)}, u32[]{:S(2)}, u32[]{:S(2)}) %collective-permute-start.2) | collective-permute-done | bytes 40 | tf_op jit(solution)/shard_map/ppermute | solution.py:220
  34.0 0.2 fusion.30
  34.4 0.6 %dynamic-slice_bitcast_fusion = f32[1,1,64]{2,1,0:T(1,128)} fusion(f32[2048]{0:T(1024)S(1)} %multiply_reduce_fusion.27, s32[]{:T(128)S(6)} %select_n.213), kind=kLoop, calls=%fused_computation.174 | loop fusion | bytes 516 | tf_op jit(solution)/shard_map/reshape | solution.py:254
  35.1 1.3 %multiply_reduce_fusion.26 = (f32[64]{0:T(128)S(1)}, f32[64]{0:T(128)S(1)}, f32[64]{0:T(128)S(1)}) fusion(f32[64,2048]{1,0:T(8,128)} %get-tuple-element.7, f32[2048]{0:T(1024)S(1)} %multiply_reduce_fusion.27, f32[64,2048]{1,0:T(8,128)S(1)} %copy-done.5, f32[64,2048]{1,0:T(8,128)S(1)} %copy-done.4), kind=kLoop, calls=%fused_computation.57 | loop fusion | flops 786240 | bytes 1581824 | tf_op jit(solution)/shard_map/reduce_sum | solution.py:252
  36.4 0.6 %maximum_multiply_fusion = f32[3,1,1,64]{3,2,1,0:T(1,128)} fusion(f32[1,1,1,64]{3,2,1,0:T(1,128)S(1)} %bitcast.48, f32[1,1,1,64]{3,2,1,0:T(1,128)S(1)} %bitcast.47, f32[1,1,1,64]{3,2,1,0:T(1,128)S(1)} %bitcast.46, f32[64]{0:T(128)S(1)} %dynamic_slice.179), kind=kLoop, calls=%fused_computation.163 | loop fusion | flops 576 | bytes 1792 | tf_op jit(solution)/shard_map/mul | solution.py:253
  (73 shorter events, 2.2 us)
Async XLA Ops:
  2.2 14.7 %all-to-all-start = ((f32[32,1,512]{2,1,0:T(1,128)}), f32[32,1,512]{2,1,0:T(1,128)S(1)}, u32[]{:S(2)}, u32[]{:S(2)}) async-start(f32[32,1,512]{2,1,0:T(1,128)} %shard_map.77), calls=%async_computation | async-start | bytes 131072 | tf_op jit(solution)/shard_map/all_to_all | solution.py:148
  20.1 1.6 %copy-start = (f32[512,512]{1,0:T(8,128)}, f32[512,512]{1,0:T(8,128)S(1)}, u32[]{:S(2)}) copy-start(f32[512,512]{1,0:T(8,128)S(1)} %get-tuple-element.91) | copy-start | bytes 3145732
  20.1 1.6 %copy-start.2 = (f32[512,512]{1,0:T(8,128)}, f32[512,512]{1,0:T(8,128)S(1)}, u32[]{:S(2)}) copy-start(f32[512,512]{1,0:T(8,128)S(1)} %get-tuple-element.92) | copy-start | bytes 3145732
  23.4 1.2 %collective-permute-start = (f32[2,2048]{1,0:T(2,128)S(1)}, f32[2,2048]{1,0:T(2,128)S(1)}, u32[]{:S(2)}, u32[]{:S(2)}) collective-permute-start(f32[2,2048]{1,0:T(2,128)S(1)} %constant_dynamic-update-slice_fusion.16), channel_id=1, source_target_pairs={{0,1},{1,0},{2,3},{3,2},{4,5},{5,4},{6,7},{7,6},{8,9},{9,8},{10,11... | collective-permute-start | bytes 49160 | tf_op jit(solution)/shard_map/ppermute | solution.py:216
  27.5 3.4 %copy-start.3 = (f32[512,512]{1,0:T(8,128)S(1)}, f32[512,512]{1,0:T(8,128)}, u32[]{:S(2)}) copy-start(f32[512,512]{1,0:T(8,128)} %copy-done.2) | copy-start | bytes 3145732
  28.2 2.7 %copy-start.1 = (f32[512,512]{1,0:T(8,128)S(1)}, f32[512,512]{1,0:T(8,128)}, u32[]{:S(2)}) copy-start(f32[512,512]{1,0:T(8,128)} %copy-done) | copy-start | bytes 3145732
  28.3 2.1 %collective-permute-start.1 = (f32[2,2048]{1,0:T(2,128)S(1)}, f32[2,2048]{1,0:T(2,128)S(1)}, u32[]{:S(2)}, u32[]{:S(2)}) collective-permute-start(f32[2,2048]{1,0:T(2,128)S(1)} %constant_dynamic-update-slice_fusion.8), channel_id=1, source_target_pairs={{0,1},{1,0},{2,3},{3,2},{4,5},{5,4},{6,7},{7,6},{8,9},{9,8},{10,11... | collective-permute-start | bytes 49160 | tf_op jit(solution)/shard_map/ppermute | solution.py:216
  31.8 3.3 %copy-start.4 = (f32[64,2048]{1,0:T(8,128)S(1)}, f32[64,2048]{1,0:T(8,128)}, u32[]{:S(2)}) copy-start(f32[64,2048]{1,0:T(8,128)} %get-tuple-element.9) | copy-start | bytes 1572868
  31.8 3.3 %copy-start.5 = (f32[64,2048]{1,0:T(8,128)S(1)}, f32[64,2048]{1,0:T(8,128)}, u32[]{:S(2)}) copy-start(f32[64,2048]{1,0:T(8,128)} %get-tuple-element.8) | copy-start | bytes 1572868
  32.7 1.2 %collective-permute-start.2 = (f32[2]{0:T(128)S(1)}, f32[2]{0:T(128)S(1)}, u32[]{:S(2)}, u32[]{:S(2)}) collective-permute-start(f32[2]{0:T(128)S(1)} %multiply_reduce_fusion.28), channel_id=1, source_target_pairs={{0,1},{1,0},{2,3},{3,2},{4,5},{5,4},{6,7},{7,6},{8,9},{9,8},{10,11... | collective-permute-start | bytes 32 | tf_op jit(solution)/shard_map/ppermute | solution.py:220

commit v7 on v6

--- a/solution.py
+++ b/solution.py
@@ -109,7 +109,7 @@
     )
 
 
-def pulling_matrices(row_geometry, col_geometry, self_pair):
+def pulling_fields(row_geometry, col_geometry, self_pair, vectors):
     separations = []
     squared = jnp.zeros(self_pair.shape, row_geometry.dtype)
     for axis_id in range(3):
@@ -128,7 +128,9 @@
         * inverse
     )
     slope = jnp.where(self_pair, 0.0, slope)
-    return [slope * separation for separation in separations]
+    return jnp.stack(
+        [jnp.stack([jnp.sum(slope * vector[None, :] * separation, 1) for separation in separations]) for vector in vectors]
+    )
 
 
 def make_shards(rows, cols):
@@ -241,15 +243,22 @@
             norm_next = jnp.sum(resid * resid, 1)
             direction = resid + (norm_next / norm_now)[:, None] * direction
             norm_now = norm_next
-        pull = pulling_matrices(own, geometry, own_index[:, None] == col_index[None, :])
-        last_curvature, pull = curvature(direction, pull)
+        fields = pulling_fields(
+            own, geometry, own_index[:, None] == col_index[None, :],
+            [solution[0], solution[1], direction[0], direction[1]],
+        ).reshape(2, 2, 3, per_brick)
+        own_solution = lax.dynamic_slice_in_dim(solution, me * per_brick, per_brick, 1)
+        own_direction = lax.dynamic_slice_in_dim(direction, me * per_brick, per_brick, 1)
+        solution_sums = jnp.sum(solution, 1)
+        direction_sums = jnp.sum(direction, 1)
+        last_curvature, fields = curvature(direction, fields)
         step_size = norm_now / last_curvature
-        solution = solution + step_size[:, None] * direction
-        totals = jnp.sum(solution, 1)
+        totals = solution_sums + step_size * direction_sums
         weights = jnp.where(jnp.arange(2) == 0, 1.0, -(totals[::-1] / totals))
-        charges = jnp.sum(weights[:, None] * solution, 0)
-        own_charges = lax.dynamic_slice_in_dim(charges, me * per_brick, per_brick, 0)
-        field = jnp.stack([jnp.sum(part * charges[None, :], 1) for part in pull])
+        own_charges = jnp.sum(weights[:, None] * (own_solution + step_size[:, None] * own_direction), 0)
+        field = jnp.sum(
+            weights[:, None, None] * (fields[0] + step_size[:, None, None] * fields[1]), 0
+        )
         forces = (own_charges[None, :] * field).reshape(3, 1, 1, per_brick)
         return (own_charges.reshape(1, 1, per_brick), forces)
 

time: 37.2 us -> 35.7 us (0.960)
  other arithmetic: 15.7 us -> 13.9 us
  waiting for transfers between devices: 8.84 us -> 10 us
  local copies, waits for them, and re-layouts: 1.68 us -> 1.03 us
    mul x1 -> x0, other arithmetic: 1.85 us -> none  [pulling_matrices(): return [slope * separation for separation in separations]]
    ppermute x2, waiting for transfers between devices: 0.71 us -> 1.73 us  [operate(): return partial + lax.ppermute(partial, everyone, partner)]
    reshape x1 -> x0, local copies, waits for them, and re-layouts: 0.59 us -> none  [shards(): return (own_charges.reshape(1, 1, per_brick), forces)]
    reduce_sum x4 -> x5, other arithmetic: 1.73 us -> 1.89 us  [the longest x1 1.35 us: pulling_fields(): jnp.sum(slope * vector[None, :] * separation, 1)]
  transfers between devices with their start and end apart: 4 -> 4, of which waited for: 3 -> 4; matrix products, arithmetic and copies ran while one was open for 6% -> 1% of each run, Pallas kernels for 0% -> 0%
where the time goes in v7:
time: 35.7 us; the launch traced here: 35.5 us
  other arithmetic  13.9 us (39%)
  waiting for transfers between devices  10 us (28%)
  starting transfers between devices  7.94 us (22%)
  Pallas kernels  1.61 us (5%)
  local copies, waits for them, and re-layouts  1.03 us (3%)
  between operations  0.98 us (3%)
    all_to_all x1, waiting for transfers between devices, shards(): got = lax.all_to_all(payload, everyone, 0, 0, tiled=True)  7.33 us
    all_to_all x1, starting transfers between devices, shards(): got = lax.all_to_all(payload, everyone, 0, 0, tiled=True)  7.3 us
    reduce_sum x5, other arithmetic, partial_image(): backward = jnp.sum(matrix[None, :, :] * row_part[:, :, None], 1)  6 us
    select_n x2, other arithmetic, screened(): return jnp.where(self_pair, row_geometry[5][:, None], off)  3.75 us
    ppermute x2, waiting for transfers between devices, operate(): return partial + lax.ppermute(partial, everyone, partner)  1.73 us
    pallas_call x1, Pallas kernels, prep(): pl.pallas_call(prep_kernel, in_specs=[pl.BlockSpec(memory_space=smem), pl...  1.61 us
    reduce_sum x1, other arithmetic, pulling_fields(): jnp.sum(slope * vector[None, :] * separation, 1)  1.35 us
    ppermute x1, waiting for transfers between devices, curvature(): return (mine + lax.ppermute(mine, everyone, partner), ready)  0.96 us
  transfers between devices with their start and end apart: 4, of which 4 were waited for; matrix products, arithmetic and copies ran while one was open for 1% of the time, Pallas kernels for 0%

profile of v7, /device:TPU:0, one launch (start us, length us, event | category | flops | bytes accessed | tf_op | source)
XLA Modules:
  0.0 35.5 jit_solution(10221282693438230377)
XLA Ops:
  0.6 1.6 %shard_map.77 = f32[32,1,512]{2,1,0:T(1,128)} custom-call(f32[4]{0:T(128)} %hard_ref.1, f32[4]{0:T(128)} %width_ref.1, f32[3,1,64]{2,1,0:T(1,128)} %bitcast.107, s32[1,64]{1,0:T(1,128)} %bitcast.108, f32[64,128]{1,0:T(8,128)} %bitcast.76, f32[4,128]{1,0:T(4,128)} %readout_ref.1), custom_call_target="tpu_custom_call" | custom-call | tf_op jit(solution)/shard_map/pallas_call | solution.py:90
  2.2 7.3 %all-to-all-start = ((f32[32,1,512]{2,1,0:T(1,128)}), f32[32,1,512]{2,1,0:T(1,128)S(1)}, u32[]{:S(2)}, u32[]{:S(2)}) async-start(f32[32,1,512]{2,1,0:T(1,128)} %shard_map.77), calls=%async_computation | async-start | bytes 131072 | tf_op jit(solution)/shard_map/all_to_all | solution.py:150
  9.6 7.3 %all-to-all-done = f32[32,1,512]{2,1,0:T(1,128)S(1)} async-done(((f32[32,1,512]{2,1,0:T(1,128)}), f32[32,1,512]{2,1,0:T(1,128)S(1)}, u32[]{:S(2)}, u32[]{:S(2)}) %all-to-all-start) | async-done | bytes 65568 | tf_op jit(solution)/shard_map/all_to_all | solution.py:150
  17.2 0.2 slice_reduce_fusion.3
  17.8 2.2 %compare_select_fusion.6 = (f32[512,512]{1,0:T(8,128)S(1)}, f32[512,512]{1,0:T(8,128)S(1)}, f32[512,512]{1,0:T(8,128)S(1)}) fusion(f32[512]{0:T(512)S(1)} %bitcast.105, f32[512]{0:T(512)S(1)} %bitcast.100, f32[512]{0:T(512)S(1)} %bitcast.101, f32[512]{0:T(512)S(1)} %bitcast.102, f32[512]{0:T(512)S(1)} %bitcast.103, s32[512]{0:T(512)S(1)} %iota_add_fusion.3, ...), kind=kLoop, calls=%fused_computation.45 | loop fusion | flops 12582912 | bytes 3170304 | tf_op jit(solution)/shard_map/jit(_where)/select_n | solution.py:30
  20.1 1.5 %compare_select_fusion = (f32[512,512]{1,0:T(8,128)S(1)}, f32[512,512]{1,0:T(8,128)S(1)}) fusion(f32[512]{0:T(512)S(1)} %bitcast.86, f32[512]{0:T(512)S(1)} %bitcast.87, f32[512]{0:T(512)S(1)} %bitcast.88, f32[512]{0:T(512)S(1)} %bitcast.89, f32[512]{0:T(512)S(1)} %bitcast.82, f32[512]{0:T(512)S(1)} %bitcast.93, f32[512]{0:T(512)S(1)} %bitcast.83, ...), kind=kLoop, calls=%fused_computation.39 | loop fusion | flops 8388608 | bytes 2129920 | tf_op jit(solution)/shard_map/jit(_where)/select_n | solution.py:30
  21.6 1.5 %multiply_reduce_fusion.16 = (f32[2,512]{1,0:T(2,128)S(1)}, f32[2,512]{1,0:T(2,128)S(1)}, f32[2,512]{1,0:T(2,128)S(1)}, f32[2,512]{1,0:T(2,128)S(1)}, f32[2,512]...) fusion(f32[2,512]{1,0:T(2,128)S(1)} %get-tuple-element.115, ...), kind=kLoop, calls=%fused_computation.16 | loop fusion | flops 8380416 | bytes 5296128 | tf_op jit(solution)/shard_map/reduce_sum | solution.py:210
  23.3 0.2 collective-permute-start
  23.6 1.0 %collective-permute-done = f32[2,2048]{1,0:T(2,128)S(1)} collective-permute-done((f32[2,2048]{1,0:T(2,128)S(1)}, f32[2,2048]{1,0:T(2,128)S(1)}, u32[]{:S(2)}, u32[]{:S(2)}) %collective-permute-start) | collective-permute-done | bytes 16416 | tf_op jit(solution)/shard_map/ppermute | solution.py:218
  24.6 0.2 fusion.22
  24.8 0.2 multiply_reduce_fusion.27
  25.1 0.7 %multiply_reduce_fusion.12 = (f32[2,512]{1,0:T(2,128)S(1)}, f32[2,512]{1,0:T(2,128)S(1)}, f32[2,512]{1,0:T(2,128)S(1)}, f32[2,512]{1,0:T(2,128)S(1)}) fusion(f32[2,512]{1,0:T(2,128)S(1)} %get-tuple-element.109, f32[512,512]{1,0:T(8,128)S(1)} %get-tuple-element.111, f32[2,512]{1,0:T(2,128)S(1)} %get-tuple-element.108, f32[512,512]{1,0:T(8,128)S(1)} %get-tuple-element.112, ...), kind=kLoop, calls=%fused_computation.12 | loop fusion | flops 4190208 | bytes 3170304 | tf_op jit(solution)/shard_map/reduce_sum | solution.py:210
  25.9 0.7 %multiply_reduce_fusion.8 = (f32[2,512]{1,0:T(2,128)S(1)}, f32[2,512]{1,0:T(2,128)S(1)}, f32[2,512]{1,0:T(2,128)S(1)}, f32[2,512]{1,0:T(2,128)S(1)}) fusion(f32[2,512]{1,0:T(2,128)S(1)} %get-tuple-element.105, f32[512,512]{1,0:T(8,128)S(1)} %get-tuple-element.113, f32[2,512]{1,0:T(2,128)S(1)} %get-tuple-element.107, f32[2,512]{1,0:T(2,128)S(1)} %get-tuple-element.106, ...), kind=kLoop, calls=%fused_computation.8 | loop fusion | flops 4190208 | bytes 2125824 | tf_op jit(solution)/shard_map/reduce_sum | solution.py:210
  26.7 0.2 collective-permute-start.1
  27.2 0.7 %collective-permute-done.1 = f32[2,2048]{1,0:T(2,128)S(1)} collective-permute-done((f32[2,2048]{1,0:T(2,128)S(1)}, f32[2,2048]{1,0:T(2,128)S(1)}, u32[]{:S(2)}, u32[]{:S(2)}) %collective-permute-start.1) | collective-permute-done | bytes 16416 | tf_op jit(solution)/shard_map/ppermute | solution.py:218
  28.0 0.2 multiply_reduce_fusion.26
  28.2 0.2 multiply_reduce_fusion.25
  28.4 0.2 fusion.49
  28.7 2.3 %multiply_reduce_fusion.4 = (f32[2,512]{1,0:T(2,128)S(1)}, f32[2,512]{1,0:T(2,128)S(1)}, f32[2,512]{1,0:T(2,128)S(1)}, f32[2,512]{1,0:T(2,128)S(1)}) fusion(f32[2,512]{1,0:T(2,128)S(1)} %get-tuple-element.103, f32[512,512]{1,0:T(8,128)} %copy-done, f32[2,512]{1,0:T(2,128)S(1)} %get-tuple-element.102, f32[512,512]{1,0:T(8,128)} %copy-done.1, ...), kind=kLoop, calls=%fused_computation.4 | loop fusion | flops 4190208 | bytes 3170304 | tf_op jit(solution)/shard_map/reduce_sum | solution.py:210
  31.0 0.7 %multiply_reduce_fusion = (f32[2,512]{1,0:T(2,128)S(1)}, f32[2,512]{1,0:T(2,128)S(1)}, f32[2,512]{1,0:T(2,128)S(1)}, f32[2,512]{1,0:T(2,128)S(1)}) fusion(f32[2,512]{1,0:T(2,128)S(1)} %get-tuple-element.99, f32[512,512]{1,0:T(8,128)S(1)} %get-tuple-element.113, f32[2,512]{1,0:T(2,128)S(1)} %get-tuple-element.101, f32[2,512]{1,0:T(2,128)S(1)} %get-tuple-element.100, ...), kind=kLoop, calls=%fused_computation | loop fusion | flops 4190208 | bytes 2125824 | tf_op jit(solution)/shard_map/reduce_sum | solution.py:210
  32.0 1.3 %fusion.8 = (f32[64]{0:T(128)S(1)}, f32[64]{0:T(128)S(1)}, f32[64]{0:T(128)S(1)}, f32[64]{0:T(128)S(1)}, f32[64]{0:T(128)S(1)}, /*index=5*/f32[64]{0:T(128)S(1)}...) fusion(f32[2048]{0:T(1024)S(1)} %bitcast.81, ...), kind=kLoop, calls=%fused_computation.64 | loop fusion | flops 6814976 | bytes 69888 | tf_op jit(solution)/shard_map/reduce_sum | solution.py:132
  33.4 0.2 collective-permute-start.2
  33.6 1.0 %collective-permute-done.2 = f32[2]{0:T(128)S(1)} collective-permute-done((f32[2]{0:T(128)S(1)}, f32[2]{0:T(128)S(1)}, u32[]{:S(2)}, u32[]{:S(2)}) %collective-permute-start.2) | collective-permute-done | bytes 40 | tf_op jit(solution)/shard_map/ppermute | solution.py:222
  34.9 0.6 %reshape_multiply_fusion = f32[3,1,1,64]{3,2,1,0:T(1,128)} fusion(f32[3,64]{1,0:T(4,128)S(1)} %fusion.43, f32[64]{0:T(128)S(1)} %fusion.46), kind=kLoop, calls=%fused_computation.190 | loop fusion | flops 192 | bytes 1792 | tf_op jit(solution)/shard_map/mul | solution.py:262
  (71 shorter events, 2.0 us)
Async XLA Ops:
  2.2 14.7 %all-to-all-start = ((f32[32,1,512]{2,1,0:T(1,128)}), f32[32,1,512]{2,1,0:T(1,128)S(1)}, u32[]{:S(2)}, u32[]{:S(2)}) async-start(f32[32,1,512]{2,1,0:T(1,128)} %shard_map.77), calls=%async_computation | async-start | bytes 131072 | tf_op jit(solution)/shard_map/all_to_all | solution.py:150
  20.0 5.0 %copy-start = (f32[512,512]{1,0:T(8,128)}, f32[512,512]{1,0:T(8,128)S(1)}, u32[]{:S(2)}) copy-start(f32[512,512]{1,0:T(8,128)S(1)} %get-tuple-element.111) | copy-start | bytes 3145732
  20.1 5.0 %copy-start.1 = (f32[512,512]{1,0:T(8,128)}, f32[512,512]{1,0:T(8,128)S(1)}, u32[]{:S(2)}) copy-start(f32[512,512]{1,0:T(8,128)S(1)} %get-tuple-element.112) | copy-start | bytes 3145732
  23.3 1.2 %collective-permute-start = (f32[2,2048]{1,0:T(2,128)S(1)}, f32[2,2048]{1,0:T(2,128)S(1)}, u32[]{:S(2)}, u32[]{:S(2)}) collective-permute-start(f32[2,2048]{1,0:T(2,128)S(1)} %constant_dynamic-update-slice_fusion.16), channel_id=1, source_target_pairs={{0,1},{1,0},{2,3},{3,2},{4,5},{5,4},{6,7},{7,6},{8,9},{9,8},{10,11... | collective-permute-start | bytes 49160 | tf_op jit(solution)/shard_map/ppermute | solution.py:218
  26.7 1.2 %collective-permute-start.1 = (f32[2,2048]{1,0:T(2,128)S(1)}, f32[2,2048]{1,0:T(2,128)S(1)}, u32[]{:S(2)}, u32[]{:S(2)}) collective-permute-start(f32[2,2048]{1,0:T(2,128)S(1)} %constant_dynamic-update-slice_fusion.8), channel_id=1, source_target_pairs={{0,1},{1,0},{2,3},{3,2},{4,5},{5,4},{6,7},{7,6},{8,9},{9,8},{10,11... | collective-permute-start | bytes 49160 | tf_op jit(solution)/shard_map/ppermute | solution.py:218
  33.4 1.2 %collective-permute-start.2 = (f32[2]{0:T(128)S(1)}, f32[2]{0:T(128)S(1)}, u32[]{:S(2)}, u32[]{:S(2)}) collective-permute-start(f32[2]{0:T(128)S(1)} %get-tuple-element.4), channel_id=1, source_target_pairs={{0,1},{1,0},{2,3},{3,2},{4,5},{5,4},{6,7},{7,6},{8,9},{9,8},{10,11... | collective-permute-start | bytes 32 | tf_op jit(solution)/shard_map/ppermute | solution.py:222
  34.8 0.7 %copy-start.2 = (f32[64]{0:T(128)}, f32[64]{0:T(128)S(1)}, u32[]{:S(2)}) copy-start(f32[64]{0:T(128)S(1)} %fusion.46) | copy-start | bytes 772

commit v8 on v7

--- a/solution.py
+++ b/solution.py
@@ -217,17 +217,17 @@
                 partial = partial_image(vectors)
                 return partial + lax.ppermute(partial, everyone, partner)
 
-            def curvature(vectors, ready):
-                mine, ready = lax.optimization_barrier((jnp.sum(vectors * partial_image(vectors), 1), ready))
-                return mine + lax.ppermute(mine, everyone, partner), ready
+            def curvature(vectors):
+                mine = jnp.sum(vectors * partial_image(vectors), 1)
+                return mine + lax.ppermute(mine, everyone, partner)
         else:
             matrix = screened(row_geometry, geometry, row_index[:, None] == col_index[None, :])
 
             def operate(vectors):
                 return assemble(jnp.sum(matrix[None, :, :] * vectors[:, None, :], 2))
 
-            def curvature(vectors, ready):
-                return jnp.sum(vectors * operate(vectors), 1), ready
+            def curvature(vectors):
+                return jnp.sum(vectors * operate(vectors), 1)
 
         rhs = jnp.stack([-geometry[4], jnp.ones((atoms,), jnp.float32)])
         solution = jnp.zeros_like(rhs)
@@ -251,7 +251,7 @@
         own_direction = lax.dynamic_slice_in_dim(direction, me * per_brick, per_brick, 1)
         solution_sums = jnp.sum(solution, 1)
         direction_sums = jnp.sum(direction, 1)
-        last_curvature, fields = curvature(direction, fields)
+        last_curvature = curvature(direction)
         step_size = norm_now / last_curvature
         totals = solution_sums + step_size * direction_sums
         weights = jnp.where(jnp.arange(2) == 0, 1.0, -(totals[::-1] / totals))

time: 35.7 us -> 34.8 us (0.975)
  waiting for transfers between devices: 10 us -> 9.06 us
    ppermute x1, waiting for transfers between devices: 0.96 us -> 0.01 us  [curvature(): return mine + lax.ppermute(mine, everyone, partner)]
  transfers between devices with their start and end apart: 4 -> 4, of which waited for: 4 -> 3; matrix products, arithmetic and copies ran while one was open for 1% -> 5% of each run, Pallas kernels for 0% -> 0%
where the time goes in v8:
time: 34.8 us; the launch traced here: 34.5 us
  other arithmetic  13.9 us (40%)
  waiting for transfers between devices  9.06 us (26%)
  starting transfers between devices  7.94 us (23%)
  Pallas kernels  1.61 us (5%)
  local copies, waits for them, and re-layouts  1.02 us (3%)
  between operations  0.98 us (3%)
    all_to_all x1, waiting for transfers between devices, shards(): got = lax.all_to_all(payload, everyone, 0, 0, tiled=True)  7.33 us
    all_to_all x1, starting transfers between devices, shards(): got = lax.all_to_all(payload, everyone, 0, 0, tiled=True)  7.3 us
    reduce_sum x5, other arithmetic, partial_image(): backward = jnp.sum(matrix[None, :, :] * row_part[:, :, None], 1)  6 us
    select_n x2, other arithmetic, screened(): return jnp.where(self_pair, row_geometry[5][:, None], off)  3.75 us
    ppermute x2, waiting for transfers between devices, operate(): return partial + lax.ppermute(partial, everyone, partner)  1.73 us
    pallas_call x1, Pallas kernels, prep(): pl.pallas_call(prep_kernel, in_specs=[pl.BlockSpec(memory_space=smem), pl...  1.61 us
    reduce_sum x1, other arithmetic, pulling_fields(): jnp.sum(slope * vector[None, :] * separation, 1)  1.34 us
  transfers between devices with their start and end apart: 4, of which 3 were waited for; matrix products, arithmetic and copies ran while one was open for 5% of the time, Pallas kernels for 0%

profile of v8, /device:TPU:0, one launch (start us, length us, event | category | flops | bytes accessed | tf_op | source)
XLA Modules:
  0.0 34.5 jit_solution(6859584556719512394)
XLA Ops:
  0.6 1.6 %shard_map.77 = f32[32,1,512]{2,1,0:T(1,128)} custom-call(f32[4]{0:T(128)} %hard_ref.1, f32[4]{0:T(128)} %width_ref.1, f32[3,1,64]{2,1,0:T(1,128)} %bitcast.95, s32[1,64]{1,0:T(1,128)} %bitcast.96, f32[64,128]{1,0:T(8,128)} %bitcast.65, f32[4,128]{1,0:T(4,128)} %readout_ref.1), custom_call_target="tpu_custom_call" | custom-call | tf_op jit(solution)/shard_map/pallas_call | solution.py:90
  2.2 7.3 %all-to-all-start = ((f32[32,1,512]{2,1,0:T(1,128)}), f32[32,1,512]{2,1,0:T(1,128)S(1)}, u32[]{:S(2)}, u32[]{:S(2)}) async-start(f32[32,1,512]{2,1,0:T(1,128)} %shard_map.77), calls=%async_computation | async-start | bytes 131072 | tf_op jit(solution)/shard_map/all_to_all | solution.py:150
  9.6 7.3 %all-to-all-done = f32[32,1,512]{2,1,0:T(1,128)S(1)} async-done(((f32[32,1,512]{2,1,0:T(1,128)}), f32[32,1,512]{2,1,0:T(1,128)S(1)}, u32[]{:S(2)}, u32[]{:S(2)}) %all-to-all-start) | async-done | bytes 65568 | tf_op jit(solution)/shard_map/all_to_all | solution.py:150
  17.2 0.2 slice_reduce_fusion.3
  17.8 2.2 %compare_select_fusion.6 = (f32[512,512]{1,0:T(8,128)S(1)}, f32[512,512]{1,0:T(8,128)S(1)}, f32[512,512]{1,0:T(8,128)S(1)}) fusion(f32[512]{0:T(512)S(1)} %bitcast.93, f32[512]{0:T(512)S(1)} %bitcast.88, f32[512]{0:T(512)S(1)} %bitcast.89, f32[512]{0:T(512)S(1)} %bitcast.90, f32[512]{0:T(512)S(1)} %bitcast.91, s32[512]{0:T(512)S(1)} %iota_add_fusion.3, ...), kind=kLoop, calls=%fused_computation.45 | loop fusion | flops 12582912 | bytes 3170304 | tf_op jit(solution)/shard_map/jit(_where)/select_n | solution.py:30
  20.1 1.5 %compare_select_fusion = (f32[512,512]{1,0:T(8,128)S(1)}, f32[512,512]{1,0:T(8,128)S(1)}) fusion(f32[512]{0:T(512)S(1)} %bitcast.74, f32[512]{0:T(512)S(1)} %bitcast.75, f32[512]{0:T(512)S(1)} %bitcast.76, f32[512]{0:T(512)S(1)} %bitcast.77, f32[512]{0:T(512)S(1)} %bitcast.70, f32[512]{0:T(512)S(1)} %bitcast.81, f32[512]{0:T(512)S(1)} %bitcast.71, ...), kind=kLoop, calls=%fused_computation.39 | loop fusion | flops 8388608 | bytes 2129920 | tf_op jit(solution)/shard_map/jit(_where)/select_n | solution.py:30
  21.6 1.5 %multiply_reduce_fusion.16 = (f32[2,512]{1,0:T(2,128)S(1)}, f32[2,512]{1,0:T(2,128)S(1)}, f32[2,512]{1,0:T(2,128)S(1)}, f32[2,512]{1,0:T(2,128)S(1)}, f32[2,512]...) fusion(f32[2,512]{1,0:T(2,128)S(1)} %get-tuple-element.111, ...), kind=kLoop, calls=%fused_computation.16 | loop fusion | flops 8380416 | bytes 5296128 | tf_op jit(solution)/shard_map/reduce_sum | solution.py:210
  23.3 0.2 collective-permute-start
  23.6 1.0 %collective-permute-done = f32[2,2048]{1,0:T(2,128)S(1)} collective-permute-done((f32[2,2048]{1,0:T(2,128)S(1)}, f32[2,2048]{1,0:T(2,128)S(1)}, u32[]{:S(2)}, u32[]{:S(2)}) %collective-permute-start) | collective-permute-done | bytes 16416 | tf_op jit(solution)/shard_map/ppermute | solution.py:218
  24.6 0.2 fusion.22
  24.8 0.2 multiply_reduce_fusion.27
  25.1 0.7 %multiply_reduce_fusion.12 = (f32[2,512]{1,0:T(2,128)S(1)}, f32[2,512]{1,0:T(2,128)S(1)}, f32[2,512]{1,0:T(2,128)S(1)}, f32[2,512]{1,0:T(2,128)S(1)}) fusion(f32[2,512]{1,0:T(2,128)S(1)} %get-tuple-element.105, f32[512,512]{1,0:T(8,128)S(1)} %get-tuple-element.107, f32[2,512]{1,0:T(2,128)S(1)} %get-tuple-element.104, f32[512,512]{1,0:T(8,128)S(1)} %get-tuple-element.108, ...), kind=kLoop, calls=%fused_computation.12 | loop fusion | flops 4190208 | bytes 3170304 | tf_op jit(solution)/shard_map/reduce_sum | solution.py:210
  25.9 0.7 %multiply_reduce_fusion.8 = (f32[2,512]{1,0:T(2,128)S(1)}, f32[2,512]{1,0:T(2,128)S(1)}, f32[2,512]{1,0:T(2,128)S(1)}, f32[2,512]{1,0:T(2,128)S(1)}) fusion(f32[2,512]{1,0:T(2,128)S(1)} %get-tuple-element.101, f32[512,512]{1,0:T(8,128)S(1)} %get-tuple-element.109, f32[2,512]{1,0:T(2,128)S(1)} %get-tuple-element.103, f32[2,512]{1,0:T(2,128)S(1)} %get-tuple-element.102, ...), kind=kLoop, calls=%fused_computation.8 | loop fusion | flops 4190208 | bytes 2125824 | tf_op jit(solution)/shard_map/reduce_sum | solution.py:210
  26.7 0.2 collective-permute-start.1
  27.2 0.7 %collective-permute-done.1 = f32[2,2048]{1,0:T(2,128)S(1)} collective-permute-done((f32[2,2048]{1,0:T(2,128)S(1)}, f32[2,2048]{1,0:T(2,128)S(1)}, u32[]{:S(2)}, u32[]{:S(2)}) %collective-permute-start.1) | collective-permute-done | bytes 16416 | tf_op jit(solution)/shard_map/ppermute | solution.py:218
  28.0 0.2 multiply_reduce_fusion.26
  28.2 0.2 multiply_reduce_fusion.25
  28.4 0.2 fusion.48
  28.7 2.3 %multiply_reduce_fusion.4 = (f32[2,512]{1,0:T(2,128)S(1)}, f32[2,512]{1,0:T(2,128)S(1)}, f32[2,512]{1,0:T(2,128)S(1)}, f32[2,512]{1,0:T(2,128)S(1)}) fusion(f32[2,512]{1,0:T(2,128)S(1)} %get-tuple-element.99, f32[512,512]{1,0:T(8,128)} %copy-done, f32[2,512]{1,0:T(2,128)S(1)} %get-tuple-element.98, f32[512,512]{1,0:T(8,128)} %copy-done.1, ...), kind=kLoop, calls=%fused_computation.4 | loop fusion | flops 4190208 | bytes 3170304 | tf_op jit(solution)/shard_map/reduce_sum | solution.py:210
  31.0 0.7 %multiply_reduce_fusion = (f32[2,512]{1,0:T(2,128)S(1)}, f32[2,512]{1,0:T(2,128)S(1)}, f32[2,512]{1,0:T(2,128)S(1)}, f32[2,512]{1,0:T(2,128)S(1)}) fusion(f32[2,512]{1,0:T(2,128)S(1)} %get-tuple-element.95, f32[512,512]{1,0:T(8,128)S(1)} %get-tuple-element.109, f32[2,512]{1,0:T(2,128)S(1)} %get-tuple-element.97, f32[2,512]{1,0:T(2,128)S(1)} %get-tuple-element.96, ...), kind=kLoop, calls=%fused_computation | loop fusion | flops 4190208 | bytes 2125824 | tf_op jit(solution)/shard_map/reduce_sum | solution.py:210
  31.8 0.2 fusion.47
  32.0 0.2 collective-permute-start.2
  32.2 1.3 %fusion.10 = (f32[64]{0:T(128)S(1)}, f32[64]{0:T(128)S(1)}, f32[64]{0:T(128)S(1)}, f32[64]{0:T(128)S(1)}, f32[64]{0:T(128)S(1)}, /*index=5*/f32[64]{0:T(128)S(1)...) fusion(f32[2048]{0:T(1024)S(1)} %bitcast.67, ...), kind=kLoop, calls=%fused_computation.66 | loop fusion | flops 6814976 | bytes 69888 | tf_op jit(solution)/shard_map/reduce_sum | solution.py:132
  33.9 0.6 %reshape_multiply_fusion = f32[3,1,1,64]{3,2,1,0:T(1,128)} fusion(f32[3,64]{1,0:T(4,128)S(1)} %fusion.42, f32[64]{0:T(128)S(1)} %fusion.45), kind=kLoop, calls=%fused_computation.189 | loop fusion | flops 192 | bytes 1792 | tf_op jit(solution)/shard_map/mul | solution.py:262
  (70 shorter events, 1.9 us)
Async XLA Ops:
  2.2 14.7 %all-to-all-start = ((f32[32,1,512]{2,1,0:T(1,128)}), f32[32,1,512]{2,1,0:T(1,128)S(1)}, u32[]{:S(2)}, u32[]{:S(2)}) async-start(f32[32,1,512]{2,1,0:T(1,128)} %shard_map.77), calls=%async_computation | async-start | bytes 131072 | tf_op jit(solution)/shard_map/all_to_all | solution.py:150
  20.0 5.0 %copy-start = (f32[512,512]{1,0:T(8,128)}, f32[512,512]{1,0:T(8,128)S(1)}, u32[]{:S(2)}) copy-start(f32[512,512]{1,0:T(8,128)S(1)} %get-tuple-element.107) | copy-start | bytes 3145732
  20.1 5.0 %copy-start.1 = (f32[512,512]{1,0:T(8,128)}, f32[512,512]{1,0:T(8,128)S(1)}, u32[]{:S(2)}) copy-start(f32[512,512]{1,0:T(8,128)S(1)} %get-tuple-element.108) | copy-start | bytes 3145732
  23.3 1.2 %collective-permute-start = (f32[2,2048]{1,0:T(2,128)S(1)}, f32[2,2048]{1,0:T(2,128)S(1)}, u32[]{:S(2)}, u32[]{:S(2)}) collective-permute-start(f32[2,2048]{1,0:T(2,128)S(1)} %constant_dynamic-update-slice_fusion.16), channel_id=1, source_target_pairs={{0,1},{1,0},{2,3},{3,2},{4,5},{5,4},{6,7},{7,6},{8,9},{9,8},{10,11... | collective-permute-start | bytes 49160 | tf_op jit(solution)/shard_map/ppermute | solution.py:218
  26.7 1.2 %collective-permute-start.1 = (f32[2,2048]{1,0:T(2,128)S(1)}, f32[2,2048]{1,0:T(2,128)S(1)}, u32[]{:S(2)}, u32[]{:S(2)}) collective-permute-start(f32[2,2048]{1,0:T(2,128)S(1)} %constant_dynamic-update-slice_fusion.8), channel_id=1, source_target_pairs={{0,1},{1,0},{2,3},{3,2},{4,5},{5,4},{6,7},{7,6},{8,9},{9,8},{10,11... | collective-permute-start | bytes 49160 | tf_op jit(solution)/shard_map/ppermute | solution.py:218
  32.0 1.6 %collective-permute-start.2 = (f32[2]{0:T(128)S(1)}, f32[2]{0:T(128)S(1)}, u32[]{:S(2)}, u32[]{:S(2)}) collective-permute-start(f32[2]{0:T(128)S(1)} %get-tuple-element.47), channel_id=1, source_target_pairs={{0,1},{1,0},{2,3},{3,2},{4,5},{5,4},{6,7},{7,6},{8,9},{9,8},{10,11... | collective-permute-start | bytes 32 | tf_op jit(solution)/shard_map/ppermute | solution.py:222
  33.8 0.7 %copy-start.2 = (f32[64]{0:T(128)}, f32[64]{0:T(128)S(1)}, u32[]{:S(2)}) copy-start(f32[64]{0:T(128)S(1)} %fusion.45) | copy-start | bytes 772

commit v9 on v8

--- a/solution.py
+++ b/solution.py
@@ -218,7 +218,12 @@
                 return partial + lax.ppermute(partial, everyone, partner)
 
             def curvature(vectors):
-                mine = jnp.sum(vectors * partial_image(vectors), 1)
+                mine = 0.0
+                for k, (matrix, (row_at, col_at)) in enumerate(zip(matrices, starts)):
+                    col_part = lax.dynamic_slice_in_dim(vectors, col_at, group, 1)
+                    row_part = lax.dynamic_slice_in_dim(vectors, row_at, group, 1)
+                    term = jnp.sum(row_part * jnp.sum(matrix[None, :, :] * col_part[:, None, :], 2), 1)
+                    mine = mine + (term if k < 2 else 2.0 * term)
                 return mine + lax.ppermute(mine, everyone, partner)
         else:
             matrix = screened(row_geometry, geometry, row_index[:, None] == col_index[None, :])

time: 34.8 us -> 34.1 us (0.980)
  other arithmetic: 13.9 us -> 12.2 us
  local copies, waits for them, and re-layouts: 1.02 us -> 2.13 us
    reduce_sum x5 -> x3, other arithmetic: 6 us -> 3.01 us  [partial_image(): backward = jnp.sum(matrix[None, :, :] * row_part[:, :, None], 1)]
    reduce_sum x1 -> x6, other arithmetic: 0.21 us -> 1.45 us  [the longest x3 1.02 us: curvature(): jnp.sum(matrix[None, :, :] * col_part[:, None, :], 2)]
    unnamed x6 -> x10, local copies, waits for them, and re-layouts: 0.01 us -> 1.15 us
where the time goes in v9:
time: 34.1 us; the launch traced here: 33.9 us
  other arithmetic  12.2 us (36%)
  waiting for transfers between devices  9.06 us (27%)
  starting transfers between devices  7.94 us (23%)
  local copies, waits for them, and re-layouts  2.13 us (6%)
  Pallas kernels  1.61 us (5%)
  between operations  0.97 us (3%)
    all_to_all x1, waiting for transfers between devices, shards(): got = lax.all_to_all(payload, everyone, 0, 0, tiled=True)  7.33 us
    all_to_all x1, starting transfers between devices, shards(): got = lax.all_to_all(payload, everyone, 0, 0, tiled=True)  7.3 us
    select_n x2, other arithmetic, screened(): return jnp.where(self_pair, row_geometry[5][:, None], off)  3.82 us
    reduce_sum x3, other arithmetic, partial_image(): backward = jnp.sum(matrix[None, :, :] * row_part[:, :, None], 1)  3.01 us
    ppermute x2, waiting for transfers between devices, operate(): return partial + lax.ppermute(partial, everyone, partner)  1.73 us
    pallas_call x1, Pallas kernels, prep(): pl.pallas_call(prep_kernel, in_specs=[pl.BlockSpec(memory_space=smem), pl...  1.61 us
    reduce_sum x1, other arithmetic, pulling_fields(): jnp.sum(slope * vector[None, :] * separation, 1)  1.35 us
    unnamed x10, local copies, waits for them, and re-layouts  1.15 us
  transfers between devices with their start and end apart: 4, of which 3 were waited for; matrix products, arithmetic and copies ran while one was open for 5% of the time, Pallas kernels for 0%

profile of v9, /device:TPU:0, one launch (start us, length us, event | category | flops | bytes accessed | tf_op | source)
XLA Modules:
  0.0 33.9 jit_solution(11638076979741393647)
XLA Ops:
  0.6 1.6 %shard_map.77 = f32[32,1,512]{2,1,0:T(1,128)} custom-call(f32[4]{0:T(128)} %hard_ref.1, f32[4]{0:T(128)} %width_ref.1, f32[3,1,64]{2,1,0:T(1,128)} %bitcast.95, s32[1,64]{1,0:T(1,128)} %bitcast.96, f32[64,128]{1,0:T(8,128)} %bitcast.65, f32[4,128]{1,0:T(4,128)} %readout_ref.1), custom_call_target="tpu_custom_call" | custom-call | tf_op jit(solution)/shard_map/pallas_call | solution.py:90
  2.2 7.3 %all-to-all-start = ((f32[32,1,512]{2,1,0:T(1,128)}), f32[32,1,512]{2,1,0:T(1,128)S(1)}, u32[]{:S(2)}, u32[]{:S(2)}) async-start(f32[32,1,512]{2,1,0:T(1,128)} %shard_map.77), calls=%async_computation | async-start | bytes 131072 | tf_op jit(solution)/shard_map/all_to_all | solution.py:150
  9.6 7.3 %all-to-all-done = f32[32,1,512]{2,1,0:T(1,128)S(1)} async-done(((f32[32,1,512]{2,1,0:T(1,128)}), f32[32,1,512]{2,1,0:T(1,128)S(1)}, u32[]{:S(2)}, u32[]{:S(2)}) %all-to-all-start) | async-done | bytes 65568 | tf_op jit(solution)/shard_map/all_to_all | solution.py:150
  17.2 0.2 slice_reduce_fusion.3
  17.8 2.3 %compare_select_fusion.6 = (f32[512,512]{1,0:T(8,128)S(1)}, f32[512,512]{1,0:T(8,128)S(1)}, f32[512,512]{1,0:T(8,128)S(1)}) fusion(f32[512]{0:T(512)S(1)} %bitcast.93, f32[512]{0:T(512)S(1)} %bitcast.88, f32[512]{0:T(512)S(1)} %bitcast.89, f32[512]{0:T(512)S(1)} %bitcast.90, f32[512]{0:T(512)S(1)} %bitcast.91, s32[512]{0:T(512)S(1)} %iota_add_fusion.3, ...), kind=kLoop, calls=%fused_computation.42 | loop fusion | flops 12582912 | bytes 3170304 | tf_op jit(solution)/shard_map/jit(_where)/select_n | solution.py:30
  20.1 1.5 %compare_select_fusion = (f32[512,512]{1,0:T(8,128)S(1)}, f32[512,512]{1,0:T(8,128)S(1)}) fusion(f32[512]{0:T(512)S(1)} %bitcast.74, f32[512]{0:T(512)S(1)} %bitcast.75, f32[512]{0:T(512)S(1)} %bitcast.76, f32[512]{0:T(512)S(1)} %bitcast.77, f32[512]{0:T(512)S(1)} %bitcast.70, f32[512]{0:T(512)S(1)} %bitcast.81, f32[512]{0:T(512)S(1)} %bitcast.71, ...), kind=kLoop, calls=%fused_computation.36 | loop fusion | flops 8388608 | bytes 2129920 | tf_op jit(solution)/shard_map/jit(_where)/select_n | solution.py:30
  21.7 1.5 %multiply_reduce_fusion.13 = (f32[2,512]{1,0:T(2,128)S(1)}, f32[2,512]{1,0:T(2,128)S(1)}, f32[2,512]{1,0:T(2,128)S(1)}, f32[2,512]{1,0:T(2,128)S(1)}, f32[2,512]...) fusion(f32[2,512]{1,0:T(2,128)S(1)} %get-tuple-element.110, ...), kind=kLoop, calls=%fused_computation.13 | loop fusion | flops 8380416 | bytes 5296128 | tf_op jit(solution)/shard_map/reduce_sum | solution.py:210
  23.6 1.0 %collective-permute-done = f32[2,2048]{1,0:T(2,128)S(1)} collective-permute-done((f32[2,2048]{1,0:T(2,128)S(1)}, f32[2,2048]{1,0:T(2,128)S(1)}, u32[]{:S(2)}, u32[]{:S(2)}) %collective-permute-start) | collective-permute-done | bytes 16416 | tf_op jit(solution)/shard_map/ppermute | solution.py:218
  24.8 0.2 multiply_reduce_fusion.23
  25.1 0.7 %multiply_reduce_fusion.9 = (f32[2,512]{1,0:T(2,128)S(1)}, f32[2,512]{1,0:T(2,128)S(1)}, f32[2,512]{1,0:T(2,128)S(1)}, f32[2,512]{1,0:T(2,128)S(1)}) fusion(f32[2,512]{1,0:T(2,128)S(1)} %get-tuple-element.104, f32[512,512]{1,0:T(8,128)S(1)} %get-tuple-element.106, f32[2,512]{1,0:T(2,128)S(1)} %get-tuple-element.103, f32[512,512]{1,0:T(8,128)S(1)} %get-tuple-element.107, ...), kind=kLoop, calls=%fused_computation.9 | loop fusion | flops 4190208 | bytes 3170304 | tf_op jit(solution)/shard_map/reduce_sum | solution.py:210
  26.0 0.7 %multiply_reduce_fusion.5 = (f32[2,512]{1,0:T(2,128)S(1)}, f32[2,512]{1,0:T(2,128)S(1)}, f32[2,512]{1,0:T(2,128)S(1)}, f32[2,512]{1,0:T(2,128)S(1)}) fusion(f32[2,512]{1,0:T(2,128)S(1)} %get-tuple-element.100, f32[512,512]{1,0:T(8,128)S(1)} %get-tuple-element.108, f32[2,512]{1,0:T(2,128)S(1)} %get-tuple-element.102, f32[2,512]{1,0:T(2,128)S(1)} %get-tuple-element.101, ...), kind=kLoop, calls=%fused_computation.5 | loop fusion | flops 4190208 | bytes 2125824 | tf_op jit(solution)/shard_map/reduce_sum | solution.py:210
  26.8 0.2 collective-permute-start.1
  27.3 0.7 %collective-permute-done.1 = f32[2,2048]{1,0:T(2,128)S(1)} collective-permute-done((f32[2,2048]{1,0:T(2,128)S(1)}, f32[2,2048]{1,0:T(2,128)S(1)}, u32[]{:S(2)}, u32[]{:S(2)}) %collective-permute-start.1) | collective-permute-done | bytes 16416 | tf_op jit(solution)/shard_map/ppermute | solution.py:218
  28.0 0.2 multiply_reduce_fusion.22
  28.2 0.2 multiply_reduce_fusion.21
  28.5 0.2 fusion.44
  28.7 0.2 multiply_reduce_fusion.4
  29.0 0.4 %multiply_reduce_fusion.3 = (f32[2,512]{1,0:T(2,128)S(1)}, f32[2,512]{1,0:T(2,128)S(1)}) fusion(f32[2,512]{1,0:T(2,128)S(1)} %get-tuple-element.95, f32[512,512]{1,0:T(8,128)S(1)} %get-tuple-element.107, f32[512,512]{1,0:T(8,128)S(1)} %get-tuple-element.106), kind=kLoop, calls=%fused_computation.3 | loop fusion | flops 2095104 | bytes 2109440 | tf_op jit(solution)/shard_map/reduce_sum | solution.py:225
  29.4 0.8 %copy-done.1 = f32[512,512]{1,0:T(8,128)S(1)} copy-done((f32[512,512]{1,0:T(8,128)S(1)}, f32[512,512]{1,0:T(8,128)}, u32[]{:S(2)}) %copy-start.1) | copy-done | bytes 1048600
  30.2 0.3 copy-done.3
  30.5 0.4 %multiply_reduce_fusion.1 = (f32[2,512]{1,0:T(2,128)S(1)}, f32[2,512]{1,0:T(2,128)S(1)}) fusion(f32[2,512]{1,0:T(2,128)S(1)} %get-tuple-element.96, f32[512,512]{1,0:T(8,128)S(1)} %copy-done.3, f32[512,512]{1,0:T(8,128)S(1)} %copy-done.1), kind=kLoop, calls=%fused_computation.1 | loop fusion | flops 2095104 | bytes 2109440 | tf_op jit(solution)/shard_map/reduce_sum | solution.py:225
  31.3 0.2 collective-permute-start.2
  31.6 1.3 %fusion.10 = (f32[64]{0:T(128)S(1)}, f32[64]{0:T(128)S(1)}, f32[64]{0:T(128)S(1)}, f32[64]{0:T(128)S(1)}, f32[64]{0:T(128)S(1)}, /*index=5*/f32[64]{0:T(128)S(1)...) fusion(f32[2048]{0:T(1024)S(1)} %bitcast.67, ...), kind=kLoop, calls=%fused_computation.63 | loop fusion | flops 6814976 | bytes 69888 | tf_op jit(solution)/shard_map/reduce_sum | solution.py:132
  33.3 0.6 %reshape_multiply_fusion = f32[3,1,1,64]{3,2,1,0:T(1,128)} fusion(f32[3,64]{1,0:T(4,128)S(1)} %fusion.39, f32[64]{0:T(128)S(1)} %fusion.42), kind=kLoop, calls=%fused_computation.172 | loop fusion | flops 192 | bytes 1792 | tf_op jit(solution)/shard_map/mul | solution.py:267
  (69 shorter events, 2.5 us)
Async XLA Ops:
  2.2 14.7 %all-to-all-start = ((f32[32,1,512]{2,1,0:T(1,128)}), f32[32,1,512]{2,1,0:T(1,128)S(1)}, u32[]{:S(2)}, u32[]{:S(2)}) async-start(f32[32,1,512]{2,1,0:T(1,128)} %shard_map.77), calls=%async_computation | async-start | bytes 131072 | tf_op jit(solution)/shard_map/all_to_all | solution.py:150
  21.7 4.3 %copy-start = (f32[512,512]{1,0:T(8,128)}, f32[512,512]{1,0:T(8,128)S(1)}, u32[]{:S(2)}) copy-start(f32[512,512]{1,0:T(8,128)S(1)} %get-tuple-element.108) | copy-start | bytes 3145732
  21.7 4.3 %copy-start.2 = (f32[512,512]{1,0:T(8,128)}, f32[512,512]{1,0:T(8,128)S(1)}, u32[]{:S(2)}) copy-start(f32[512,512]{1,0:T(8,128)S(1)} %get-tuple-element.109) | copy-start | bytes 3145732
  23.4 1.2 %collective-permute-start = (f32[2,2048]{1,0:T(2,128)S(1)}, f32[2,2048]{1,0:T(2,128)S(1)}, u32[]{:S(2)}, u32[]{:S(2)}) collective-permute-start(f32[2,2048]{1,0:T(2,128)S(1)} %constant_dynamic-update-slice_fusion.8), channel_id=1, source_target_pairs={{0,1},{1,0},{2,3},{3,2},{4,5},{5,4},{6,7},{7,6},{8,9},{9,8},{10,11... | collective-permute-start | bytes 49160 | tf_op jit(solution)/shard_map/ppermute | solution.py:218
  26.8 1.2 %collective-permute-start.1 = (f32[2,2048]{1,0:T(2,128)S(1)}, f32[2,2048]{1,0:T(2,128)S(1)}, u32[]{:S(2)}, u32[]{:S(2)}) collective-permute-start(f32[2,2048]{1,0:T(2,128)S(1)} %constant_dynamic-update-slice_fusion), channel_id=1, source_target_pairs={{0,1},{1,0},{2,3},{3,2},{4,5},{5,4},{6,7},{7,6},{8,9},{9,8},{10,11... | collective-permute-start | bytes 49160 | tf_op jit(solution)/shard_map/ppermute | solution.py:218
  29.0 1.2 %copy-start.1 = (f32[512,512]{1,0:T(8,128)S(1)}, f32[512,512]{1,0:T(8,128)}, u32[]{:S(2)}) copy-start(f32[512,512]{1,0:T(8,128)} %copy-done) | copy-start | bytes 3145732
  29.0 1.5 %copy-start.3 = (f32[512,512]{1,0:T(8,128)S(1)}, f32[512,512]{1,0:T(8,128)}, u32[]{:S(2)}) copy-start(f32[512,512]{1,0:T(8,128)} %copy-done.2) | copy-start | bytes 3145732
  31.3 1.7 %collective-permute-start.2 = (f32[2]{0:T(128)S(1)}, f32[2]{0:T(128)S(1)}, u32[]{:S(2)}, u32[]{:S(2)}) collective-permute-start(f32[2]{0:T(128)S(1)} %multiply_add_fusion.2), channel_id=1, source_target_pairs={{0,1},{1,0},{2,3},{3,2},{4,5},{5,4},{6,7},{7,6},{8,9},{9,8},{10,11... | collective-permute-start | bytes 32 | tf_op jit(solution)/shard_map/ppermute | solution.py:227
  33.2 0.7 %copy-start.4 = (f32[64]{0:T(128)}, f32[64]{0:T(128)S(1)}, u32[]{:S(2)}) copy-start(f32[64]{0:T(128)S(1)} %fusion.42) | copy-start | bytes 772

commit v10 on v9

--- a/solution.py
+++ b/solution.py
@@ -12,6 +12,7 @@
 TWO_ROOT = 1.1283791670955126
 
 PAIR_LIMIT = 16 * 1024 * 1024
+FEATURES = 6
 BLOCKS = (
     ((0, 0), (1, 1), (0, 1), (0, 2), (1, 2)),
     ((2, 2), (3, 3), (2, 3), (0, 3), (1, 3)),
@@ -98,7 +99,7 @@
             pl.BlockSpec(memory_space=pltpu.VMEM),
         ],
         out_specs=pl.BlockSpec(memory_space=pltpu.VMEM),
-        out_shape=jax.ShapeDtypeStruct((devices, 1, 8 * per_brick), jnp.float32),
+        out_shape=jax.ShapeDtypeStruct((devices, 1, FEATURES * per_brick), jnp.float32),
     )(
         hardness,
         widths,
@@ -148,7 +149,7 @@
         me = lax.axis_index("row") * cols + lax.axis_index("col")
         payload = prep(positions, species, descriptors, readout, hardness, widths, devices)
         got = lax.all_to_all(payload, everyone, 0, 0, tiled=True)
-        geometry = jnp.moveaxis(got.reshape(devices, 8, per_brick), 0, 1).reshape(8, atoms)
+        geometry = jnp.moveaxis(got.reshape(devices, FEATURES, per_brick), 0, 1).reshape(FEATURES, atoms)
         own = lax.dynamic_slice_in_dim(geometry, me * per_brick, per_brick, 1)
         col_index = jnp.arange(atoms, dtype=jnp.int32)
 

time: 34.1 us -> 34 us (level)
  no operation moved by 1% of the time
where the time goes in v10:
time: 34 us; the launch traced here: 33.8 us
  other arithmetic  12.1 us (36%)
  waiting for transfers between devices  8.98 us (26%)
  starting transfers between devices  7.94 us (23%)
  local copies, waits for them, and re-layouts  2.12 us (6%)
  Pallas kernels  1.61 us (5%)
  between operations  0.97 us (3%)
    all_to_all x1, starting transfers between devices, shards(): got = lax.all_to_all(payload, everyone, 0, 0, tiled=True)  7.3 us
    all_to_all x1, waiting for transfers between devices, shards(): got = lax.all_to_all(payload, everyone, 0, 0, tiled=True)  7.25 us
    select_n x2, other arithmetic, screened(): return jnp.where(self_pair, row_geometry[5][:, None], off)  3.82 us
    reduce_sum x3, other arithmetic, partial_image(): backward = jnp.sum(matrix[None, :, :] * row_part[:, :, None], 1)  3.01 us
    ppermute x2, waiting for transfers between devices, operate(): return partial + lax.ppermute(partial, everyone, partner)  1.73 us
    pallas_call x1, Pallas kernels, prep(): pl.pallas_call(prep_kernel, in_specs=[pl.BlockSpec(memory_space=smem), pl...  1.61 us
    reduce_sum x1, other arithmetic, pulling_fields(): jnp.sum(slope * vector[None, :] * separation, 1)  1.35 us
    unnamed x10, local copies, waits for them, and re-layouts  1.15 us
  transfers between devices with their start and end apart: 4, of which 3 were waited for; matrix products, arithmetic and copies ran while one was open for 5% of the time, Pallas kernels for 0%

profile of v10, /device:TPU:0, one launch (start us, length us, event | category | flops | bytes accessed | tf_op | source)
XLA Modules:
  0.0 33.8 jit_solution(15969555813267462830)
XLA Ops:
  0.6 1.6 %shard_map.77 = f32[32,1,384]{2,1,0:T(1,128)} custom-call(f32[4]{0:T(128)} %hard_ref.1, f32[4]{0:T(128)} %width_ref.1, f32[3,1,64]{2,1,0:T(1,128)} %bitcast.95, s32[1,64]{1,0:T(1,128)} %bitcast.96, f32[64,128]{1,0:T(8,128)} %bitcast.65, f32[4,128]{1,0:T(4,128)} %readout_ref.1), custom_call_target="tpu_custom_call" | custom-call | tf_op jit(solution)/shard_map/pallas_call | solution.py:91
  2.2 7.3 %all-to-all-start = ((f32[32,1,384]{2,1,0:T(1,128)}), f32[32,1,384]{2,1,0:T(1,128)S(1)}, u32[]{:S(2)}, u32[]{:S(2)}) async-start(f32[32,1,384]{2,1,0:T(1,128)} %shard_map.77), calls=%async_computation | async-start | bytes 98304 | tf_op jit(solution)/shard_map/all_to_all | solution.py:151
  9.6 7.3 %all-to-all-done = f32[32,1,384]{2,1,0:T(1,128)S(1)} async-done(((f32[32,1,384]{2,1,0:T(1,128)}), f32[32,1,384]{2,1,0:T(1,128)S(1)}, u32[]{:S(2)}, u32[]{:S(2)}) %all-to-all-start) | async-done | bytes 49184 | tf_op jit(solution)/shard_map/all_to_all | solution.py:151
  17.1 0.2 slice_reduce_fusion.3
  17.7 2.3 %compare_select_fusion.6 = (f32[512,512]{1,0:T(8,128)S(1)}, f32[512,512]{1,0:T(8,128)S(1)}, f32[512,512]{1,0:T(8,128)S(1)}) fusion(f32[512]{0:T(512)S(1)} %bitcast.93, f32[512]{0:T(512)S(1)} %bitcast.88, f32[512]{0:T(512)S(1)} %bitcast.89, f32[512]{0:T(512)S(1)} %bitcast.90, f32[512]{0:T(512)S(1)} %bitcast.91, s32[512]{0:T(512)S(1)} %iota_add_fusion.3, ...), kind=kLoop, calls=%fused_computation.42 | loop fusion | flops 12582912 | bytes 3170304 | tf_op jit(solution)/shard_map/jit(_where)/select_n | solution.py:31
  20.0 1.5 %compare_select_fusion = (f32[512,512]{1,0:T(8,128)S(1)}, f32[512,512]{1,0:T(8,128)S(1)}) fusion(f32[512]{0:T(512)S(1)} %bitcast.74, f32[512]{0:T(512)S(1)} %bitcast.75, f32[512]{0:T(512)S(1)} %bitcast.76, f32[512]{0:T(512)S(1)} %bitcast.77, f32[512]{0:T(512)S(1)} %bitcast.70, f32[512]{0:T(512)S(1)} %bitcast.81, f32[512]{0:T(512)S(1)} %bitcast.71, ...), kind=kLoop, calls=%fused_computation.36 | loop fusion | flops 8388608 | bytes 2129920 | tf_op jit(solution)/shard_map/jit(_where)/select_n | solution.py:31
  21.6 1.5 %multiply_reduce_fusion.13 = (f32[2,512]{1,0:T(2,128)S(1)}, f32[2,512]{1,0:T(2,128)S(1)}, f32[2,512]{1,0:T(2,128)S(1)}, f32[2,512]{1,0:T(2,128)S(1)}, f32[2,512]...) fusion(f32[2,512]{1,0:T(2,128)S(1)} %get-tuple-element.110, ...), kind=kLoop, calls=%fused_computation.13 | loop fusion | flops 8380416 | bytes 5296128 | tf_op jit(solution)/shard_map/reduce_sum | solution.py:211
  23.5 1.0 %collective-permute-done = f32[2,2048]{1,0:T(2,128)S(1)} collective-permute-done((f32[2,2048]{1,0:T(2,128)S(1)}, f32[2,2048]{1,0:T(2,128)S(1)}, u32[]{:S(2)}, u32[]{:S(2)}) %collective-permute-start) | collective-permute-done | bytes 16416 | tf_op jit(solution)/shard_map/ppermute | solution.py:219
  24.7 0.2 multiply_reduce_fusion.23
  25.0 0.7 %multiply_reduce_fusion.9 = (f32[2,512]{1,0:T(2,128)S(1)}, f32[2,512]{1,0:T(2,128)S(1)}, f32[2,512]{1,0:T(2,128)S(1)}, f32[2,512]{1,0:T(2,128)S(1)}) fusion(f32[2,512]{1,0:T(2,128)S(1)} %get-tuple-element.104, f32[512,512]{1,0:T(8,128)S(1)} %get-tuple-element.106, f32[2,512]{1,0:T(2,128)S(1)} %get-tuple-element.103, f32[512,512]{1,0:T(8,128)S(1)} %get-tuple-element.107, ...), kind=kLoop, calls=%fused_computation.9 | loop fusion | flops 4190208 | bytes 3170304 | tf_op jit(solution)/shard_map/reduce_sum | solution.py:211
  25.9 0.7 %multiply_reduce_fusion.5 = (f32[2,512]{1,0:T(2,128)S(1)}, f32[2,512]{1,0:T(2,128)S(1)}, f32[2,512]{1,0:T(2,128)S(1)}, f32[2,512]{1,0:T(2,128)S(1)}) fusion(f32[2,512]{1,0:T(2,128)S(1)} %get-tuple-element.100, f32[512,512]{1,0:T(8,128)S(1)} %get-tuple-element.108, f32[2,512]{1,0:T(2,128)S(1)} %get-tuple-element.102, f32[2,512]{1,0:T(2,128)S(1)} %get-tuple-element.101, ...), kind=kLoop, calls=%fused_computation.5 | loop fusion | flops 4190208 | bytes 2125824 | tf_op jit(solution)/shard_map/reduce_sum | solution.py:211
  26.7 0.2 collective-permute-start.1
  27.2 0.7 %collective-permute-done.1 = f32[2,2048]{1,0:T(2,128)S(1)} collective-permute-done((f32[2,2048]{1,0:T(2,128)S(1)}, f32[2,2048]{1,0:T(2,128)S(1)}, u32[]{:S(2)}, u32[]{:S(2)}) %collective-permute-start.1) | collective-permute-done | bytes 16416 | tf_op jit(solution)/shard_map/ppermute | solution.py:219
  27.9 0.2 multiply_reduce_fusion.22
  28.1 0.2 multiply_reduce_fusion.21
  28.3 0.2 fusion.44
  28.6 0.2 multiply_reduce_fusion.4
  28.9 0.4 %multiply_reduce_fusion.3 = (f32[2,512]{1,0:T(2,128)S(1)}, f32[2,512]{1,0:T(2,128)S(1)}) fusion(f32[2,512]{1,0:T(2,128)S(1)} %get-tuple-element.95, f32[512,512]{1,0:T(8,128)S(1)} %get-tuple-element.107, f32[512,512]{1,0:T(8,128)S(1)} %get-tuple-element.106), kind=kLoop, calls=%fused_computation.3 | loop fusion | flops 2095104 | bytes 2109440 | tf_op jit(solution)/shard_map/reduce_sum | solution.py:226
  29.2 0.8 %copy-done.1 = f32[512,512]{1,0:T(8,128)S(1)} copy-done((f32[512,512]{1,0:T(8,128)S(1)}, f32[512,512]{1,0:T(8,128)}, u32[]{:S(2)}) %copy-start.1) | copy-done | bytes 1048600
  30.1 0.3 copy-done.3
  30.4 0.4 %multiply_reduce_fusion.1 = (f32[2,512]{1,0:T(2,128)S(1)}, f32[2,512]{1,0:T(2,128)S(1)}) fusion(f32[2,512]{1,0:T(2,128)S(1)} %get-tuple-element.96, f32[512,512]{1,0:T(8,128)S(1)} %copy-done.3, f32[512,512]{1,0:T(8,128)S(1)} %copy-done.1), kind=kLoop, calls=%fused_computation.1 | loop fusion | flops 2095104 | bytes 2109440 | tf_op jit(solution)/shard_map/reduce_sum | solution.py:226
  31.2 0.2 collective-permute-start.2
  31.5 1.3 %fusion.10 = (f32[64]{0:T(128)S(1)}, f32[64]{0:T(128)S(1)}, f32[64]{0:T(128)S(1)}, f32[64]{0:T(128)S(1)}, f32[64]{0:T(128)S(1)}, /*index=5*/f32[64]{0:T(128)S(1)...) fusion(f32[2048]{0:T(1024)S(1)} %bitcast.67, ...), kind=kLoop, calls=%fused_computation.63 | loop fusion | flops 6814976 | bytes 69888 | tf_op jit(solution)/shard_map/reduce_sum | solution.py:133
  33.2 0.6 %reshape_multiply_fusion = f32[3,1,1,64]{3,2,1,0:T(1,128)} fusion(f32[3,64]{1,0:T(4,128)S(1)} %fusion.39, f32[64]{0:T(128)S(1)} %fusion.42), kind=kLoop, calls=%fused_computation.172 | loop fusion | flops 192 | bytes 1792 | tf_op jit(solution)/shard_map/mul | solution.py:268
  (69 shorter events, 2.5 us)
Async XLA Ops:
  2.2 14.6 %all-to-all-start = ((f32[32,1,384]{2,1,0:T(1,128)}), f32[32,1,384]{2,1,0:T(1,128)S(1)}, u32[]{:S(2)}, u32[]{:S(2)}) async-start(f32[32,1,384]{2,1,0:T(1,128)} %shard_map.77), calls=%async_computation | async-start | bytes 98304 | tf_op jit(solution)/shard_map/all_to_all | solution.py:151
  21.5 4.3 %copy-start = (f32[512,512]{1,0:T(8,128)}, f32[512,512]{1,0:T(8,128)S(1)}, u32[]{:S(2)}) copy-start(f32[512,512]{1,0:T(8,128)S(1)} %get-tuple-element.108) | copy-start | bytes 3145732
  21.5 4.3 %copy-start.2 = (f32[512,512]{1,0:T(8,128)}, f32[512,512]{1,0:T(8,128)S(1)}, u32[]{:S(2)}) copy-start(f32[512,512]{1,0:T(8,128)S(1)} %get-tuple-element.109) | copy-start | bytes 3145732
  23.3 1.2 %collective-permute-start = (f32[2,2048]{1,0:T(2,128)S(1)}, f32[2,2048]{1,0:T(2,128)S(1)}, u32[]{:S(2)}, u32[]{:S(2)}) collective-permute-start(f32[2,2048]{1,0:T(2,128)S(1)} %constant_dynamic-update-slice_fusion.8), channel_id=1, source_target_pairs={{0,1},{1,0},{2,3},{3,2},{4,5},{5,4},{6,7},{7,6},{8,9},{9,8},{10,11... | collective-permute-start | bytes 49160 | tf_op jit(solution)/shard_map/ppermute | solution.py:219
  26.7 1.2 %collective-permute-start.1 = (f32[2,2048]{1,0:T(2,128)S(1)}, f32[2,2048]{1,0:T(2,128)S(1)}, u32[]{:S(2)}, u32[]{:S(2)}) collective-permute-start(f32[2,2048]{1,0:T(2,128)S(1)} %constant_dynamic-update-slice_fusion), channel_id=1, source_target_pairs={{0,1},{1,0},{2,3},{3,2},{4,5},{5,4},{6,7},{7,6},{8,9},{9,8},{10,11... | collective-permute-start | bytes 49160 | tf_op jit(solution)/shard_map/ppermute | solution.py:219
  28.8 1.2 %copy-start.1 = (f32[512,512]{1,0:T(8,128)S(1)}, f32[512,512]{1,0:T(8,128)}, u32[]{:S(2)}) copy-start(f32[512,512]{1,0:T(8,128)} %copy-done) | copy-start | bytes 3145732
  28.8 1.5 %copy-start.3 = (f32[512,512]{1,0:T(8,128)S(1)}, f32[512,512]{1,0:T(8,128)}, u32[]{:S(2)}) copy-start(f32[512,512]{1,0:T(8,128)} %copy-done.2) | copy-start | bytes 3145732
  31.2 1.7 %collective-permute-start.2 = (f32[2]{0:T(128)S(1)}, f32[2]{0:T(128)S(1)}, u32[]{:S(2)}, u32[]{:S(2)}) collective-permute-start(f32[2]{0:T(128)S(1)} %multiply_add_fusion.2), channel_id=1, source_target_pairs={{0,1},{1,0},{2,3},{3,2},{4,5},{5,4},{6,7},{7,6},{8,9},{9,8},{10,11... | collective-permute-start | bytes 32 | tf_op jit(solution)/shard_map/ppermute | solution.py:228
  33.1 0.7 %copy-start.4 = (f32[64]{0:T(128)}, f32[64]{0:T(128)S(1)}, u32[]{:S(2)}) copy-start(f32[64]{0:T(128)S(1)} %fusion.42) | copy-start | bytes 772

commit v11 on v10

--- a/solution.py
+++ b/solution.py
@@ -13,6 +13,7 @@
 
 PAIR_LIMIT = 16 * 1024 * 1024
 FEATURES = 6
+CURVATURE_ORDER = (2, 1, 0, 3, 4)
 BLOCKS = (
     ((0, 0), (1, 1), (0, 1), (0, 2), (1, 2)),
     ((2, 2), (3, 3), (2, 3), (0, 3), (1, 3)),
@@ -220,7 +221,8 @@
 
             def curvature(vectors):
                 mine = 0.0
-                for k, (matrix, (row_at, col_at)) in enumerate(zip(matrices, starts)):
+                for k in CURVATURE_ORDER:
+                    matrix, (row_at, col_at) = matrices[k], starts[k]
                     col_part = lax.dynamic_slice_in_dim(vectors, col_at, group, 1)
                     row_part = lax.dynamic_slice_in_dim(vectors, row_at, group, 1)
                     term = jnp.sum(row_part * jnp.sum(matrix[None, :, :] * col_part[:, None, :], 2), 1)

time: 34 us -> 34 us (level)
  no operation moved by 1% of the time
where the time goes in v11:
time: 34 us; the launch traced here: 33.8 us
  other arithmetic  12.1 us (36%)
  waiting for transfers between devices  8.98 us (26%)
  starting transfers between devices  7.94 us (23%)
  local copies, waits for them, and re-layouts  2.12 us (6%)
  Pallas kernels  1.61 us (5%)
  between operations  0.97 us (3%)
    all_to_all x1, starting transfers between devices, shards(): got = lax.all_to_all(payload, everyone, 0, 0, tiled=True)  7.3 us
    all_to_all x1, waiting for transfers between devices, shards(): got = lax.all_to_all(payload, everyone, 0, 0, tiled=True)  7.25 us
    select_n x2, other arithmetic, screened(): return jnp.where(self_pair, row_geometry[5][:, None], off)  3.82 us
    reduce_sum x3, other arithmetic, partial_image(): backward = jnp.sum(matrix[None, :, :] * row_part[:, :, None], 1)  3.01 us
    ppermute x2, waiting for transfers between devices, operate(): return partial + lax.ppermute(partial, everyone, partner)  1.73 us
    pallas_call x1, Pallas kernels, prep(): pl.pallas_call(prep_kernel, in_specs=[pl.BlockSpec(memory_space=smem), pl...  1.61 us
    reduce_sum x1, other arithmetic, pulling_fields(): jnp.sum(slope * vector[None, :] * separation, 1)  1.35 us
    unnamed x10, local copies, waits for them, and re-layouts  1.15 us
  transfers between devices with their start and end apart: 4, of which 3 were waited for; matrix products, arithmetic and copies ran while one was open for 5% of the time, Pallas kernels for 0%

profile of v11, /device:TPU:0, one launch (start us, length us, event | category | flops | bytes accessed | tf_op | source)
XLA Modules:
  0.0 33.8 jit_solution(7607267882659145149)
XLA Ops:
  0.6 1.6 %shard_map.77 = f32[32,1,384]{2,1,0:T(1,128)} custom-call(f32[4]{0:T(128)} %hard_ref.1, f32[4]{0:T(128)} %width_ref.1, f32[3,1,64]{2,1,0:T(1,128)} %bitcast.95, s32[1,64]{1,0:T(1,128)} %bitcast.96, f32[64,128]{1,0:T(8,128)} %bitcast.65, f32[4,128]{1,0:T(4,128)} %readout_ref.1), custom_call_target="tpu_custom_call" | custom-call | tf_op jit(solution)/shard_map/pallas_call | solution.py:92
  2.2 7.3 %all-to-all-start = ((f32[32,1,384]{2,1,0:T(1,128)}), f32[32,1,384]{2,1,0:T(1,128)S(1)}, u32[]{:S(2)}, u32[]{:S(2)}) async-start(f32[32,1,384]{2,1,0:T(1,128)} %shard_map.77), calls=%async_computation | async-start | bytes 98304 | tf_op jit(solution)/shard_map/all_to_all | solution.py:152
  9.6 7.3 %all-to-all-done = f32[32,1,384]{2,1,0:T(1,128)S(1)} async-done(((f32[32,1,384]{2,1,0:T(1,128)}), f32[32,1,384]{2,1,0:T(1,128)S(1)}, u32[]{:S(2)}, u32[]{:S(2)}) %all-to-all-start) | async-done | bytes 49184 | tf_op jit(solution)/shard_map/all_to_all | solution.py:152
  17.1 0.2 slice_reduce_fusion.3
  17.7 2.3 %compare_select_fusion.6 = (f32[512,512]{1,0:T(8,128)S(1)}, f32[512,512]{1,0:T(8,128)S(1)}, f32[512,512]{1,0:T(8,128)S(1)}) fusion(f32[512]{0:T(512)S(1)} %bitcast.93, f32[512]{0:T(512)S(1)} %bitcast.88, f32[512]{0:T(512)S(1)} %bitcast.89, f32[512]{0:T(512)S(1)} %bitcast.90, f32[512]{0:T(512)S(1)} %bitcast.91, s32[512]{0:T(512)S(1)} %iota_add_fusion.3, ...), kind=kLoop, calls=%fused_computation.42 | loop fusion | flops 12582912 | bytes 3170304 | tf_op jit(solution)/shard_map/jit(_where)/select_n | solution.py:32
  20.0 1.5 %compare_select_fusion = (f32[512,512]{1,0:T(8,128)S(1)}, f32[512,512]{1,0:T(8,128)S(1)}) fusion(f32[512]{0:T(512)S(1)} %bitcast.74, f32[512]{0:T(512)S(1)} %bitcast.75, f32[512]{0:T(512)S(1)} %bitcast.76, f32[512]{0:T(512)S(1)} %bitcast.77, f32[512]{0:T(512)S(1)} %bitcast.70, f32[512]{0:T(512)S(1)} %bitcast.81, f32[512]{0:T(512)S(1)} %bitcast.71, ...), kind=kLoop, calls=%fused_computation.36 | loop fusion | flops 8388608 | bytes 2129920 | tf_op jit(solution)/shard_map/jit(_where)/select_n | solution.py:32
  21.6 1.5 %multiply_reduce_fusion.13 = (f32[2,512]{1,0:T(2,128)S(1)}, f32[2,512]{1,0:T(2,128)S(1)}, f32[2,512]{1,0:T(2,128)S(1)}, f32[2,512]{1,0:T(2,128)S(1)}, f32[2,512]...) fusion(f32[2,512]{1,0:T(2,128)S(1)} %get-tuple-element.110, ...), kind=kLoop, calls=%fused_computation.13 | loop fusion | flops 8380416 | bytes 5296128 | tf_op jit(solution)/shard_map/reduce_sum | solution.py:212
  23.5 1.0 %collective-permute-done = f32[2,2048]{1,0:T(2,128)S(1)} collective-permute-done((f32[2,2048]{1,0:T(2,128)S(1)}, f32[2,2048]{1,0:T(2,128)S(1)}, u32[]{:S(2)}, u32[]{:S(2)}) %collective-permute-start) | collective-permute-done | bytes 16416 | tf_op jit(solution)/shard_map/ppermute | solution.py:220
  24.7 0.2 multiply_reduce_fusion.23
  25.0 0.7 %multiply_reduce_fusion.9 = (f32[2,512]{1,0:T(2,128)S(1)}, f32[2,512]{1,0:T(2,128)S(1)}, f32[2,512]{1,0:T(2,128)S(1)}, f32[2,512]{1,0:T(2,128)S(1)}) fusion(f32[2,512]{1,0:T(2,128)S(1)} %get-tuple-element.104, f32[512,512]{1,0:T(8,128)S(1)} %get-tuple-element.106, f32[2,512]{1,0:T(2,128)S(1)} %get-tuple-element.103, f32[512,512]{1,0:T(8,128)S(1)} %get-tuple-element.107, ...), kind=kLoop, calls=%fused_computation.9 | loop fusion | flops 4190208 | bytes 3170304 | tf_op jit(solution)/shard_map/reduce_sum | solution.py:212
  25.9 0.7 %multiply_reduce_fusion.5 = (f32[2,512]{1,0:T(2,128)S(1)}, f32[2,512]{1,0:T(2,128)S(1)}, f32[2,512]{1,0:T(2,128)S(1)}, f32[2,512]{1,0:T(2,128)S(1)}) fusion(f32[2,512]{1,0:T(2,128)S(1)} %get-tuple-element.100, f32[512,512]{1,0:T(8,128)S(1)} %get-tuple-element.108, f32[2,512]{1,0:T(2,128)S(1)} %get-tuple-element.102, f32[2,512]{1,0:T(2,128)S(1)} %get-tuple-element.101, ...), kind=kLoop, calls=%fused_computation.5 | loop fusion | flops 4190208 | bytes 2125824 | tf_op jit(solution)/shard_map/reduce_sum | solution.py:212
  26.7 0.2 collective-permute-start.1
  27.2 0.7 %collective-permute-done.1 = f32[2,2048]{1,0:T(2,128)S(1)} collective-permute-done((f32[2,2048]{1,0:T(2,128)S(1)}, f32[2,2048]{1,0:T(2,128)S(1)}, u32[]{:S(2)}, u32[]{:S(2)}) %collective-permute-start.1) | collective-permute-done | bytes 16416 | tf_op jit(solution)/shard_map/ppermute | solution.py:220
  27.9 0.2 multiply_reduce_fusion.22
  28.1 0.2 multiply_reduce_fusion.21
  28.3 0.2 fusion.44
  28.6 0.2 multiply_reduce_fusion.2
  28.9 0.4 %multiply_reduce_fusion.4 = (f32[2,512]{1,0:T(2,128)S(1)}, f32[2,512]{1,0:T(2,128)S(1)}) fusion(f32[2,512]{1,0:T(2,128)S(1)} %get-tuple-element.95, f32[512,512]{1,0:T(8,128)S(1)} %get-tuple-element.106, f32[512,512]{1,0:T(8,128)S(1)} %get-tuple-element.107), kind=kLoop, calls=%fused_computation.4 | loop fusion | flops 2095104 | bytes 2109440 | tf_op jit(solution)/shard_map/reduce_sum | solution.py:228
  29.2 0.8 %copy-done.1 = f32[512,512]{1,0:T(8,128)S(1)} copy-done((f32[512,512]{1,0:T(8,128)S(1)}, f32[512,512]{1,0:T(8,128)}, u32[]{:S(2)}) %copy-start.1) | copy-done | bytes 1048600
  30.1 0.3 copy-done.3
  30.4 0.4 %multiply_reduce_fusion.1 = (f32[2,512]{1,0:T(2,128)S(1)}, f32[2,512]{1,0:T(2,128)S(1)}) fusion(f32[2,512]{1,0:T(2,128)S(1)} %get-tuple-element.96, f32[512,512]{1,0:T(8,128)S(1)} %copy-done.3, f32[512,512]{1,0:T(8,128)S(1)} %copy-done.1), kind=kLoop, calls=%fused_computation.1 | loop fusion | flops 2095104 | bytes 2109440 | tf_op jit(solution)/shard_map/reduce_sum | solution.py:228
  31.2 0.2 collective-permute-start.2
  31.5 1.3 %fusion.10 = (f32[64]{0:T(128)S(1)}, f32[64]{0:T(128)S(1)}, f32[64]{0:T(128)S(1)}, f32[64]{0:T(128)S(1)}, f32[64]{0:T(128)S(1)}, /*index=5*/f32[64]{0:T(128)S(1)...) fusion(f32[2048]{0:T(1024)S(1)} %bitcast.67, ...), kind=kLoop, calls=%fused_computation.63 | loop fusion | flops 6814976 | bytes 69888 | tf_op jit(solution)/shard_map/reduce_sum | solution.py:134
  33.2 0.6 %reshape_multiply_fusion = f32[3,1,1,64]{3,2,1,0:T(1,128)} fusion(f32[3,64]{1,0:T(4,128)S(1)} %fusion.39, f32[64]{0:T(128)S(1)} %fusion.42), kind=kLoop, calls=%fused_computation.172 | loop fusion | flops 192 | bytes 1792 | tf_op jit(solution)/shard_map/mul | solution.py:270
  (69 shorter events, 2.5 us)
Async XLA Ops:
  2.2 14.6 %all-to-all-start = ((f32[32,1,384]{2,1,0:T(1,128)}), f32[32,1,384]{2,1,0:T(1,128)S(1)}, u32[]{:S(2)}, u32[]{:S(2)}) async-start(f32[32,1,384]{2,1,0:T(1,128)} %shard_map.77), calls=%async_computation | async-start | bytes 98304 | tf_op jit(solution)/shard_map/all_to_all | solution.py:152
  21.5 4.3 %copy-start = (f32[512,512]{1,0:T(8,128)}, f32[512,512]{1,0:T(8,128)S(1)}, u32[]{:S(2)}) copy-start(f32[512,512]{1,0:T(8,128)S(1)} %get-tuple-element.108) | copy-start | bytes 3145732
  21.5 4.3 %copy-start.2 = (f32[512,512]{1,0:T(8,128)}, f32[512,512]{1,0:T(8,128)S(1)}, u32[]{:S(2)}) copy-start(f32[512,512]{1,0:T(8,128)S(1)} %get-tuple-element.109) | copy-start | bytes 3145732
  23.3 1.2 %collective-permute-start = (f32[2,2048]{1,0:T(2,128)S(1)}, f32[2,2048]{1,0:T(2,128)S(1)}, u32[]{:S(2)}, u32[]{:S(2)}) collective-permute-start(f32[2,2048]{1,0:T(2,128)S(1)} %constant_dynamic-update-slice_fusion.8), channel_id=1, source_target_pairs={{0,1},{1,0},{2,3},{3,2},{4,5},{5,4},{6,7},{7,6},{8,9},{9,8},{10,11... | collective-permute-start | bytes 49160 | tf_op jit(solution)/shard_map/ppermute | solution.py:220
  26.7 1.2 %collective-permute-start.1 = (f32[2,2048]{1,0:T(2,128)S(1)}, f32[2,2048]{1,0:T(2,128)S(1)}, u32[]{:S(2)}, u32[]{:S(2)}) collective-permute-start(f32[2,2048]{1,0:T(2,128)S(1)} %constant_dynamic-update-slice_fusion), channel_id=1, source_target_pairs={{0,1},{1,0},{2,3},{3,2},{4,5},{5,4},{6,7},{7,6},{8,9},{9,8},{10,11... | collective-permute-start | bytes 49160 | tf_op jit(solution)/shard_map/ppermute | solution.py:220
  28.8 1.2 %copy-start.1 = (f32[512,512]{1,0:T(8,128)S(1)}, f32[512,512]{1,0:T(8,128)}, u32[]{:S(2)}) copy-start(f32[512,512]{1,0:T(8,128)} %copy-done) | copy-start | bytes 3145732
  28.8 1.5 %copy-start.3 = (f32[512,512]{1,0:T(8,128)S(1)}, f32[512,512]{1,0:T(8,128)}, u32[]{:S(2)}) copy-start(f32[512,512]{1,0:T(8,128)} %copy-done.2) | copy-start | bytes 3145732
  31.2 1.7 %collective-permute-start.2 = (f32[2]{0:T(128)S(1)}, f32[2]{0:T(128)S(1)}, u32[]{:S(2)}, u32[]{:S(2)}) collective-permute-start(f32[2]{0:T(128)S(1)} %multiply_add_fusion.2), channel_id=1, source_target_pairs={{0,1},{1,0},{2,3},{3,2},{4,5},{5,4},{6,7},{7,6},{8,9},{9,8},{10,11... | collective-permute-start | bytes 32 | tf_op jit(solution)/shard_map/ppermute | solution.py:230
  33.1 0.7 %copy-start.4 = (f32[64]{0:T(128)}, f32[64]{0:T(128)S(1)}, u32[]{:S(2)}) copy-start(f32[64]{0:T(128)S(1)} %fusion.42) | copy-start | bytes 772

commit v12 on v10

--- a/solution.py
+++ b/solution.py
@@ -20,14 +20,17 @@
 
 
 def screened(row_geometry, col_geometry, self_pair):
-    squared = jnp.zeros(self_pair.shape, row_geometry.dtype)
+    squared = 0.0
     for axis_id in range(3):
         separation = row_geometry[axis_id][:, None] - col_geometry[axis_id][None, :]
         squared = squared + separation * separation
-    squared = jnp.where(self_pair, 1.0, squared)
+    if self_pair is not None:
+        squared = jnp.where(self_pair, 1.0, squared)
     inverse = lax.rsqrt(squared)
     screening = lax.rsqrt(2.0 * (row_geometry[3][:, None] + col_geometry[3][None, :]))
     off = lax.erf(screening * squared * inverse) * inverse
+    if self_pair is None:
+        return off
     return jnp.where(self_pair, row_geometry[5][:, None], off)
 
 
@@ -194,7 +197,7 @@
                     screened(
                         lax.dynamic_slice_in_dim(geometry, row_at, group, 1),
                         lax.dynamic_slice_in_dim(geometry, col_at, group, 1),
-                        (row_at + offsets)[:, None] == (col_at + offsets)[None, :],
+                        offsets[:, None] == offsets[None, :] if k < 2 else None,
                     )
                 )
 

time: 34 us -> 33.3 us (0.979)
  other arithmetic: 12.1 us -> 11.4 us
    select_n x2 -> x1, other arithmetic: 3.82 us -> 1.88 us  [screened(): return jnp.where(self_pair, row_geometry[5][:, None], off)]
    mul x0 -> x1, other arithmetic: none -> 1.19 us  [screened(): off = lax.erf(screening * squared * inverse) * inverse]
where the time goes in v12:
time: 33.3 us; the launch traced here: 33 us
  other arithmetic  11.4 us (34%)
  waiting for transfers between devices  9.03 us (27%)
  starting transfers between devices  7.94 us (24%)
  local copies, waits for them, and re-layouts  2.12 us (6%)
  Pallas kernels  1.61 us (5%)
  between operations  0.94 us (3%)
    all_to_all x1, starting transfers between devices, shards(): got = lax.all_to_all(payload, everyone, 0, 0, tiled=True)  7.3 us
    all_to_all x1, waiting for transfers between devices, shards(): got = lax.all_to_all(payload, everyone, 0, 0, tiled=True)  7.3 us
    reduce_sum x3, other arithmetic, partial_image(): backward = jnp.sum(matrix[None, :, :] * row_part[:, :, None], 1)  3.01 us
    select_n x1, other arithmetic, screened(): return jnp.where(self_pair, row_geometry[5][:, None], off)  1.88 us
    ppermute x2, waiting for transfers between devices, operate(): return partial + lax.ppermute(partial, everyone, partner)  1.73 us
    pallas_call x1, Pallas kernels, prep(): pl.pallas_call(prep_kernel, in_specs=[pl.BlockSpec(memory_space=smem), pl...  1.61 us
    reduce_sum x1, other arithmetic, pulling_fields(): jnp.sum(slope * vector[None, :] * separation, 1)  1.35 us
    mul x1, other arithmetic, screened(): off = lax.erf(screening * squared * inverse) * inverse  1.19 us
  transfers between devices with their start and end apart: 4, of which 3 were waited for; matrix products, arithmetic and copies ran while one was open for 5% of the time, Pallas kernels for 0%

profile of v12, /device:TPU:0, one launch (start us, length us, event | category | flops | bytes accessed | tf_op | source)
XLA Modules:
  0.0 33.0 jit_solution(8569593289465261069)
XLA Ops:
  0.6 1.6 %shard_map.77 = f32[32,1,384]{2,1,0:T(1,128)} custom-call(f32[4]{0:T(128)} %hard_ref.1, f32[4]{0:T(128)} %width_ref.1, f32[3,1,64]{2,1,0:T(1,128)} %bitcast.91, s32[1,64]{1,0:T(1,128)} %bitcast.92, f32[64,128]{1,0:T(8,128)} %bitcast.63, f32[4,128]{1,0:T(4,128)} %readout_ref.1), custom_call_target="tpu_custom_call" | custom-call | tf_op jit(solution)/shard_map/pallas_call | solution.py:94
  2.2 7.3 %all-to-all-start = ((f32[32,1,384]{2,1,0:T(1,128)}), f32[32,1,384]{2,1,0:T(1,128)S(1)}, u32[]{:S(2)}, u32[]{:S(2)}) async-start(f32[32,1,384]{2,1,0:T(1,128)} %shard_map.77), calls=%async_computation | async-start | bytes 98304 | tf_op jit(solution)/shard_map/all_to_all | solution.py:154
  9.6 7.3 %all-to-all-done = f32[32,1,384]{2,1,0:T(1,128)S(1)} async-done(((f32[32,1,384]{2,1,0:T(1,128)}), f32[32,1,384]{2,1,0:T(1,128)S(1)}, u32[]{:S(2)}, u32[]{:S(2)}) %all-to-all-start) | async-done | bytes 49184 | tf_op jit(solution)/shard_map/all_to_all | solution.py:154
  17.1 0.2 slice_reduce_fusion.3
  17.7 1.9 %fusion.1 = (f32[512,512]{1,0:T(8,128)S(1)}, f32[512,512]{1,0:T(8,128)S(1)}, f32[512,512]{1,0:T(8,128)S(1)}) fusion(f32[512]{0:T(512)S(1)} %bitcast.89, f32[512]{0:T(512)S(1)} %bitcast.84, f32[512]{0:T(512)S(1)} %bitcast.85, f32[512]{0:T(512)S(1)} %bitcast.86, f32[512]{0:T(512)S(1)} %bitcast.87, f32[512]{0:T(512)S(1)} %bitcast.88, f32[512]{0:T(512)S(1)} %bitcast.80, ...), kind=kLoop, calls=%fused_computation.42 | loop fusion | flops 11534336 | bytes 3166208 | tf_op jit(solution)/shard_map/jit(_where)/select_n | solution.py:34
  19.6 1.2 %erf_multiply_fusion = (f32[512,512]{1,0:T(8,128)S(1)}, f32[512,512]{1,0:T(8,128)S(1)}) fusion(f32[512]{0:T(512)S(1)} %bitcast.72, f32[512]{0:T(512)S(1)} %bitcast.73, f32[512]{0:T(512)S(1)} %bitcast.74, f32[512]{0:T(512)S(1)} %bitcast.68, f32[512]{0:T(512)S(1)} %bitcast.78, f32[512]{0:T(512)S(1)} %bitcast.69, f32[512]{0:T(512)S(1)} %bitcast.70, ...), kind=kLoop, calls=%fused_computation.36 | loop fusion | flops 6815744 | bytes 2121728 | tf_op jit(solution)/shard_map/mul | solution.py:31
  20.8 1.5 %multiply_reduce_fusion.13 = (f32[2,512]{1,0:T(2,128)S(1)}, f32[2,512]{1,0:T(2,128)S(1)}, f32[2,512]{1,0:T(2,128)S(1)}, f32[2,512]{1,0:T(2,128)S(1)}, f32[2,512]...) fusion(f32[2,512]{1,0:T(2,128)S(1)} %get-tuple-element.105, ...), kind=kLoop, calls=%fused_computation.13 | loop fusion | flops 8380416 | bytes 5296128 | tf_op jit(solution)/shard_map/reduce_sum | solution.py:214
  22.8 1.0 %collective-permute-done = f32[2,2048]{1,0:T(2,128)S(1)} collective-permute-done((f32[2,2048]{1,0:T(2,128)S(1)}, f32[2,2048]{1,0:T(2,128)S(1)}, u32[]{:S(2)}, u32[]{:S(2)}) %collective-permute-start) | collective-permute-done | bytes 16416 | tf_op jit(solution)/shard_map/ppermute | solution.py:222
  23.9 0.2 multiply_reduce_fusion.23
  24.2 0.7 %multiply_reduce_fusion.9 = (f32[2,512]{1,0:T(2,128)S(1)}, f32[2,512]{1,0:T(2,128)S(1)}, f32[2,512]{1,0:T(2,128)S(1)}, f32[2,512]{1,0:T(2,128)S(1)}) fusion(f32[2,512]{1,0:T(2,128)S(1)} %get-tuple-element.102, f32[512,512]{1,0:T(8,128)S(1)} %get-tuple-element.111, f32[2,512]{1,0:T(2,128)S(1)} %get-tuple-element.101, f32[512,512]{1,0:T(8,128)S(1)} %get-tuple-element.112, ...), kind=kLoop, calls=%fused_computation.9 | loop fusion | flops 4190208 | bytes 3170304 | tf_op jit(solution)/shard_map/reduce_sum | solution.py:214
  25.1 0.7 %multiply_reduce_fusion.5 = (f32[2,512]{1,0:T(2,128)S(1)}, f32[2,512]{1,0:T(2,128)S(1)}, f32[2,512]{1,0:T(2,128)S(1)}, f32[2,512]{1,0:T(2,128)S(1)}) fusion(f32[2,512]{1,0:T(2,128)S(1)} %get-tuple-element.98, f32[512,512]{1,0:T(8,128)S(1)} %get-tuple-element.103, f32[2,512]{1,0:T(2,128)S(1)} %get-tuple-element.100, f32[2,512]{1,0:T(2,128)S(1)} %get-tuple-element.99, ...), kind=kLoop, calls=%fused_computation.5 | loop fusion | flops 4190208 | bytes 2125824 | tf_op jit(solution)/shard_map/reduce_sum | solution.py:214
  25.9 0.2 collective-permute-start.1
  26.4 0.7 %collective-permute-done.1 = f32[2,2048]{1,0:T(2,128)S(1)} collective-permute-done((f32[2,2048]{1,0:T(2,128)S(1)}, f32[2,2048]{1,0:T(2,128)S(1)}, u32[]{:S(2)}, u32[]{:S(2)}) %collective-permute-start.1) | collective-permute-done | bytes 16416 | tf_op jit(solution)/shard_map/ppermute | solution.py:222
  27.1 0.2 multiply_reduce_fusion.22
  27.4 0.2 multiply_reduce_fusion.21
  27.6 0.2 fusion.45
  27.8 0.2 multiply_reduce_fusion.4
  28.1 0.4 %multiply_reduce_fusion.3 = (f32[2,512]{1,0:T(2,128)S(1)}, f32[2,512]{1,0:T(2,128)S(1)}) fusion(f32[2,512]{1,0:T(2,128)S(1)} %get-tuple-element.93, f32[512,512]{1,0:T(8,128)S(1)} %get-tuple-element.112, f32[512,512]{1,0:T(8,128)S(1)} %get-tuple-element.111), kind=kLoop, calls=%fused_computation.3 | loop fusion | flops 2095104 | bytes 2109440 | tf_op jit(solution)/shard_map/reduce_sum | solution.py:229
  28.5 0.8 %copy-done.1 = f32[512,512]{1,0:T(8,128)S(1)} copy-done((f32[512,512]{1,0:T(8,128)S(1)}, f32[512,512]{1,0:T(8,128)}, u32[]{:S(2)}) %copy-start.1) | copy-done | bytes 1048600
  29.3 0.3 copy-done.3
  29.6 0.4 %multiply_reduce_fusion.1 = (f32[2,512]{1,0:T(2,128)S(1)}, f32[2,512]{1,0:T(2,128)S(1)}) fusion(f32[2,512]{1,0:T(2,128)S(1)} %get-tuple-element.94, f32[512,512]{1,0:T(8,128)S(1)} %copy-done.3, f32[512,512]{1,0:T(8,128)S(1)} %copy-done.1), kind=kLoop, calls=%fused_computation.1 | loop fusion | flops 2095104 | bytes 2109440 | tf_op jit(solution)/shard_map/reduce_sum | solution.py:229
  30.5 0.2 collective-permute-start.2
  30.7 1.3 %fusion.11 = (f32[64]{0:T(128)S(1)}, f32[64]{0:T(128)S(1)}, f32[64]{0:T(128)S(1)}, f32[64]{0:T(128)S(1)}, f32[64]{0:T(128)S(1)}, /*index=5*/f32[64]{0:T(128)S(1)...) fusion(f32[2048]{0:T(1024)S(1)} %bitcast.65, ...), kind=kLoop, calls=%fused_computation.56 | loop fusion | flops 6814976 | bytes 69888 | tf_op jit(solution)/shard_map/reduce_sum | solution.py:136
  32.4 0.6 %reshape_multiply_fusion = f32[3,1,1,64]{3,2,1,0:T(1,128)} fusion(f32[3,64]{1,0:T(4,128)S(1)} %fusion.40, f32[64]{0:T(128)S(1)} %fusion.43), kind=kLoop, calls=%fused_computation.161 | loop fusion | flops 192 | bytes 1792 | tf_op jit(solution)/shard_map/mul | solution.py:271
  (65 shorter events, 2.5 us)
Async XLA Ops:
  2.2 14.6 %all-to-all-start = ((f32[32,1,384]{2,1,0:T(1,128)}), f32[32,1,384]{2,1,0:T(1,128)S(1)}, u32[]{:S(2)}, u32[]{:S(2)}) async-start(f32[32,1,384]{2,1,0:T(1,128)} %shard_map.77), calls=%async_computation | async-start | bytes 98304 | tf_op jit(solution)/shard_map/all_to_all | solution.py:154
  20.8 4.3 %copy-start = (f32[512,512]{1,0:T(8,128)}, f32[512,512]{1,0:T(8,128)S(1)}, u32[]{:S(2)}) copy-start(f32[512,512]{1,0:T(8,128)S(1)} %get-tuple-element.103) | copy-start | bytes 3145732
  20.8 4.3 %copy-start.2 = (f32[512,512]{1,0:T(8,128)}, f32[512,512]{1,0:T(8,128)S(1)}, u32[]{:S(2)}) copy-start(f32[512,512]{1,0:T(8,128)S(1)} %get-tuple-element.104) | copy-start | bytes 3145732
  22.5 1.2 %collective-permute-start = (f32[2,2048]{1,0:T(2,128)S(1)}, f32[2,2048]{1,0:T(2,128)S(1)}, u32[]{:S(2)}, u32[]{:S(2)}) collective-permute-start(f32[2,2048]{1,0:T(2,128)S(1)} %constant_dynamic-update-slice_fusion.8), channel_id=1, source_target_pairs={{0,1},{1,0},{2,3},{3,2},{4,5},{5,4},{6,7},{7,6},{8,9},{9,8},{10,11... | collective-permute-start | bytes 49160 | tf_op jit(solution)/shard_map/ppermute | solution.py:222
  25.9 1.2 %collective-permute-start.1 = (f32[2,2048]{1,0:T(2,128)S(1)}, f32[2,2048]{1,0:T(2,128)S(1)}, u32[]{:S(2)}, u32[]{:S(2)}) collective-permute-start(f32[2,2048]{1,0:T(2,128)S(1)} %constant_dynamic-update-slice_fusion), channel_id=1, source_target_pairs={{0,1},{1,0},{2,3},{3,2},{4,5},{5,4},{6,7},{7,6},{8,9},{9,8},{10,11... | collective-permute-start | bytes 49160 | tf_op jit(solution)/shard_map/ppermute | solution.py:222
  28.1 1.2 %copy-start.1 = (f32[512,512]{1,0:T(8,128)S(1)}, f32[512,512]{1,0:T(8,128)}, u32[]{:S(2)}) copy-start(f32[512,512]{1,0:T(8,128)} %copy-done) | copy-start | bytes 3145732
  28.1 1.5 %copy-start.3 = (f32[512,512]{1,0:T(8,128)S(1)}, f32[512,512]{1,0:T(8,128)}, u32[]{:S(2)}) copy-start(f32[512,512]{1,0:T(8,128)} %copy-done.2) | copy-start | bytes 3145732
  30.5 1.7 %collective-permute-start.2 = (f32[2]{0:T(128)S(1)}, f32[2]{0:T(128)S(1)}, u32[]{:S(2)}, u32[]{:S(2)}) collective-permute-start(f32[2]{0:T(128)S(1)} %multiply_add_fusion.2), channel_id=1, source_target_pairs={{0,1},{1,0},{2,3},{3,2},{4,5},{5,4},{6,7},{7,6},{8,9},{9,8},{10,11... | collective-permute-start | bytes 32 | tf_op jit(solution)/shard_map/ppermute | solution.py:231
  32.3 0.7 %copy-start.4 = (f32[64]{0:T(128)}, f32[64]{0:T(128)S(1)}, u32[]{:S(2)}) copy-start(f32[64]{0:T(128)S(1)} %fusion.43) | copy-start | bytes 772

commit v13 on v12

--- a/solution.py
+++ b/solution.py
@@ -27,7 +27,7 @@
     if self_pair is not None:
         squared = jnp.where(self_pair, 1.0, squared)
     inverse = lax.rsqrt(squared)
-    screening = lax.rsqrt(2.0 * (row_geometry[3][:, None] + col_geometry[3][None, :]))
+    screening = lax.rsqrt(row_geometry[3][:, None] + col_geometry[3][None, :])
     off = lax.erf(screening * squared * inverse) * inverse
     if self_pair is None:
         return off
@@ -43,7 +43,7 @@
         squared = squared + separation * separation
     squared = jnp.where(self_pair, 1.0, squared)
     inverse = lax.rsqrt(squared)
-    screening = lax.rsqrt(2.0 * (row_geometry[3][:, None] + col_geometry[3][None, :]))
+    screening = lax.rsqrt(row_geometry[3][:, None] + col_geometry[3][None, :])
     slope = (
         (
             lax.erf(screening * squared * inverse) * inverse
@@ -81,7 +81,7 @@
         negativity = jnp.where(kinds == kind, scores[kind : kind + 1, :], negativity)
     self_term = hard + 1.0 / (width * ROOT_PI)
     per_brick = kinds.shape[-1]
-    features = [pos_ref[0], pos_ref[1], pos_ref[2], width * width, negativity, self_term]
+    features = [pos_ref[0], pos_ref[1], pos_ref[2], 2.0 * (width * width), negativity, self_term]
     features = features + [jnp.zeros(kinds.shape, jnp.float32)] * (out_ref.shape[-1] // per_brick - len(features))
     block = jnp.concatenate(features, 1)
     for slot in range(out_ref.shape[0]):
@@ -122,7 +122,7 @@
         squared = squared + separation * separation
     squared = jnp.where(self_pair, 1.0, squared)
     inverse = lax.rsqrt(squared)
-    screening = lax.rsqrt(2.0 * (row_geometry[3][:, None] + col_geometry[3][None, :]))
+    screening = lax.rsqrt(row_geometry[3][:, None] + col_geometry[3][None, :])
     slope = (
         (
             lax.erf(screening * squared * inverse) * inverse
@@ -201,24 +201,30 @@
                     )
                 )
 
-            def partial_image(vectors):
+            def partial_image(vectors, second_ones=False):
                 partial = jnp.zeros_like(vectors)
                 for k, (matrix, (row_at, col_at)) in enumerate(zip(matrices, starts)):
                     col_part = lax.dynamic_slice_in_dim(vectors, col_at, group, 1)
-                    forward = jnp.sum(matrix[None, :, :] * col_part[:, None, :], 2)
+                    if second_ones:
+                        forward = jnp.stack([jnp.sum(matrix * col_part[0][None, :], 1), jnp.sum(matrix, 1)])
+                    else:
+                        forward = jnp.sum(matrix[None, :, :] * col_part[:, None, :], 2)
                     partial = lax.dynamic_update_slice_in_dim(
                         partial, lax.dynamic_slice_in_dim(partial, row_at, group, 1) + forward, row_at, 1
                     )
                     if k >= 2:
                         row_part = lax.dynamic_slice_in_dim(vectors, row_at, group, 1)
-                        backward = jnp.sum(matrix[None, :, :] * row_part[:, :, None], 1)
+                        if second_ones:
+                            backward = jnp.stack([jnp.sum(matrix * row_part[0][:, None], 0), jnp.sum(matrix, 0)])
+                        else:
+                            backward = jnp.sum(matrix[None, :, :] * row_part[:, :, None], 1)
                         partial = lax.dynamic_update_slice_in_dim(
                             partial, lax.dynamic_slice_in_dim(partial, col_at, group, 1) + backward, col_at, 1
                         )
                 return partial
 
-            def operate(vectors):
-                partial = partial_image(vectors)
+            def operate(vectors, second_ones=False):
+                partial = partial_image(vectors, second_ones)
                 return partial + lax.ppermute(partial, everyone, partner)
 
             def curvature(vectors):
@@ -232,7 +238,7 @@
         else:
             matrix = screened(row_geometry, geometry, row_index[:, None] == col_index[None, :])
 
-            def operate(vectors):
+            def operate(vectors, second_ones=False):
                 return assemble(jnp.sum(matrix[None, :, :] * vectors[:, None, :], 2))
 
             def curvature(vectors):
@@ -245,7 +251,7 @@
         norm_now = jnp.sum(resid * resid, 1)
         own_index = me * per_brick + jnp.arange(per_brick, dtype=jnp.int32)
         for iteration in range(ITERS - 1):
-            image = operate(direction)
+            image = operate(direction, second_ones=iteration == 0)
             step_size = norm_now / jnp.sum(direction * image, 1)
             solution = solution + step_size[:, None] * direction
             resid = resid - step_size[:, None] * image

time: 33.3 us -> 33.5 us (level)
  other arithmetic: 11.4 us -> 12.9 us
  local copies, waits for them, and re-layouts: 2.12 us -> 0.96 us
    reduce_sum x0 -> x2, other arithmetic: none -> 4.63 us  [partial_image(): jnp.sum(matrix * row_part[0][:, None], 0)]
    select_n x1 -> x0, other arithmetic: 1.88 us -> none  [screened(): return jnp.where(self_pair, row_geometry[5][:, None], off)]
    reduce_sum x3 -> x2, other arithmetic: 3.01 us -> 1.47 us  [partial_image(): backward = jnp.sum(matrix[None, :, :] * row_part[:, :, None], 1)]
    reduce_sum x3 -> x2, other arithmetic: 1.02 us -> 2.46 us  [curvature(): jnp.sum(matrix[None, :, :] * col_part[:, None, :], 2)]
    mul x1 -> x0, other arithmetic: 1.19 us -> none  [screened(): off = lax.erf(screening * squared * inverse) * inverse]
    unnamed x10 -> x6, local copies, waits for them, and re-layouts: 1.15 us -> 0.01 us
where the time goes in v13:
time: 33.5 us; the launch traced here: 33.3 us
  other arithmetic  12.9 us (39%)
  waiting for transfers between devices  9.03 us (27%)
  starting transfers between devices  7.94 us (24%)
  Pallas kernels  1.61 us (5%)
  local copies, waits for them, and re-layouts  0.96 us (3%)
  between operations  0.88 us (3%)
    all_to_all x1, starting transfers between devices, shards(): got = lax.all_to_all(payload, everyone, 0, 0, tiled=True)  7.3 us
    all_to_all x1, waiting for transfers between devices, shards(): got = lax.all_to_all(payload, everyone, 0, 0, tiled=True)  7.3 us
    reduce_sum x2, other arithmetic, partial_image(): jnp.sum(matrix * row_part[0][:, None], 0)  4.63 us
    reduce_sum x2, other arithmetic, curvature(): jnp.sum(matrix[None, :, :] * col_part[:, None, :], 2)  2.46 us
    ppermute x2, waiting for transfers between devices, operate(): return partial + lax.ppermute(partial, everyone, partner)  1.73 us
    pallas_call x1, Pallas kernels, prep(): pl.pallas_call(prep_kernel, in_specs=[pl.BlockSpec(memory_space=smem), pl...  1.61 us
    reduce_sum x2, other arithmetic, partial_image(): backward = jnp.sum(matrix[None, :, :] * row_part[:, :, None], 1)  1.47 us
    reduce_sum x1, other arithmetic, pulling_fields(): jnp.sum(slope * vector[None, :] * separation, 1)  1.32 us
  transfers between devices with their start and end apart: 4, of which 3 were waited for; matrix products, arithmetic and copies ran while one was open for 5% of the time, Pallas kernels for 0%

profile of v13, /device:TPU:0, one launch (start us, length us, event | category | flops | bytes accessed | tf_op | source)
XLA Modules:
  0.0 33.3 jit_solution(10049222104989403309)
XLA Ops:
  0.6 1.6 %shard_map.77 = f32[32,1,384]{2,1,0:T(1,128)} custom-call(f32[4]{0:T(128)} %hard_ref.1, f32[4]{0:T(128)} %width_ref.1, f32[3,1,64]{2,1,0:T(1,128)} %bitcast.133, s32[1,64]{1,0:T(1,128)} %bitcast.134, f32[64,128]{1,0:T(8,128)} %bitcast.84, f32[4,128]{1,0:T(4,128)} %readout_ref.1), custom_call_target="tpu_custom_call" | custom-call | tf_op jit(solution)/shard_map/pallas_call | solution.py:94
  2.2 7.3 %all-to-all-start = ((f32[32,1,384]{2,1,0:T(1,128)}), f32[32,1,384]{2,1,0:T(1,128)S(1)}, u32[]{:S(2)}, u32[]{:S(2)}) async-start(f32[32,1,384]{2,1,0:T(1,128)} %shard_map.77), calls=%async_computation | async-start | bytes 98304 | tf_op jit(solution)/shard_map/all_to_all | solution.py:154
  9.6 7.3 %all-to-all-done = f32[32,1,384]{2,1,0:T(1,128)S(1)} async-done(((f32[32,1,384]{2,1,0:T(1,128)}), f32[32,1,384]{2,1,0:T(1,128)S(1)}, u32[]{:S(2)}, u32[]{:S(2)}) %all-to-all-start) | async-done | bytes 49184 | tf_op jit(solution)/shard_map/all_to_all | solution.py:154
  17.1 0.2 slice_reduce_fusion.3
  17.7 2.7 %multiply_reduce_fusion.17 = (f32[512]{0:T(512)S(1)}, f32[512]{0:T(512)S(1)}, f32[512]{0:T(512)S(1)}, f32[512]{0:T(512)S(1)}, f32[512]{0:T(512)S(1)}, /*index=5*...) fusion(f32[512]{0:T(512)S(1)} %bitcast.105, ...), kind=kLoop, calls=%fused_computation.37 | loop fusion | flops 13889536 | bytes 3186688 | tf_op jit(solution)/shard_map/reduce_sum | solution.py:218
  20.5 1.9 %multiply_reduce_fusion.15 = (f32[512]{0:T(512)S(1)}, f32[512]{0:T(512)S(1)}, f32[512]{0:T(512)S(1)}, f32[512]{0:T(512)S(1)}, f32[512]{0:T(512)S(1)}, /*index=5*...) fusion(f32[512]{0:T(512)S(1)} %bitcast.91, ...), kind=kLoop, calls=%fused_computation.35 | loop fusion | flops 9433088 | bytes 2144256 | tf_op jit(solution)/shard_map/reduce_sum | solution.py:218
  22.5 0.2 collective-permute-start
  22.8 1.0 %collective-permute-done = f32[2,2048]{1,0:T(2,128)S(1)} collective-permute-done((f32[2,2048]{1,0:T(2,128)S(1)}, f32[2,2048]{1,0:T(2,128)S(1)}, u32[]{:S(2)}, u32[]{:S(2)}) %collective-permute-start) | collective-permute-done | bytes 16416 | tf_op jit(solution)/shard_map/ppermute | solution.py:228
  23.8 0.2 fusion.25
  24.0 0.2 multiply_reduce_fusion.23
  24.3 0.7 %multiply_reduce_fusion.9 = (f32[2,512]{1,0:T(2,128)S(1)}, f32[2,512]{1,0:T(2,128)S(1)}, f32[2,512]{1,0:T(2,128)S(1)}, f32[2,512]{1,0:T(2,128)S(1)}) fusion(f32[2,512]{1,0:T(2,128)S(1)} %get-tuple-element.116, f32[512,512]{1,0:T(8,128)S(1)} %get-tuple-element.117, f32[2,512]{1,0:T(2,128)S(1)} %get-tuple-element.115, f32[512,512]{1,0:T(8,128)S(1)} %get-tuple-element.119, ...), kind=kLoop, calls=%fused_computation.9 | loop fusion | flops 4190208 | bytes 3170304 | tf_op jit(solution)/shard_map/reduce_sum | solution.py:220
  25.1 0.7 %multiply_reduce_fusion.5 = (f32[2,512]{1,0:T(2,128)S(1)}, f32[2,512]{1,0:T(2,128)S(1)}, f32[2,512]{1,0:T(2,128)S(1)}, f32[2,512]{1,0:T(2,128)S(1)}) fusion(f32[2,512]{1,0:T(2,128)S(1)} %get-tuple-element.112, f32[512,512]{1,0:T(8,128)S(1)} %get-tuple-element.110, f32[2,512]{1,0:T(2,128)S(1)} %get-tuple-element.114, f32[2,512]{1,0:T(2,128)S(1)} %get-tuple-element.113, ...), kind=kLoop, calls=%fused_computation.5 | loop fusion | flops 4190208 | bytes 2125824 | tf_op jit(solution)/shard_map/reduce_sum | solution.py:220
  25.9 0.2 collective-permute-start.1
  26.4 0.7 %collective-permute-done.1 = f32[2,2048]{1,0:T(2,128)S(1)} collective-permute-done((f32[2,2048]{1,0:T(2,128)S(1)}, f32[2,2048]{1,0:T(2,128)S(1)}, u32[]{:S(2)}, u32[]{:S(2)}) %collective-permute-start.1) | collective-permute-done | bytes 16416 | tf_op jit(solution)/shard_map/ppermute | solution.py:228
  27.2 0.2 multiply_reduce_fusion.22
  27.4 0.2 multiply_reduce_fusion.21
  27.6 0.2 fusion.53
  27.8 1.9 %multiply_reduce_fusion.1 = (f32[2,512]{1,0:T(2,128)S(1)}, f32[2,512]{1,0:T(2,128)S(1)}) fusion(f32[2,512]{1,0:T(2,128)S(1)} %get-tuple-element.106, f32[512,512]{1,0:T(8,128)} %copy-done.1, f32[512,512]{1,0:T(8,128)} %copy-done), kind=kLoop, calls=%fused_computation.1 | loop fusion | flops 2095104 | bytes 2109440 | tf_op jit(solution)/shard_map/reduce_sum | solution.py:235
  29.8 0.5 %multiply_reduce_fusion.3 = (f32[2,512]{1,0:T(2,128)S(1)}, f32[2,512]{1,0:T(2,128)S(1)}, f32[2,512]{1,0:T(2,128)S(1)}) fusion(f32[2,512]{1,0:T(2,128)S(1)} %get-tuple-element.105, f32[512,512]{1,0:T(8,128)S(1)} %get-tuple-element.119, f32[512,512]{1,0:T(8,128)S(1)} %get-tuple-element.117, f32[2,512]{1,0:T(2,128)S(1)} %get-tuple-element.107, ...), kind=kLoop, calls=%fused_computation.3 | loop fusion | flops 3142656 | bytes 3166208 | tf_op jit(solution)/shard_map/reduce_sum | solution.py:235
  30.4 0.1 fusion.40
  30.6 0.2 multiply_reduce_fusion.26
  30.7 0.2 collective-permute-start.2
  31.0 1.3 %fusion.11 = (f32[64]{0:T(128)S(1)}, f32[64]{0:T(128)S(1)}, f32[64]{0:T(128)S(1)}, f32[64]{0:T(128)S(1)}, f32[64]{0:T(128)S(1)}, /*index=5*/f32[64]{0:T(128)S(1)...) fusion(f32[2048]{0:T(1024)S(1)} %bitcast.87, ...), kind=kLoop, calls=%fused_computation.56 | loop fusion | flops 6683904 | bytes 69888 | tf_op jit(solution)/shard_map/reduce_sum | solution.py:136
  32.7 0.6 %reshape_multiply_fusion = f32[3,1,1,64]{3,2,1,0:T(1,128)} fusion(f32[3,64]{1,0:T(4,128)S(1)} %fusion.42, f32[64]{0:T(128)S(1)} %fusion.45), kind=kLoop, calls=%fused_computation.161 | loop fusion | flops 192 | bytes 1792 | tf_op jit(solution)/shard_map/mul | solution.py:277
  (58 shorter events, 1.8 us)
Async XLA Ops:
  2.2 14.6 %all-to-all-start = ((f32[32,1,384]{2,1,0:T(1,128)}), f32[32,1,384]{2,1,0:T(1,128)S(1)}, u32[]{:S(2)}, u32[]{:S(2)}) async-start(f32[32,1,384]{2,1,0:T(1,128)} %shard_map.77), calls=%async_computation | async-start | bytes 98304 | tf_op jit(solution)/shard_map/all_to_all | solution.py:154
  22.4 2.7 %copy-start = (f32[512,512]{1,0:T(8,128)}, f32[512,512]{1,0:T(8,128)S(1)}, u32[]{:S(2)}) copy-start(f32[512,512]{1,0:T(8,128)S(1)} %get-tuple-element.110) | copy-start | bytes 3145732
  22.4 2.7 %copy-start.1 = (f32[512,512]{1,0:T(8,128)}, f32[512,512]{1,0:T(8,128)S(1)}, u32[]{:S(2)}) copy-start(f32[512,512]{1,0:T(8,128)S(1)} %get-tuple-element.111) | copy-start | bytes 3145732
  22.5 1.2 %collective-permute-start = (f32[2,2048]{1,0:T(2,128)S(1)}, f32[2,2048]{1,0:T(2,128)S(1)}, u32[]{:S(2)}, u32[]{:S(2)}) collective-permute-start(f32[2,2048]{1,0:T(2,128)S(1)} %constant_dynamic-update-slice_fusion.8), channel_id=1, source_target_pairs={{0,1},{1,0},{2,3},{3,2},{4,5},{5,4},{6,7},{7,6},{8,9},{9,8},{10,11... | collective-permute-start | bytes 49160 | tf_op jit(solution)/shard_map/ppermute | solution.py:228
  25.9 1.2 %collective-permute-start.1 = (f32[2,2048]{1,0:T(2,128)S(1)}, f32[2,2048]{1,0:T(2,128)S(1)}, u32[]{:S(2)}, u32[]{:S(2)}) collective-permute-start(f32[2,2048]{1,0:T(2,128)S(1)} %constant_dynamic-update-slice_fusion), channel_id=1, source_target_pairs={{0,1},{1,0},{2,3},{3,2},{4,5},{5,4},{6,7},{7,6},{8,9},{9,8},{10,11... | collective-permute-start | bytes 49160 | tf_op jit(solution)/shard_map/ppermute | solution.py:228
  30.7 1.6 %collective-permute-start.2 = (f32[2]{0:T(128)S(1)}, f32[2]{0:T(128)S(1)}, u32[]{:S(2)}, u32[]{:S(2)}) collective-permute-start(f32[2]{0:T(128)S(1)} %multiply_add_fusion.2), channel_id=1, source_target_pairs={{0,1},{1,0},{2,3},{3,2},{4,5},{5,4},{6,7},{7,6},{8,9},{9,8},{10,11... | collective-permute-start | bytes 32 | tf_op jit(solution)/shard_map/ppermute | solution.py:237
  32.6 0.7 %copy-start.2 = (f32[64]{0:T(128)}, f32[64]{0:T(128)S(1)}, u32[]{:S(2)}) copy-start(f32[64]{0:T(128)S(1)} %fusion.45) | copy-start | bytes 772

commit v14 on v12

--- a/solution.py
+++ b/solution.py
@@ -27,7 +27,7 @@
     if self_pair is not None:
         squared = jnp.where(self_pair, 1.0, squared)
     inverse = lax.rsqrt(squared)
-    screening = lax.rsqrt(2.0 * (row_geometry[3][:, None] + col_geometry[3][None, :]))
+    screening = lax.rsqrt(row_geometry[3][:, None] + col_geometry[3][None, :])
     off = lax.erf(screening * squared * inverse) * inverse
     if self_pair is None:
         return off
@@ -43,7 +43,7 @@
         squared = squared + separation * separation
     squared = jnp.where(self_pair, 1.0, squared)
     inverse = lax.rsqrt(squared)
-    screening = lax.rsqrt(2.0 * (row_geometry[3][:, None] + col_geometry[3][None, :]))
+    screening = lax.rsqrt(row_geometry[3][:, None] + col_geometry[3][None, :])
     slope = (
         (
             lax.erf(screening * squared * inverse) * inverse
@@ -81,7 +81,7 @@
         negativity = jnp.where(kinds == kind, scores[kind : kind + 1, :], negativity)
     self_term = hard + 1.0 / (width * ROOT_PI)
     per_brick = kinds.shape[-1]
-    features = [pos_ref[0], pos_ref[1], pos_ref[2], width * width, negativity, self_term]
+    features = [pos_ref[0], pos_ref[1], pos_ref[2], 2.0 * (width * width), negativity, self_term]
     features = features + [jnp.zeros(kinds.shape, jnp.float32)] * (out_ref.shape[-1] // per_brick - len(features))
     block = jnp.concatenate(features, 1)
     for slot in range(out_ref.shape[0]):
@@ -122,7 +122,7 @@
         squared = squared + separation * separation
     squared = jnp.where(self_pair, 1.0, squared)
     inverse = lax.rsqrt(squared)
-    screening = lax.rsqrt(2.0 * (row_geometry[3][:, None] + col_geometry[3][None, :]))
+    screening = lax.rsqrt(row_geometry[3][:, None] + col_geometry[3][None, :])
     slope = (
         (
             lax.erf(screening * squared * inverse) * inverse

time: 33.3 us -> 33.1 us (level)
  no operation moved by 1% of the time
where the time goes in v14:
time: 33.1 us; the launch traced here: 32.8 us
  other arithmetic  11.2 us (34%)
  waiting for transfers between devices  9.03 us (27%)
  starting transfers between devices  7.94 us (24%)
  local copies, waits for them, and re-layouts  2.12 us (6%)
  Pallas kernels  1.61 us (5%)
  between operations  0.94 us (3%)
    all_to_all x1, starting transfers between devices, shards(): got = lax.all_to_all(payload, everyone, 0, 0, tiled=True)  7.3 us
    all_to_all x1, waiting for transfers between devices, shards(): got = lax.all_to_all(payload, everyone, 0, 0, tiled=True)  7.3 us
    reduce_sum x3, other arithmetic, partial_image(): backward = jnp.sum(matrix[None, :, :] * row_part[:, :, None], 1)  3.01 us
    select_n x1, other arithmetic, screened(): return jnp.where(self_pair, row_geometry[5][:, None], off)  1.8 us
    ppermute x2, waiting for transfers between devices, operate(): return partial + lax.ppermute(partial, everyone, partner)  1.73 us
    pallas_call x1, Pallas kernels, prep(): pl.pallas_call(prep_kernel, in_specs=[pl.BlockSpec(memory_space=smem), pl...  1.61 us
    reduce_sum x1, other arithmetic, pulling_fields(): jnp.sum(slope * vector[None, :] * separation, 1)  1.33 us
    unnamed x10, local copies, waits for them, and re-layouts  1.15 us
  transfers between devices with their start and end apart: 4, of which 3 were waited for; matrix products, arithmetic and copies ran while one was open for 5% of the time, Pallas kernels for 0%

profile of v14, /device:TPU:0, one launch (start us, length us, event | category | flops | bytes accessed | tf_op | source)
XLA Modules:
  0.0 32.8 jit_solution(3646656363020637657)
XLA Ops:
  0.6 1.6 %shard_map.77 = f32[32,1,384]{2,1,0:T(1,128)} custom-call(f32[4]{0:T(128)} %hard_ref.1, f32[4]{0:T(128)} %width_ref.1, f32[3,1,64]{2,1,0:T(1,128)} %bitcast.91, s32[1,64]{1,0:T(1,128)} %bitcast.92, f32[64,128]{1,0:T(8,128)} %bitcast.63, f32[4,128]{1,0:T(4,128)} %readout_ref.1), custom_call_target="tpu_custom_call" | custom-call | tf_op jit(solution)/shard_map/pallas_call | solution.py:94
  2.2 7.3 %all-to-all-start = ((f32[32,1,384]{2,1,0:T(1,128)}), f32[32,1,384]{2,1,0:T(1,128)S(1)}, u32[]{:S(2)}, u32[]{:S(2)}) async-start(f32[32,1,384]{2,1,0:T(1,128)} %shard_map.77), calls=%async_computation | async-start | bytes 98304 | tf_op jit(solution)/shard_map/all_to_all | solution.py:154
  9.6 7.3 %all-to-all-done = f32[32,1,384]{2,1,0:T(1,128)S(1)} async-done(((f32[32,1,384]{2,1,0:T(1,128)}), f32[32,1,384]{2,1,0:T(1,128)S(1)}, u32[]{:S(2)}, u32[]{:S(2)}) %all-to-all-start) | async-done | bytes 49184 | tf_op jit(solution)/shard_map/all_to_all | solution.py:154
  17.1 0.2 slice_reduce_fusion.3
  17.7 1.8 %fusion.1 = (f32[512,512]{1,0:T(8,128)S(1)}, f32[512,512]{1,0:T(8,128)S(1)}, f32[512,512]{1,0:T(8,128)S(1)}) fusion(f32[512]{0:T(512)S(1)} %bitcast.89, f32[512]{0:T(512)S(1)} %bitcast.84, f32[512]{0:T(512)S(1)} %bitcast.85, f32[512]{0:T(512)S(1)} %bitcast.86, f32[512]{0:T(512)S(1)} %bitcast.87, f32[512]{0:T(512)S(1)} %bitcast.88, f32[512]{0:T(512)S(1)} %bitcast.80, ...), kind=kLoop, calls=%fused_computation.42 | loop fusion | flops 10747904 | bytes 3166208 | tf_op jit(solution)/shard_map/jit(_where)/select_n | solution.py:34
  19.5 1.1 %erf_multiply_fusion = (f32[512,512]{1,0:T(8,128)S(1)}, f32[512,512]{1,0:T(8,128)S(1)}) fusion(f32[512]{0:T(512)S(1)} %bitcast.72, f32[512]{0:T(512)S(1)} %bitcast.73, f32[512]{0:T(512)S(1)} %bitcast.74, f32[512]{0:T(512)S(1)} %bitcast.68, f32[512]{0:T(512)S(1)} %bitcast.78, f32[512]{0:T(512)S(1)} %bitcast.69, f32[512]{0:T(512)S(1)} %bitcast.70, ...), kind=kLoop, calls=%fused_computation.36 | loop fusion | flops 6291456 | bytes 2121728 | tf_op jit(solution)/shard_map/mul | solution.py:31
  20.7 1.5 %multiply_reduce_fusion.13 = (f32[2,512]{1,0:T(2,128)S(1)}, f32[2,512]{1,0:T(2,128)S(1)}, f32[2,512]{1,0:T(2,128)S(1)}, f32[2,512]{1,0:T(2,128)S(1)}, f32[2,512]...) fusion(f32[2,512]{1,0:T(2,128)S(1)} %get-tuple-element.105, ...), kind=kLoop, calls=%fused_computation.13 | loop fusion | flops 8380416 | bytes 5296128 | tf_op jit(solution)/shard_map/reduce_sum | solution.py:214
  22.6 1.0 %collective-permute-done = f32[2,2048]{1,0:T(2,128)S(1)} collective-permute-done((f32[2,2048]{1,0:T(2,128)S(1)}, f32[2,2048]{1,0:T(2,128)S(1)}, u32[]{:S(2)}, u32[]{:S(2)}) %collective-permute-start) | collective-permute-done | bytes 16416 | tf_op jit(solution)/shard_map/ppermute | solution.py:222
  23.8 0.2 multiply_reduce_fusion.23
  24.1 0.7 %multiply_reduce_fusion.9 = (f32[2,512]{1,0:T(2,128)S(1)}, f32[2,512]{1,0:T(2,128)S(1)}, f32[2,512]{1,0:T(2,128)S(1)}, f32[2,512]{1,0:T(2,128)S(1)}) fusion(f32[2,512]{1,0:T(2,128)S(1)} %get-tuple-element.102, f32[512,512]{1,0:T(8,128)S(1)} %get-tuple-element.111, f32[2,512]{1,0:T(2,128)S(1)} %get-tuple-element.101, f32[512,512]{1,0:T(8,128)S(1)} %get-tuple-element.112, ...), kind=kLoop, calls=%fused_computation.9 | loop fusion | flops 4190208 | bytes 3170304 | tf_op jit(solution)/shard_map/reduce_sum | solution.py:214
  25.0 0.7 %multiply_reduce_fusion.5 = (f32[2,512]{1,0:T(2,128)S(1)}, f32[2,512]{1,0:T(2,128)S(1)}, f32[2,512]{1,0:T(2,128)S(1)}, f32[2,512]{1,0:T(2,128)S(1)}) fusion(f32[2,512]{1,0:T(2,128)S(1)} %get-tuple-element.98, f32[512,512]{1,0:T(8,128)S(1)} %get-tuple-element.103, f32[2,512]{1,0:T(2,128)S(1)} %get-tuple-element.100, f32[2,512]{1,0:T(2,128)S(1)} %get-tuple-element.99, ...), kind=kLoop, calls=%fused_computation.5 | loop fusion | flops 4190208 | bytes 2125824 | tf_op jit(solution)/shard_map/reduce_sum | solution.py:214
  25.8 0.2 collective-permute-start.1
  26.3 0.7 %collective-permute-done.1 = f32[2,2048]{1,0:T(2,128)S(1)} collective-permute-done((f32[2,2048]{1,0:T(2,128)S(1)}, f32[2,2048]{1,0:T(2,128)S(1)}, u32[]{:S(2)}, u32[]{:S(2)}) %collective-permute-start.1) | collective-permute-done | bytes 16416 | tf_op jit(solution)/shard_map/ppermute | solution.py:222
  27.0 0.2 multiply_reduce_fusion.22
  27.2 0.2 multiply_reduce_fusion.21
  27.4 0.2 fusion.45
  27.7 0.2 multiply_reduce_fusion.4
  28.0 0.4 %multiply_reduce_fusion.3 = (f32[2,512]{1,0:T(2,128)S(1)}, f32[2,512]{1,0:T(2,128)S(1)}) fusion(f32[2,512]{1,0:T(2,128)S(1)} %get-tuple-element.93, f32[512,512]{1,0:T(8,128)S(1)} %get-tuple-element.112, f32[512,512]{1,0:T(8,128)S(1)} %get-tuple-element.111), kind=kLoop, calls=%fused_computation.3 | loop fusion | flops 2095104 | bytes 2109440 | tf_op jit(solution)/shard_map/reduce_sum | solution.py:229
  28.3 0.8 %copy-done.1 = f32[512,512]{1,0:T(8,128)S(1)} copy-done((f32[512,512]{1,0:T(8,128)S(1)}, f32[512,512]{1,0:T(8,128)}, u32[]{:S(2)}) %copy-start.1) | copy-done | bytes 1048600
  29.2 0.3 copy-done.3
  29.5 0.4 %multiply_reduce_fusion.1 = (f32[2,512]{1,0:T(2,128)S(1)}, f32[2,512]{1,0:T(2,128)S(1)}) fusion(f32[2,512]{1,0:T(2,128)S(1)} %get-tuple-element.94, f32[512,512]{1,0:T(8,128)S(1)} %copy-done.3, f32[512,512]{1,0:T(8,128)S(1)} %copy-done.1), kind=kLoop, calls=%fused_computation.1 | loop fusion | flops 2095104 | bytes 2109440 | tf_op jit(solution)/shard_map/reduce_sum | solution.py:229
  30.3 0.2 collective-permute-start.2
  30.6 1.3 %fusion.11 = (f32[64]{0:T(128)S(1)}, f32[64]{0:T(128)S(1)}, f32[64]{0:T(128)S(1)}, f32[64]{0:T(128)S(1)}, f32[64]{0:T(128)S(1)}, /*index=5*/f32[64]{0:T(128)S(1)...) fusion(f32[2048]{0:T(1024)S(1)} %bitcast.65, ...), kind=kLoop, calls=%fused_computation.56 | loop fusion | flops 6683904 | bytes 69888 | tf_op jit(solution)/shard_map/reduce_sum | solution.py:136
  32.3 0.6 %reshape_multiply_fusion = f32[3,1,1,64]{3,2,1,0:T(1,128)} fusion(f32[3,64]{1,0:T(4,128)S(1)} %fusion.40, f32[64]{0:T(128)S(1)} %fusion.43), kind=kLoop, calls=%fused_computation.161 | loop fusion | flops 192 | bytes 1792 | tf_op jit(solution)/shard_map/mul | solution.py:271
  (65 shorter events, 2.5 us)
Async XLA Ops:
  2.2 14.6 %all-to-all-start = ((f32[32,1,384]{2,1,0:T(1,128)}), f32[32,1,384]{2,1,0:T(1,128)S(1)}, u32[]{:S(2)}, u32[]{:S(2)}) async-start(f32[32,1,384]{2,1,0:T(1,128)} %shard_map.77), calls=%async_computation | async-start | bytes 98304 | tf_op jit(solution)/shard_map/all_to_all | solution.py:154
  20.6 4.3 %copy-start = (f32[512,512]{1,0:T(8,128)}, f32[512,512]{1,0:T(8,128)S(1)}, u32[]{:S(2)}) copy-start(f32[512,512]{1,0:T(8,128)S(1)} %get-tuple-element.103) | copy-start | bytes 3145732
  20.6 4.3 %copy-start.2 = (f32[512,512]{1,0:T(8,128)}, f32[512,512]{1,0:T(8,128)S(1)}, u32[]{:S(2)}) copy-start(f32[512,512]{1,0:T(8,128)S(1)} %get-tuple-element.104) | copy-start | bytes 3145732
  22.4 1.2 %collective-permute-start = (f32[2,2048]{1,0:T(2,128)S(1)}, f32[2,2048]{1,0:T(2,128)S(1)}, u32[]{:S(2)}, u32[]{:S(2)}) collective-permute-start(f32[2,2048]{1,0:T(2,128)S(1)} %constant_dynamic-update-slice_fusion.8), channel_id=1, source_target_pairs={{0,1},{1,0},{2,3},{3,2},{4,5},{5,4},{6,7},{7,6},{8,9},{9,8},{10,11... | collective-permute-start | bytes 49160 | tf_op jit(solution)/shard_map/ppermute | solution.py:222
  25.8 1.2 %collective-permute-start.1 = (f32[2,2048]{1,0:T(2,128)S(1)}, f32[2,2048]{1,0:T(2,128)S(1)}, u32[]{:S(2)}, u32[]{:S(2)}) collective-permute-start(f32[2,2048]{1,0:T(2,128)S(1)} %constant_dynamic-update-slice_fusion), channel_id=1, source_target_pairs={{0,1},{1,0},{2,3},{3,2},{4,5},{5,4},{6,7},{7,6},{8,9},{9,8},{10,11... | collective-permute-start | bytes 49160 | tf_op jit(solution)/shard_map/ppermute | solution.py:222
  27.9 1.2 %copy-start.1 = (f32[512,512]{1,0:T(8,128)S(1)}, f32[512,512]{1,0:T(8,128)}, u32[]{:S(2)}) copy-start(f32[512,512]{1,0:T(8,128)} %copy-done) | copy-start | bytes 3145732
  27.9 1.5 %copy-start.3 = (f32[512,512]{1,0:T(8,128)S(1)}, f32[512,512]{1,0:T(8,128)}, u32[]{:S(2)}) copy-start(f32[512,512]{1,0:T(8,128)} %copy-done.2) | copy-start | bytes 3145732
  30.3 1.6 %collective-permute-start.2 = (f32[2]{0:T(128)S(1)}, f32[2]{0:T(128)S(1)}, u32[]{:S(2)}, u32[]{:S(2)}) collective-permute-start(f32[2]{0:T(128)S(1)} %multiply_add_fusion.2), channel_id=1, source_target_pairs={{0,1},{1,0},{2,3},{3,2},{4,5},{5,4},{6,7},{7,6},{8,9},{9,8},{10,11... | collective-permute-start | bytes 32 | tf_op jit(solution)/shard_map/ppermute | solution.py:231
  32.2 0.7 %copy-start.4 = (f32[64]{0:T(128)}, f32[64]{0:T(128)S(1)}, u32[]{:S(2)}) copy-start(f32[64]{0:T(128)S(1)} %fusion.43) | copy-start | bytes 772

commit v15 on v14

--- a/solution.py
+++ b/solution.py
@@ -194,10 +194,12 @@
                 starts.append((row_at, col_at))
                 offsets = jnp.arange(group, dtype=jnp.int32)
                 matrices.append(
-                    screened(
-                        lax.dynamic_slice_in_dim(geometry, row_at, group, 1),
-                        lax.dynamic_slice_in_dim(geometry, col_at, group, 1),
-                        offsets[:, None] == offsets[None, :] if k < 2 else None,
+                    lax.optimization_barrier(
+                        screened(
+                            lax.dynamic_slice_in_dim(geometry, row_at, group, 1),
+                            lax.dynamic_slice_in_dim(geometry, col_at, group, 1),
+                            offsets[:, None] == offsets[None, :] if k < 2 else None,
+                        )
                     )
                 )
 

time: 33.1 us -> 33.2 us (level)
  other arithmetic: 11.2 us -> 12.4 us
  local copies, waits for them, and re-layouts: 2.12 us -> 0.99 us
    reduce_sum x3, other arithmetic: 1.02 us -> 2.25 us  [curvature(): jnp.sum(matrix[None, :, :] * col_part[:, None, :], 2)]
    unnamed x10 -> x8, local copies, waits for them, and re-layouts: 1.15 us -> 0.02 us
where the time goes in v15:
time: 33.2 us; the launch traced here: 32.9 us
  other arithmetic  12.4 us (37%)
  waiting for transfers between devices  9.02 us (27%)
  starting transfers between devices  7.94 us (24%)
  Pallas kernels  1.61 us (5%)
  local copies, waits for them, and re-layouts  0.99 us (3%)
  between operations  0.93 us (3%)
    all_to_all x1, starting transfers between devices, shards(): got = lax.all_to_all(payload, everyone, 0, 0, tiled=True)  7.3 us
    all_to_all x1, waiting for transfers between devices, shards(): got = lax.all_to_all(payload, everyone, 0, 0, tiled=True)  7.3 us
    reduce_sum x3, other arithmetic, partial_image(): backward = jnp.sum(matrix[None, :, :] * row_part[:, :, None], 1)  3.01 us
    reduce_sum x3, other arithmetic, curvature(): jnp.sum(matrix[None, :, :] * col_part[:, None, :], 2)  2.25 us
    select_n x1, other arithmetic, screened(): return jnp.where(self_pair, row_geometry[5][:, None], off)  1.79 us
    ppermute x2, waiting for transfers between devices, operate(): return partial + lax.ppermute(partial, everyone, partner)  1.73 us
    pallas_call x1, Pallas kernels, prep(): pl.pallas_call(prep_kernel, in_specs=[pl.BlockSpec(memory_space=smem), pl...  1.61 us
    reduce_sum x1, other arithmetic, pulling_fields(): jnp.sum(slope * vector[None, :] * separation, 1)  1.33 us
  transfers between devices with their start and end apart: 4, of which 3 were waited for; matrix products, arithmetic and copies ran while one was open for 5% of the time, Pallas kernels for 0%

profile of v15, /device:TPU:0, one launch (start us, length us, event | category | flops | bytes accessed | tf_op | source)
XLA Modules:
  0.0 32.9 jit_solution(761021241250711505)
XLA Ops:
  0.6 1.6 %shard_map.77 = f32[32,1,384]{2,1,0:T(1,128)} custom-call(f32[4]{0:T(128)} %hard_ref.1, f32[4]{0:T(128)} %width_ref.1, f32[3,1,64]{2,1,0:T(1,128)} %bitcast.91, s32[1,64]{1,0:T(1,128)} %bitcast.92, f32[64,128]{1,0:T(8,128)} %bitcast.63, f32[4,128]{1,0:T(4,128)} %readout_ref.1), custom_call_target="tpu_custom_call" | custom-call | tf_op jit(solution)/shard_map/pallas_call | solution.py:94
  2.2 7.3 %all-to-all-start = ((f32[32,1,384]{2,1,0:T(1,128)}), f32[32,1,384]{2,1,0:T(1,128)S(1)}, u32[]{:S(2)}, u32[]{:S(2)}) async-start(f32[32,1,384]{2,1,0:T(1,128)} %shard_map.77), calls=%async_computation | async-start | bytes 98304 | tf_op jit(solution)/shard_map/all_to_all | solution.py:154
  9.6 7.3 %all-to-all-done = f32[32,1,384]{2,1,0:T(1,128)S(1)} async-done(((f32[32,1,384]{2,1,0:T(1,128)}), f32[32,1,384]{2,1,0:T(1,128)S(1)}, u32[]{:S(2)}, u32[]{:S(2)}) %all-to-all-start) | async-done | bytes 49184 | tf_op jit(solution)/shard_map/all_to_all | solution.py:154
  17.1 0.2 slice_reduce_fusion.3
  17.7 1.1 %erf_multiply_fusion = (f32[512,512]{1,0:T(8,128)S(1)}, f32[512,512]{1,0:T(8,128)S(1)}) fusion(f32[512]{0:T(512)S(1)} %bitcast.82, f32[512]{0:T(512)S(1)} %bitcast.83, f32[512]{0:T(512)S(1)} %bitcast.84, f32[512]{0:T(512)S(1)} %bitcast.78, f32[512]{0:T(512)S(1)} %bitcast.88, f32[512]{0:T(512)S(1)} %bitcast.79, f32[512]{0:T(512)S(1)} %bitcast.80, ...), kind=kLoop, calls=%fused_computation.36 | loop fusion | flops 6291456 | bytes 2121728 | tf_op jit(solution)/shard_map/mul | solution.py:31
  18.8 1.8 %fusion.1 = (f32[512,512]{1,0:T(8,128)S(1)}, f32[512,512]{1,0:T(8,128)S(1)}, f32[512,512]{1,0:T(8,128)S(1)}) fusion(f32[512]{0:T(512)S(1)} %bitcast.77, f32[512]{0:T(512)S(1)} %bitcast.72, f32[512]{0:T(512)S(1)} %bitcast.73, f32[512]{0:T(512)S(1)} %bitcast.74, f32[512]{0:T(512)S(1)} %bitcast.75, f32[512]{0:T(512)S(1)} %bitcast.76, f32[512]{0:T(512)S(1)} %bitcast.68, ...), kind=kLoop, calls=%fused_computation.42 | loop fusion | flops 10747904 | bytes 3166208 | tf_op jit(solution)/shard_map/jit(_where)/select_n | solution.py:34
  20.6 1.5 %multiply_reduce_fusion.13 = (f32[2,512]{1,0:T(2,128)S(1)}, f32[2,512]{1,0:T(2,128)S(1)}, f32[2,512]{1,0:T(2,128)S(1)}, f32[2,512]{1,0:T(2,128)S(1)}, f32[2,512]...) fusion(f32[2,512]{1,0:T(2,128)S(1)} %get-tuple-element.105, ...), kind=kLoop, calls=%fused_computation.13 | loop fusion | flops 8380416 | bytes 5296128 | tf_op jit(solution)/shard_map/reduce_sum | solution.py:216
  22.4 0.2 collective-permute-start
  22.6 1.0 %collective-permute-done = f32[2,2048]{1,0:T(2,128)S(1)} collective-permute-done((f32[2,2048]{1,0:T(2,128)S(1)}, f32[2,2048]{1,0:T(2,128)S(1)}, u32[]{:S(2)}, u32[]{:S(2)}) %collective-permute-start) | collective-permute-done | bytes 16416 | tf_op jit(solution)/shard_map/ppermute | solution.py:224
  23.6 0.2 fusion.23
  23.8 0.2 multiply_reduce_fusion.23
  24.1 0.7 %multiply_reduce_fusion.9 = (f32[2,512]{1,0:T(2,128)S(1)}, f32[2,512]{1,0:T(2,128)S(1)}, f32[2,512]{1,0:T(2,128)S(1)}, f32[2,512]{1,0:T(2,128)S(1)}) fusion(f32[2,512]{1,0:T(2,128)S(1)} %get-tuple-element.102, f32[512,512]{1,0:T(8,128)S(1)} %get-tuple-element.111, f32[2,512]{1,0:T(2,128)S(1)} %get-tuple-element.101, f32[512,512]{1,0:T(8,128)S(1)} %get-tuple-element.112, ...), kind=kLoop, calls=%fused_computation.9 | loop fusion | flops 4190208 | bytes 3170304 | tf_op jit(solution)/shard_map/reduce_sum | solution.py:216
  24.9 0.7 %multiply_reduce_fusion.5 = (f32[2,512]{1,0:T(2,128)S(1)}, f32[2,512]{1,0:T(2,128)S(1)}, f32[2,512]{1,0:T(2,128)S(1)}, f32[2,512]{1,0:T(2,128)S(1)}) fusion(f32[2,512]{1,0:T(2,128)S(1)} %get-tuple-element.98, f32[512,512]{1,0:T(8,128)S(1)} %get-tuple-element.103, f32[2,512]{1,0:T(2,128)S(1)} %get-tuple-element.100, f32[2,512]{1,0:T(2,128)S(1)} %get-tuple-element.99, ...), kind=kLoop, calls=%fused_computation.5 | loop fusion | flops 4190208 | bytes 2125824 | tf_op jit(solution)/shard_map/reduce_sum | solution.py:216
  25.7 0.2 collective-permute-start.1
  26.3 0.7 %collective-permute-done.1 = f32[2,2048]{1,0:T(2,128)S(1)} collective-permute-done((f32[2,2048]{1,0:T(2,128)S(1)}, f32[2,2048]{1,0:T(2,128)S(1)}, u32[]{:S(2)}, u32[]{:S(2)}) %collective-permute-start.1) | collective-permute-done | bytes 16416 | tf_op jit(solution)/shard_map/ppermute | solution.py:224
  27.0 0.2 multiply_reduce_fusion.22
  27.2 0.2 multiply_reduce_fusion.21
  27.4 0.2 fusion.45
  27.7 1.5 %multiply_reduce_fusion.4 = f32[2,512]{1,0:T(2,128)S(1)} fusion(f32[2,512]{1,0:T(2,128)S(1)} %get-tuple-element.95, f32[512,512]{1,0:T(8,128)} %copy-done.2), kind=kLoop, calls=%fused_computation.4 | loop fusion | flops 1047552 | bytes 1056768 | tf_op jit(solution)/shard_map/reduce_sum | solution.py:231
  29.2 0.4 %multiply_reduce_fusion.3 = (f32[2,512]{1,0:T(2,128)S(1)}, f32[2,512]{1,0:T(2,128)S(1)}) fusion(f32[2,512]{1,0:T(2,128)S(1)} %get-tuple-element.93, f32[512,512]{1,0:T(8,128)S(1)} %copy-done.1, f32[512,512]{1,0:T(8,128)S(1)} %get-tuple-element.111), kind=kLoop, calls=%fused_computation.3 | loop fusion | flops 2095104 | bytes 2109440 | tf_op jit(solution)/shard_map/reduce_sum | solution.py:231
  29.6 0.4 %multiply_reduce_fusion.1 = (f32[2,512]{1,0:T(2,128)S(1)}, f32[2,512]{1,0:T(2,128)S(1)}) fusion(f32[2,512]{1,0:T(2,128)S(1)} %get-tuple-element.94, f32[512,512]{1,0:T(8,128)S(1)} %get-tuple-element.104, f32[512,512]{1,0:T(8,128)S(1)} %get-tuple-element.103), kind=kLoop, calls=%fused_computation.1 | loop fusion | flops 2095104 | bytes 2109440 | tf_op jit(solution)/shard_map/reduce_sum | solution.py:231
  30.4 0.2 collective-permute-start.2
  30.6 1.3 %fusion.11 = (f32[64]{0:T(128)S(1)}, f32[64]{0:T(128)S(1)}, f32[64]{0:T(128)S(1)}, f32[64]{0:T(128)S(1)}, f32[64]{0:T(128)S(1)}, /*index=5*/f32[64]{0:T(128)S(1)...) fusion(f32[2048]{0:T(1024)S(1)} %bitcast.65, ...), kind=kLoop, calls=%fused_computation.56 | loop fusion | flops 6683904 | bytes 69888 | tf_op jit(solution)/shard_map/reduce_sum | solution.py:136
  32.3 0.6 %reshape_multiply_fusion = f32[3,1,1,64]{3,2,1,0:T(1,128)} fusion(f32[3,64]{1,0:T(4,128)S(1)} %fusion.40, f32[64]{0:T(128)S(1)} %fusion.43), kind=kLoop, calls=%fused_computation.161 | loop fusion | flops 192 | bytes 1792 | tf_op jit(solution)/shard_map/mul | solution.py:273
  (63 shorter events, 2.1 us)
Async XLA Ops:
  2.2 14.6 %all-to-all-start = ((f32[32,1,384]{2,1,0:T(1,128)}), f32[32,1,384]{2,1,0:T(1,128)S(1)}, u32[]{:S(2)}, u32[]{:S(2)}) async-start(f32[32,1,384]{2,1,0:T(1,128)} %shard_map.77), calls=%async_computation | async-start | bytes 98304 | tf_op jit(solution)/shard_map/all_to_all | solution.py:154
  20.6 3.5 %copy-start = (f32[512,512]{1,0:T(8,128)}, f32[512,512]{1,0:T(8,128)S(1)}, u32[]{:S(2)}) copy-start(f32[512,512]{1,0:T(8,128)S(1)} %get-tuple-element.112) | copy-start | bytes 3145732
  20.6 3.5 %copy-start.2 = (f32[512,512]{1,0:T(8,128)}, f32[512,512]{1,0:T(8,128)S(1)}, u32[]{:S(2)}) copy-start(f32[512,512]{1,0:T(8,128)S(1)} %get-tuple-element.110) | copy-start | bytes 3145732
  22.4 1.2 %collective-permute-start = (f32[2,2048]{1,0:T(2,128)S(1)}, f32[2,2048]{1,0:T(2,128)S(1)}, u32[]{:S(2)}, u32[]{:S(2)}) collective-permute-start(f32[2,2048]{1,0:T(2,128)S(1)} %constant_dynamic-update-slice_fusion.8), channel_id=1, source_target_pairs={{0,1},{1,0},{2,3},{3,2},{4,5},{5,4},{6,7},{7,6},{8,9},{9,8},{10,11... | collective-permute-start | bytes 49160 | tf_op jit(solution)/shard_map/ppermute | solution.py:224
  25.7 1.2 %collective-permute-start.1 = (f32[2,2048]{1,0:T(2,128)S(1)}, f32[2,2048]{1,0:T(2,128)S(1)}, u32[]{:S(2)}, u32[]{:S(2)}) collective-permute-start(f32[2,2048]{1,0:T(2,128)S(1)} %constant_dynamic-update-slice_fusion), channel_id=1, source_target_pairs={{0,1},{1,0},{2,3},{3,2},{4,5},{5,4},{6,7},{7,6},{8,9},{9,8},{10,11... | collective-permute-start | bytes 49160 | tf_op jit(solution)/shard_map/ppermute | solution.py:224
  26.3 2.9 %copy-start.1 = (f32[512,512]{1,0:T(8,128)S(1)}, f32[512,512]{1,0:T(8,128)}, u32[]{:S(2)}) copy-start(f32[512,512]{1,0:T(8,128)} %copy-done) | copy-start | bytes 3145732
  30.4 1.6 %collective-permute-start.2 = (f32[2]{0:T(128)S(1)}, f32[2]{0:T(128)S(1)}, u32[]{:S(2)}, u32[]{:S(2)}) collective-permute-start(f32[2]{0:T(128)S(1)} %multiply_add_fusion.2), channel_id=1, source_target_pairs={{0,1},{1,0},{2,3},{3,2},{4,5},{5,4},{6,7},{7,6},{8,9},{9,8},{10,11... | collective-permute-start | bytes 32 | tf_op jit(solution)/shard_map/ppermute | solution.py:233
  32.3 0.7 %copy-start.3 = (f32[64]{0:T(128)}, f32[64]{0:T(128)S(1)}, u32[]{:S(2)}) copy-start(f32[64]{0:T(128)S(1)} %fusion.43) | copy-start | bytes 772

commit v16 on v15

--- a/solution.py
+++ b/solution.py
@@ -64,11 +64,13 @@
 
 def prep_kernel(hard_ref, width_ref, pos_ref, species_ref, desc_ref, readout_ref, out_ref):
     kinds = species_ref[...]
+    hard_row = hard_ref[...]
+    width_row = width_ref[...]
     hard = jnp.zeros(kinds.shape, jnp.float32)
     width = jnp.zeros(kinds.shape, jnp.float32)
-    for kind in range(hard_ref.shape[0]):
-        hard = jnp.where(kinds == kind, hard_ref[kind], hard)
-        width = jnp.where(kinds == kind, width_ref[kind], width)
+    for kind in range(hard_ref.shape[1]):
+        hard = jnp.where(kinds == kind, hard_row[:, kind : kind + 1], hard)
+        width = jnp.where(kinds == kind, width_row[:, kind : kind + 1], width)
     scores = lax.dot_general(
         readout_ref[...],
         desc_ref[...],
@@ -77,7 +79,7 @@
         preferred_element_type=jnp.float32,
     )
     negativity = jnp.zeros(kinds.shape, jnp.float32)
-    for kind in range(hard_ref.shape[0]):
+    for kind in range(hard_ref.shape[1]):
         negativity = jnp.where(kinds == kind, scores[kind : kind + 1, :], negativity)
     self_term = hard + 1.0 / (width * ROOT_PI)
     per_brick = kinds.shape[-1]
@@ -90,12 +92,11 @@
 
 def prep(positions, species, descriptors, readout, hardness, widths, devices):
     per_brick = species.shape[-1]
-    smem = pltpu.MemorySpace.SMEM if hasattr(pltpu, "MemorySpace") else pltpu.SMEM
     return pl.pallas_call(
         prep_kernel,
         in_specs=[
-            pl.BlockSpec(memory_space=smem),
-            pl.BlockSpec(memory_space=smem),
+            pl.BlockSpec(memory_space=pltpu.VMEM),
+            pl.BlockSpec(memory_space=pltpu.VMEM),
             pl.BlockSpec(memory_space=pltpu.VMEM),
             pl.BlockSpec(memory_space=pltpu.VMEM),
             pl.BlockSpec(memory_space=pltpu.VMEM),
@@ -104,8 +105,8 @@
         out_specs=pl.BlockSpec(memory_space=pltpu.VMEM),
         out_shape=jax.ShapeDtypeStruct((devices, 1, FEATURES * per_brick), jnp.float32),
     )(
-        hardness,
-        widths,
+        hardness.reshape(1, -1),
+        widths.reshape(1, -1),
         positions.reshape(3, 1, per_brick),
         species.reshape(1, per_brick),
         descriptors.reshape(descriptors.shape[0], per_brick).T,

time: 33.2 us -> 33.2 us (level)
  no operation moved by 1% of the time
where the time goes in v16:
time: 33.2 us; the launch traced here: 32.9 us
  other arithmetic  12.4 us (37%)
  waiting for transfers between devices  9.02 us (27%)
  starting transfers between devices  7.94 us (24%)
  Pallas kernels  1.63 us (5%)
  local copies, waits for them, and re-layouts  0.99 us (3%)
  between operations  0.93 us (3%)
    all_to_all x1, starting transfers between devices, shards(): got = lax.all_to_all(payload, everyone, 0, 0, tiled=True)  7.3 us
    all_to_all x1, waiting for transfers between devices, shards(): got = lax.all_to_all(payload, everyone, 0, 0, tiled=True)  7.3 us
    reduce_sum x3, other arithmetic, partial_image(): backward = jnp.sum(matrix[None, :, :] * row_part[:, :, None], 1)  3.01 us
    reduce_sum x3, other arithmetic, curvature(): jnp.sum(matrix[None, :, :] * col_part[:, None, :], 2)  2.25 us
    select_n x1, other arithmetic, screened(): return jnp.where(self_pair, row_geometry[5][:, None], off)  1.79 us
    ppermute x2, waiting for transfers between devices, operate(): return partial + lax.ppermute(partial, everyone, partner)  1.73 us
    pallas_call x1, Pallas kernels, prep(): pl.pallas_call(prep_kernel, in_specs=[pl.BlockSpec(memory_space=pltpu.VME...  1.63 us
    reduce_sum x1, other arithmetic, pulling_fields(): jnp.sum(slope * vector[None, :] * separation, 1)  1.33 us
  transfers between devices with their start and end apart: 4, of which 3 were waited for; matrix products, arithmetic and copies ran while one was open for 5% of the time, Pallas kernels for 0%

profile of v16, /device:TPU:0, one launch (start us, length us, event | category | flops | bytes accessed | tf_op | source)
XLA Modules:
  0.0 32.9 jit_solution(1266848753219349616)
XLA Ops:
  0.6 1.6 %shard_map.77 = f32[32,1,384]{2,1,0:T(1,128)} custom-call(f32[1,4]{1,0:T(1,128)} %bitcast.94, f32[1,4]{1,0:T(1,128)} %bitcast.95, f32[3,1,64]{2,1,0:T(1,128)} %bitcast.93, s32[1,64]{1,0:T(1,128)} %bitcast.96, f32[64,128]{1,0:T(8,128)} %bitcast.65, f32[4,128]{1,0:T(4,128)} %readout_ref.1), custom_call_target="tpu_custom_call" | custom-call | tf_op jit(solution)/shard_map/pallas_call | solution.py:95
  2.3 7.3 %all-to-all-start = ((f32[32,1,384]{2,1,0:T(1,128)}), f32[32,1,384]{2,1,0:T(1,128)S(1)}, u32[]{:S(2)}, u32[]{:S(2)}) async-start(f32[32,1,384]{2,1,0:T(1,128)} %shard_map.77), calls=%async_computation | async-start | bytes 98304 | tf_op jit(solution)/shard_map/all_to_all | solution.py:155
  9.6 7.3 %all-to-all-done = f32[32,1,384]{2,1,0:T(1,128)S(1)} async-done(((f32[32,1,384]{2,1,0:T(1,128)}), f32[32,1,384]{2,1,0:T(1,128)S(1)}, u32[]{:S(2)}, u32[]{:S(2)}) %all-to-all-start) | async-done | bytes 49184 | tf_op jit(solution)/shard_map/all_to_all | solution.py:155
  17.1 0.2 slice_reduce_fusion.3
  17.7 1.1 %erf_multiply_fusion = (f32[512,512]{1,0:T(8,128)S(1)}, f32[512,512]{1,0:T(8,128)S(1)}) fusion(f32[512]{0:T(512)S(1)} %bitcast.84, f32[512]{0:T(512)S(1)} %bitcast.85, f32[512]{0:T(512)S(1)} %bitcast.86, f32[512]{0:T(512)S(1)} %bitcast.80, f32[512]{0:T(512)S(1)} %bitcast.90, f32[512]{0:T(512)S(1)} %bitcast.81, f32[512]{0:T(512)S(1)} %bitcast.82, ...), kind=kLoop, calls=%fused_computation.36 | loop fusion | flops 6291456 | bytes 2121728 | tf_op jit(solution)/shard_map/mul | solution.py:31
  18.8 1.8 %fusion.1 = (f32[512,512]{1,0:T(8,128)S(1)}, f32[512,512]{1,0:T(8,128)S(1)}, f32[512,512]{1,0:T(8,128)S(1)}) fusion(f32[512]{0:T(512)S(1)} %bitcast.79, f32[512]{0:T(512)S(1)} %bitcast.74, f32[512]{0:T(512)S(1)} %bitcast.75, f32[512]{0:T(512)S(1)} %bitcast.76, f32[512]{0:T(512)S(1)} %bitcast.77, f32[512]{0:T(512)S(1)} %bitcast.78, f32[512]{0:T(512)S(1)} %bitcast.70, ...), kind=kLoop, calls=%fused_computation.42 | loop fusion | flops 10747904 | bytes 3166208 | tf_op jit(solution)/shard_map/jit(_where)/select_n | solution.py:34
  20.7 1.5 %multiply_reduce_fusion.13 = (f32[2,512]{1,0:T(2,128)S(1)}, f32[2,512]{1,0:T(2,128)S(1)}, f32[2,512]{1,0:T(2,128)S(1)}, f32[2,512]{1,0:T(2,128)S(1)}, f32[2,512]...) fusion(f32[2,512]{1,0:T(2,128)S(1)} %get-tuple-element.105, ...), kind=kLoop, calls=%fused_computation.13 | loop fusion | flops 8380416 | bytes 5296128 | tf_op jit(solution)/shard_map/reduce_sum | solution.py:217
  22.4 0.2 collective-permute-start
  22.6 1.0 %collective-permute-done = f32[2,2048]{1,0:T(2,128)S(1)} collective-permute-done((f32[2,2048]{1,0:T(2,128)S(1)}, f32[2,2048]{1,0:T(2,128)S(1)}, u32[]{:S(2)}, u32[]{:S(2)}) %collective-permute-start) | collective-permute-done | bytes 16416 | tf_op jit(solution)/shard_map/ppermute | solution.py:225
  23.6 0.2 fusion.23
  23.8 0.2 multiply_reduce_fusion.23
  24.1 0.7 %multiply_reduce_fusion.9 = (f32[2,512]{1,0:T(2,128)S(1)}, f32[2,512]{1,0:T(2,128)S(1)}, f32[2,512]{1,0:T(2,128)S(1)}, f32[2,512]{1,0:T(2,128)S(1)}) fusion(f32[2,512]{1,0:T(2,128)S(1)} %get-tuple-element.102, f32[512,512]{1,0:T(8,128)S(1)} %get-tuple-element.111, f32[2,512]{1,0:T(2,128)S(1)} %get-tuple-element.101, f32[512,512]{1,0:T(8,128)S(1)} %get-tuple-element.112, ...), kind=kLoop, calls=%fused_computation.9 | loop fusion | flops 4190208 | bytes 3170304 | tf_op jit(solution)/shard_map/reduce_sum | solution.py:217
  25.0 0.7 %multiply_reduce_fusion.5 = (f32[2,512]{1,0:T(2,128)S(1)}, f32[2,512]{1,0:T(2,128)S(1)}, f32[2,512]{1,0:T(2,128)S(1)}, f32[2,512]{1,0:T(2,128)S(1)}) fusion(f32[2,512]{1,0:T(2,128)S(1)} %get-tuple-element.98, f32[512,512]{1,0:T(8,128)S(1)} %get-tuple-element.103, f32[2,512]{1,0:T(2,128)S(1)} %get-tuple-element.100, f32[2,512]{1,0:T(2,128)S(1)} %get-tuple-element.99, ...), kind=kLoop, calls=%fused_computation.5 | loop fusion | flops 4190208 | bytes 2125824 | tf_op jit(solution)/shard_map/reduce_sum | solution.py:217
  25.8 0.2 collective-permute-start.1
  26.3 0.7 %collective-permute-done.1 = f32[2,2048]{1,0:T(2,128)S(1)} collective-permute-done((f32[2,2048]{1,0:T(2,128)S(1)}, f32[2,2048]{1,0:T(2,128)S(1)}, u32[]{:S(2)}, u32[]{:S(2)}) %collective-permute-start.1) | collective-permute-done | bytes 16416 | tf_op jit(solution)/shard_map/ppermute | solution.py:225
  27.0 0.2 multiply_reduce_fusion.22
  27.2 0.2 multiply_reduce_fusion.21
  27.4 0.2 fusion.45
  27.7 1.5 %multiply_reduce_fusion.4 = f32[2,512]{1,0:T(2,128)S(1)} fusion(f32[2,512]{1,0:T(2,128)S(1)} %get-tuple-element.95, f32[512,512]{1,0:T(8,128)} %copy-done.2), kind=kLoop, calls=%fused_computation.4 | loop fusion | flops 1047552 | bytes 1056768 | tf_op jit(solution)/shard_map/reduce_sum | solution.py:232
  29.2 0.4 %multiply_reduce_fusion.3 = (f32[2,512]{1,0:T(2,128)S(1)}, f32[2,512]{1,0:T(2,128)S(1)}) fusion(f32[2,512]{1,0:T(2,128)S(1)} %get-tuple-element.93, f32[512,512]{1,0:T(8,128)S(1)} %copy-done.1, f32[512,512]{1,0:T(8,128)S(1)} %get-tuple-element.111), kind=kLoop, calls=%fused_computation.3 | loop fusion | flops 2095104 | bytes 2109440 | tf_op jit(solution)/shard_map/reduce_sum | solution.py:232
  29.6 0.4 %multiply_reduce_fusion.1 = (f32[2,512]{1,0:T(2,128)S(1)}, f32[2,512]{1,0:T(2,128)S(1)}) fusion(f32[2,512]{1,0:T(2,128)S(1)} %get-tuple-element.94, f32[512,512]{1,0:T(8,128)S(1)} %get-tuple-element.104, f32[512,512]{1,0:T(8,128)S(1)} %get-tuple-element.103), kind=kLoop, calls=%fused_computation.1 | loop fusion | flops 2095104 | bytes 2109440 | tf_op jit(solution)/shard_map/reduce_sum | solution.py:232
  30.4 0.2 collective-permute-start.2
  30.6 1.3 %fusion.11 = (f32[64]{0:T(128)S(1)}, f32[64]{0:T(128)S(1)}, f32[64]{0:T(128)S(1)}, f32[64]{0:T(128)S(1)}, f32[64]{0:T(128)S(1)}, /*index=5*/f32[64]{0:T(128)S(1)...) fusion(f32[2048]{0:T(1024)S(1)} %bitcast.67, ...), kind=kLoop, calls=%fused_computation.56 | loop fusion | flops 6683904 | bytes 69888 | tf_op jit(solution)/shard_map/reduce_sum | solution.py:137
  32.4 0.6 %reshape_multiply_fusion = f32[3,1,1,64]{3,2,1,0:T(1,128)} fusion(f32[3,64]{1,0:T(4,128)S(1)} %fusion.40, f32[64]{0:T(128)S(1)} %fusion.43), kind=kLoop, calls=%fused_computation.161 | loop fusion | flops 192 | bytes 1792 | tf_op jit(solution)/shard_map/mul | solution.py:274
  (63 shorter events, 2.1 us)
Async XLA Ops:
  2.3 14.6 %all-to-all-start = ((f32[32,1,384]{2,1,0:T(1,128)}), f32[32,1,384]{2,1,0:T(1,128)S(1)}, u32[]{:S(2)}, u32[]{:S(2)}) async-start(f32[32,1,384]{2,1,0:T(1,128)} %shard_map.77), calls=%async_computation | async-start | bytes 98304 | tf_op jit(solution)/shard_map/all_to_all | solution.py:155
  20.6 3.5 %copy-start = (f32[512,512]{1,0:T(8,128)}, f32[512,512]{1,0:T(8,128)S(1)}, u32[]{:S(2)}) copy-start(f32[512,512]{1,0:T(8,128)S(1)} %get-tuple-element.112) | copy-start | bytes 3145732
  20.6 3.5 %copy-start.2 = (f32[512,512]{1,0:T(8,128)}, f32[512,512]{1,0:T(8,128)S(1)}, u32[]{:S(2)}) copy-start(f32[512,512]{1,0:T(8,128)S(1)} %get-tuple-element.110) | copy-start | bytes 3145732
  22.4 1.2 %collective-permute-start = (f32[2,2048]{1,0:T(2,128)S(1)}, f32[2,2048]{1,0:T(2,128)S(1)}, u32[]{:S(2)}, u32[]{:S(2)}) collective-permute-start(f32[2,2048]{1,0:T(2,128)S(1)} %constant_dynamic-update-slice_fusion.8), channel_id=1, source_target_pairs={{0,1},{1,0},{2,3},{3,2},{4,5},{5,4},{6,7},{7,6},{8,9},{9,8},{10,11... | collective-permute-start | bytes 49160 | tf_op jit(solution)/shard_map/ppermute | solution.py:225
  25.8 1.2 %collective-permute-start.1 = (f32[2,2048]{1,0:T(2,128)S(1)}, f32[2,2048]{1,0:T(2,128)S(1)}, u32[]{:S(2)}, u32[]{:S(2)}) collective-permute-start(f32[2,2048]{1,0:T(2,128)S(1)} %constant_dynamic-update-slice_fusion), channel_id=1, source_target_pairs={{0,1},{1,0},{2,3},{3,2},{4,5},{5,4},{6,7},{7,6},{8,9},{9,8},{10,11... | collective-permute-start | bytes 49160 | tf_op jit(solution)/shard_map/ppermute | solution.py:225
  26.3 2.9 %copy-start.1 = (f32[512,512]{1,0:T(8,128)S(1)}, f32[512,512]{1,0:T(8,128)}, u32[]{:S(2)}) copy-start(f32[512,512]{1,0:T(8,128)} %copy-done) | copy-start | bytes 3145732
  30.4 1.6 %collective-permute-start.2 = (f32[2]{0:T(128)S(1)}, f32[2]{0:T(128)S(1)}, u32[]{:S(2)}, u32[]{:S(2)}) collective-permute-start(f32[2]{0:T(128)S(1)} %multiply_add_fusion.2), channel_id=1, source_target_pairs={{0,1},{1,0},{2,3},{3,2},{4,5},{5,4},{6,7},{7,6},{8,9},{9,8},{10,11... | collective-permute-start | bytes 32 | tf_op jit(solution)/shard_map/ppermute | solution.py:234
  32.3 0.7 %copy-start.3 = (f32[64]{0:T(128)}, f32[64]{0:T(128)S(1)}, u32[]{:S(2)}) copy-start(f32[64]{0:T(128)S(1)} %fusion.43) | copy-start | bytes 772

commit v17 on v15

--- a/solution.py
+++ b/solution.py
@@ -113,12 +113,10 @@
     )
 
 
-def pulling_fields(row_geometry, col_geometry, self_pair, vectors):
-    separations = []
+def pulling_slope(row_geometry, col_geometry, self_pair):
     squared = jnp.zeros(self_pair.shape, row_geometry.dtype)
     for axis_id in range(3):
         separation = row_geometry[axis_id][:, None] - col_geometry[axis_id][None, :]
-        separations.append(separation)
         squared = squared + separation * separation
     squared = jnp.where(self_pair, 1.0, squared)
     inverse = lax.rsqrt(squared)
@@ -131,7 +129,11 @@
         * inverse
         * inverse
     )
-    slope = jnp.where(self_pair, 0.0, slope)
+    return jnp.where(self_pair, 0.0, slope)
+
+
+def pulling_fields(row_geometry, col_geometry, slope, vectors):
+    separations = [row_geometry[axis_id][:, None] - col_geometry[axis_id][None, :] for axis_id in range(3)]
     return jnp.stack(
         [jnp.stack([jnp.sum(slope * vector[None, :] * separation, 1) for separation in separations]) for vector in vectors]
     )
@@ -240,6 +242,8 @@
             def curvature(vectors):
                 return jnp.sum(vectors * operate(vectors), 1)
 
+        own_index = me * per_brick + jnp.arange(per_brick, dtype=jnp.int32)
+        slope = lax.optimization_barrier(pulling_slope(own, geometry, own_index[:, None] == col_index[None, :]))
         rhs = jnp.stack([-geometry[4], jnp.ones((atoms,), jnp.float32)])
         solution = jnp.zeros_like(rhs)
         resid = rhs
@@ -255,8 +259,7 @@
             direction = resid + (norm_next / norm_now)[:, None] * direction
             norm_now = norm_next
         fields = pulling_fields(
-            own, geometry, own_index[:, None] == col_index[None, :],
-            [solution[0], solution[1], direction[0], direction[1]],
+            own, geometry, slope, [solution[0], solution[1], direction[0], direction[1]]
         ).reshape(2, 2, 3, per_brick)
         own_solution = lax.dynamic_slice_in_dim(solution, me * per_brick, per_brick, 1)
         own_direction = lax.dynamic_slice_in_dim(direction, me * per_brick, per_brick, 1)

time: 33.2 us -> 34.1 us (1.027)
  local copies, waits for them, and re-layouts: 0.99 us -> 2.05 us
  waiting for transfers between devices: 9.02 us -> 8.39 us
  other arithmetic: 12.4 us -> 12.9 us
    reduce_sum x3, other arithmetic: 3.01 us -> 4.52 us  [partial_image(): backward = jnp.sum(matrix[None, :, :] * row_part[:, :, None], 1)]
    reduce_sum x3, other arithmetic: 2.25 us -> 1.02 us  [curvature(): jnp.sum(matrix[None, :, :] * col_part[:, None, :], 2)]
    unnamed x8 -> x10, local copies, waits for them, and re-layouts: 0.02 us -> 1.07 us
    ppermute x2, waiting for transfers between devices: 1.73 us -> 1.03 us  [operate(): return partial + lax.ppermute(partial, everyone, partner)]
    select_n x0 -> x1, other arithmetic: none -> 0.68 us  [pulling_slope(): return jnp.where(self_pair, 0.0, slope)]
    reduce_sum x1, other arithmetic: 1.33 us -> 0.81 us  [pulling_fields(): jnp.sum(slope * vector[None, :] * separation, 1)]
  transfers between devices with their start and end apart: 4 -> 4, of which waited for: 3 -> 4; matrix products, arithmetic and copies ran while one was open for 5% -> 6% of each run, Pallas kernels for 0% -> 0%
where the time goes in v17:
time: 34.1 us; the launch traced here: 33.8 us
  other arithmetic  12.9 us (38%)
  waiting for transfers between devices  8.39 us (25%)
  starting transfers between devices  7.94 us (23%)
  local copies, waits for them, and re-layouts  2.05 us (6%)
  Pallas kernels  1.61 us (5%)
  between operations  0.94 us (3%)
    all_to_all x1, starting transfers between devices, shards(): got = lax.all_to_all(payload, everyone, 0, 0, tiled=True)  7.3 us
    all_to_all x1, waiting for transfers between devices, shards(): got = lax.all_to_all(payload, everyone, 0, 0, tiled=True)  7.3 us
    reduce_sum x3, other arithmetic, partial_image(): backward = jnp.sum(matrix[None, :, :] * row_part[:, :, None], 1)  4.52 us
    select_n x1, other arithmetic, screened(): return jnp.where(self_pair, row_geometry[5][:, None], off)  1.79 us
    pallas_call x1, Pallas kernels, prep(): pl.pallas_call(prep_kernel, in_specs=[pl.BlockSpec(memory_space=smem), pl...  1.61 us
    mul x1, other arithmetic, screened(): off = lax.erf(screening * squared * inverse) * inverse  1.13 us
    unnamed x10, local copies, waits for them, and re-layouts  1.07 us
    ppermute x2, waiting for transfers between devices, operate(): return partial + lax.ppermute(partial, everyone, partner)  1.03 us
  transfers between devices with their start and end apart: 4, of which 4 were waited for; matrix products, arithmetic and copies ran while one was open for 6% of the time, Pallas kernels for 0%

profile of v17, /device:TPU:0, one launch (start us, length us, event | category | flops | bytes accessed | tf_op | source)
XLA Modules:
  0.0 33.8 jit_solution(9334281026884970979)
XLA Ops:
  0.6 1.6 %shard_map.77 = f32[32,1,384]{2,1,0:T(1,128)} custom-call(f32[4]{0:T(128)} %hard_ref.1, f32[4]{0:T(128)} %width_ref.1, f32[3,1,64]{2,1,0:T(1,128)} %bitcast.103, s32[1,64]{1,0:T(1,128)} %bitcast.104, f32[64,128]{1,0:T(8,128)} %bitcast.67, f32[4,128]{1,0:T(4,128)} %readout_ref.1), custom_call_target="tpu_custom_call" | custom-call | tf_op jit(solution)/shard_map/pallas_call | solution.py:94
  2.2 7.3 %all-to-all-start = ((f32[32,1,384]{2,1,0:T(1,128)}), f32[32,1,384]{2,1,0:T(1,128)S(1)}, u32[]{:S(2)}, u32[]{:S(2)}) async-start(f32[32,1,384]{2,1,0:T(1,128)} %shard_map.77), calls=%async_computation | async-start | bytes 98304 | tf_op jit(solution)/shard_map/all_to_all | solution.py:156
  9.6 7.3 %all-to-all-done = f32[32,1,384]{2,1,0:T(1,128)S(1)} async-done(((f32[32,1,384]{2,1,0:T(1,128)}), f32[32,1,384]{2,1,0:T(1,128)S(1)}, u32[]{:S(2)}, u32[]{:S(2)}) %all-to-all-start) | async-done | bytes 49184 | tf_op jit(solution)/shard_map/all_to_all | solution.py:156
  17.1 0.2 slice_reduce_fusion.3
  17.7 1.1 %erf_multiply_fusion = (f32[512,512]{1,0:T(8,128)S(1)}, f32[512,512]{1,0:T(8,128)S(1)}) fusion(f32[512]{0:T(512)S(1)} %bitcast.82, f32[512]{0:T(512)S(1)} %bitcast.83, f32[512]{0:T(512)S(1)} %bitcast.84, f32[512]{0:T(512)S(1)} %bitcast.78, f32[512]{0:T(512)S(1)} %bitcast.88, f32[512]{0:T(512)S(1)} %bitcast.79, f32[512]{0:T(512)S(1)} %bitcast.80, ...), kind=kLoop, calls=%fused_computation.36 | loop fusion | flops 6291456 | bytes 2121728 | tf_op jit(solution)/shard_map/mul | solution.py:31
  18.8 1.8 %fusion.1 = (f32[512,512]{1,0:T(8,128)S(1)}, f32[512,512]{1,0:T(8,128)S(1)}, f32[512,512]{1,0:T(8,128)S(1)}) fusion(f32[512]{0:T(512)S(1)} %bitcast.77, f32[512]{0:T(512)S(1)} %bitcast.72, f32[512]{0:T(512)S(1)} %bitcast.73, f32[512]{0:T(512)S(1)} %bitcast.74, f32[512]{0:T(512)S(1)} %bitcast.75, f32[512]{0:T(512)S(1)} %bitcast.76, f32[512]{0:T(512)S(1)} %bitcast.68, ...), kind=kLoop, calls=%fused_computation.42 | loop fusion | flops 10747904 | bytes 3166208 | tf_op jit(solution)/shard_map/jit(_where)/select_n | solution.py:34
  20.7 1.5 %multiply_reduce_fusion.13 = (f32[2,512]{1,0:T(2,128)S(1)}, f32[2,512]{1,0:T(2,128)S(1)}, f32[2,512]{1,0:T(2,128)S(1)}, f32[2,512]{1,0:T(2,128)S(1)}, f32[2,512]...) fusion(f32[2,512]{1,0:T(2,128)S(1)} %get-tuple-element.108, ...), kind=kLoop, calls=%fused_computation.13 | loop fusion | flops 8380416 | bytes 5296128 | tf_op jit(solution)/shard_map/reduce_sum | solution.py:218
  22.9 0.7 %collective-permute-done = f32[2,2048]{1,0:T(2,128)S(1)} collective-permute-done((f32[2,2048]{1,0:T(2,128)S(1)}, f32[2,2048]{1,0:T(2,128)S(1)}, u32[]{:S(2)}, u32[]{:S(2)}) %collective-permute-start) | collective-permute-done | bytes 16416 | tf_op jit(solution)/shard_map/ppermute | solution.py:226
  23.8 0.2 multiply_reduce_fusion.23
  24.1 2.3 %multiply_reduce_fusion.9 = (f32[2,512]{1,0:T(2,128)S(1)}, f32[2,512]{1,0:T(2,128)S(1)}, f32[2,512]{1,0:T(2,128)S(1)}, f32[2,512]{1,0:T(2,128)S(1)}) fusion(f32[2,512]{1,0:T(2,128)S(1)} %get-tuple-element.105, f32[512,512]{1,0:T(8,128)S(1)} %get-tuple-element.114, f32[2,512]{1,0:T(2,128)S(1)} %get-tuple-element.104, f32[512,512]{1,0:T(8,128)} %copy-done, ...), kind=kLoop, calls=%fused_computation.9 | loop fusion | flops 4190208 | bytes 3170304 | tf_op jit(solution)/shard_map/reduce_sum | solution.py:218
  26.5 0.7 %multiply_reduce_fusion.5 = (f32[2,512]{1,0:T(2,128)S(1)}, f32[2,512]{1,0:T(2,128)S(1)}, f32[2,512]{1,0:T(2,128)S(1)}, f32[2,512]{1,0:T(2,128)S(1)}) fusion(f32[2,512]{1,0:T(2,128)S(1)} %get-tuple-element.101, f32[512,512]{1,0:T(8,128)S(1)} %get-tuple-element.106, f32[2,512]{1,0:T(2,128)S(1)} %get-tuple-element.103, f32[2,512]{1,0:T(2,128)S(1)} %get-tuple-element.102, ...), kind=kLoop, calls=%fused_computation.5 | loop fusion | flops 4190208 | bytes 2125824 | tf_op jit(solution)/shard_map/reduce_sum | solution.py:218
  27.3 0.2 collective-permute-start.1
  27.5 0.7 %fusion.21 = f32[64,2048]{1,0:T(8,128)S(1)} fusion(f32[2048]{0:T(1024)S(1)} %sub.353, f32[64]{0:T(128)S(1)} %get-tuple-element.117, f32[2048]{0:T(1024)S(1)} %sub.348, f32[64]{0:T(128)S(1)} %get-tuple-element.118, f32[2048]{0:T(1024)S(1)} %sub.343, f32[64]{0:T(128)S(1)} %get-tuple-element.119, f32[2048]{0:T(1024)S(1)} %add.362, ...), kind=kLoop, calls=%fused_computation.66 | loop fusion | flops 3014656 | bytes 558336 | tf_op jit(solution)/shard_map/jit(_where)/select_n | solution.py:132
  28.2 0.3 collective-permute-done.1
  28.7 0.2 multiply_reduce_fusion.21
  29.0 0.2 fusion.45
  29.2 0.4 %multiply_reduce_fusion.1 = (f32[2,512]{1,0:T(2,128)S(1)}, f32[2,512]{1,0:T(2,128)S(1)}) fusion(f32[2,512]{1,0:T(2,128)S(1)} %get-tuple-element.97, f32[512,512]{1,0:T(8,128)S(1)} %get-tuple-element.107, f32[512,512]{1,0:T(8,128)S(1)} %get-tuple-element.106), kind=kLoop, calls=%fused_computation.1 | loop fusion | flops 2095104 | bytes 2109440 | tf_op jit(solution)/shard_map/reduce_sum | solution.py:233
  29.6 0.8 %copy-done.3 = f32[512,512]{1,0:T(8,128)S(1)} copy-done((f32[512,512]{1,0:T(8,128)S(1)}, f32[512,512]{1,0:T(8,128)}, u32[]{:S(2)}) %copy-start.3) | copy-done | bytes 1048600
  30.4 0.2 multiply_reduce_fusion.4
  30.7 0.2 copy-done.1
  30.9 0.4 %multiply_reduce_fusion.3 = (f32[2,512]{1,0:T(2,128)S(1)}, f32[2,512]{1,0:T(2,128)S(1)}) fusion(f32[2,512]{1,0:T(2,128)S(1)} %get-tuple-element.96, f32[512,512]{1,0:T(8,128)S(1)} %copy-done.1, f32[512,512]{1,0:T(8,128)S(1)} %get-tuple-element.114), kind=kLoop, calls=%fused_computation.3 | loop fusion | flops 2095104 | bytes 2109440 | tf_op jit(solution)/shard_map/reduce_sum | solution.py:233
  31.8 0.2 collective-permute-start.2
  32.0 0.8 %fusion.19 = (f32[64]{0:T(128)S(1)}, f32[64]{0:T(128)S(1)}, f32[64]{0:T(128)S(1)}, f32[64]{0:T(128)S(1)}, f32[64]{0:T(128)S(1)}, /*index=5*/f32[64]{0:T(128)S(1)...) fusion(f32[64,2048]{1,0:T(8,128)S(1)} %fusion.21, ...), kind=kLoop, calls=%fused_computation.64 | loop fusion | flops 4062464 | bytes 585472 | tf_op jit(solution)/shard_map/reduce_sum | solution.py:138
  33.2 0.6 %reshape_multiply_fusion = f32[3,1,1,64]{3,2,1,0:T(1,128)} fusion(f32[3,64]{1,0:T(4,128)S(1)} %fusion.40, f32[64]{0:T(128)S(1)} %fusion.43), kind=kLoop, calls=%fused_computation.161 | loop fusion | flops 192 | bytes 1792 | tf_op jit(solution)/shard_map/mul | solution.py:276
  (66 shorter events, 2.7 us)
Async XLA Ops:
  2.2 14.6 %all-to-all-start = ((f32[32,1,384]{2,1,0:T(1,128)}), f32[32,1,384]{2,1,0:T(1,128)S(1)}, u32[]{:S(2)}, u32[]{:S(2)}) async-start(f32[32,1,384]{2,1,0:T(1,128)} %shard_map.77), calls=%async_computation | async-start | bytes 98304 | tf_op jit(solution)/shard_map/all_to_all | solution.py:156
  20.6 1.6 %copy-start = (f32[512,512]{1,0:T(8,128)}, f32[512,512]{1,0:T(8,128)S(1)}, u32[]{:S(2)}) copy-start(f32[512,512]{1,0:T(8,128)S(1)} %get-tuple-element.115) | copy-start | bytes 3145732
  20.6 1.6 %copy-start.2 = (f32[512,512]{1,0:T(8,128)}, f32[512,512]{1,0:T(8,128)S(1)}, u32[]{:S(2)}) copy-start(f32[512,512]{1,0:T(8,128)S(1)} %get-tuple-element.113) | copy-start | bytes 3145732
  22.4 1.2 %collective-permute-start = (f32[2,2048]{1,0:T(2,128)S(1)}, f32[2,2048]{1,0:T(2,128)S(1)}, u32[]{:S(2)}, u32[]{:S(2)}) collective-permute-start(f32[2,2048]{1,0:T(2,128)S(1)} %constant_dynamic-update-slice_fusion.8), channel_id=1, source_target_pairs={{0,1},{1,0},{2,3},{3,2},{4,5},{5,4},{6,7},{7,6},{8,9},{9,8},{10,11... | collective-permute-start | bytes 49160 | tf_op jit(solution)/shard_map/ppermute | solution.py:226
  27.3 1.2 %collective-permute-start.1 = (f32[2,2048]{1,0:T(2,128)S(1)}, f32[2,2048]{1,0:T(2,128)S(1)}, u32[]{:S(2)}, u32[]{:S(2)}) collective-permute-start(f32[2,2048]{1,0:T(2,128)S(1)} %constant_dynamic-update-slice_fusion), channel_id=1, source_target_pairs={{0,1},{1,0},{2,3},{3,2},{4,5},{5,4},{6,7},{7,6},{8,9},{9,8},{10,11... | collective-permute-start | bytes 49160 | tf_op jit(solution)/shard_map/ppermute | solution.py:226
  29.2 1.2 %copy-start.3 = (f32[512,512]{1,0:T(8,128)S(1)}, f32[512,512]{1,0:T(8,128)}, u32[]{:S(2)}) copy-start(f32[512,512]{1,0:T(8,128)} %copy-done.2) | copy-start | bytes 3145732
  29.6 1.3 %copy-start.1 = (f32[512,512]{1,0:T(8,128)S(1)}, f32[512,512]{1,0:T(8,128)}, u32[]{:S(2)}) copy-start(f32[512,512]{1,0:T(8,128)} %copy-done) | copy-start | bytes 3145732
  31.8 1.2 %collective-permute-start.2 = (f32[2]{0:T(128)S(1)}, f32[2]{0:T(128)S(1)}, u32[]{:S(2)}, u32[]{:S(2)}) collective-permute-start(f32[2]{0:T(128)S(1)} %multiply_add_fusion.2), channel_id=1, source_target_pairs={{0,1},{1,0},{2,3},{3,2},{4,5},{5,4},{6,7},{7,6},{8,9},{9,8},{10,11... | collective-permute-start | bytes 32 | tf_op jit(solution)/shard_map/ppermute | solution.py:235
  33.1 0.7 %copy-start.4 = (f32[64]{0:T(128)}, f32[64]{0:T(128)S(1)}, u32[]{:S(2)}) copy-start(f32[64]{0:T(128)S(1)} %fusion.43) | copy-start | bytes 772

commit v18 on v15

--- a/solution.py
+++ b/solution.py
@@ -184,38 +184,46 @@
             def assemble(mine):
                 return gather_all(mine.reshape(2, per_brick))
 
-        if pair and atoms % 4 == 0:
+        if pair and atoms % 8 == 0:
             group = atoms // 4
+            half = group // 2
+            specs = []
+            for (row_a, col_a), (row_b, col_b) in zip(BLOCKS[0][:2], BLOCKS[1][:2]):
+                for low, high in ((0, 0), (1, 1), (0, 1)):
+                    specs.append((row_a * group + low * half, row_b * group + low * half,
+                                  col_a * group + high * half, col_b * group + high * half, half, low == high))
+            for (row_a, col_a), (row_b, col_b) in zip(BLOCKS[0][2:], BLOCKS[1][2:]):
+                specs.append((row_a * group, row_b * group, col_a * group, col_b * group, group, False))
             starts = []
             matrices = []
-            for k, ((row_a, col_a), (row_b, col_b)) in enumerate(zip(BLOCKS[0], BLOCKS[1])):
-                row_at = jnp.where(parity == 0, row_a, row_b) * group
-                col_at = jnp.where(parity == 0, col_a, col_b) * group
-                starts.append((row_at, col_at))
-                offsets = jnp.arange(group, dtype=jnp.int32)
+            for row_a, row_b, col_a, col_b, size, diagonal in specs:
+                row_at = jnp.where(parity == 0, row_a, row_b)
+                col_at = jnp.where(parity == 0, col_a, col_b)
+                starts.append((row_at, col_at, size, diagonal))
+                offsets = jnp.arange(size, dtype=jnp.int32)
                 matrices.append(
                     lax.optimization_barrier(
                         screened(
-                            lax.dynamic_slice_in_dim(geometry, row_at, group, 1),
-                            lax.dynamic_slice_in_dim(geometry, col_at, group, 1),
-                            offsets[:, None] == offsets[None, :] if k < 2 else None,
+                            lax.dynamic_slice_in_dim(geometry, row_at, size, 1),
+                            lax.dynamic_slice_in_dim(geometry, col_at, size, 1),
+                            offsets[:, None] == offsets[None, :] if diagonal else None,
                         )
                     )
                 )
 
             def partial_image(vectors):
                 partial = jnp.zeros_like(vectors)
-                for k, (matrix, (row_at, col_at)) in enumerate(zip(matrices, starts)):
-                    col_part = lax.dynamic_slice_in_dim(vectors, col_at, group, 1)
+                for matrix, (row_at, col_at, size, diagonal) in zip(matrices, starts):
+                    col_part = lax.dynamic_slice_in_dim(vectors, col_at, size, 1)
                     forward = jnp.sum(matrix[None, :, :] * col_part[:, None, :], 2)
                     partial = lax.dynamic_update_slice_in_dim(
-                        partial, lax.dynamic_slice_in_dim(partial, row_at, group, 1) + forward, row_at, 1
+                        partial, lax.dynamic_slice_in_dim(partial, row_at, size, 1) + forward, row_at, 1
                     )
-                    if k >= 2:
-                        row_part = lax.dynamic_slice_in_dim(vectors, row_at, group, 1)
+                    if not diagonal:
+                        row_part = lax.dynamic_slice_in_dim(vectors, row_at, size, 1)
                         backward = jnp.sum(matrix[None, :, :] * row_part[:, :, None], 1)
                         partial = lax.dynamic_update_slice_in_dim(
-                            partial, lax.dynamic_slice_in_dim(partial, col_at, group, 1) + backward, col_at, 1
+                            partial, lax.dynamic_slice_in_dim(partial, col_at, size, 1) + backward, col_at, 1
                         )
                 return partial
 
@@ -225,11 +233,11 @@
 
             def curvature(vectors):
                 mine = 0.0
-                for k, (matrix, (row_at, col_at)) in enumerate(zip(matrices, starts)):
-                    col_part = lax.dynamic_slice_in_dim(vectors, col_at, group, 1)
-                    row_part = lax.dynamic_slice_in_dim(vectors, row_at, group, 1)
+                for matrix, (row_at, col_at, size, diagonal) in zip(matrices, starts):
+                    col_part = lax.dynamic_slice_in_dim(vectors, col_at, size, 1)
+                    row_part = lax.dynamic_slice_in_dim(vectors, row_at, size, 1)
                     term = jnp.sum(row_part * jnp.sum(matrix[None, :, :] * col_part[:, None, :], 2), 1)
-                    mine = mine + (term if k < 2 else 2.0 * term)
+                    mine = mine + (term if diagonal else 2.0 * term)
                 return mine + lax.ppermute(mine, everyone, partner)
         else:
             matrix = screened(row_geometry, geometry, row_index[:, None] == col_index[None, :])

time: 33.2 us -> 38.5 us (1.16)
  other arithmetic: 12.4 us -> 17.4 us
  local copies, waits for them, and re-layouts: 0.99 us -> 2.14 us
  waiting for transfers between devices: 9.02 us -> 7.9 us
    reduce_sum x3 -> x6, other arithmetic: 2.25 us -> 4.22 us  [curvature(): jnp.sum(matrix[None, :, :] * col_part[:, None, :], 2)]
    reduce_sum x3 -> x6, other arithmetic: 3.01 us -> 3.85 us  [partial_image(): backward = jnp.sum(matrix[None, :, :] * row_part[:, :, None], 1)]
    select_n x1 -> x2, other arithmetic: 1.79 us -> 1.01 us  [screened(): return jnp.where(self_pair, row_geometry[5][:, None], off)]
    div x2, other arithmetic: 0.01 us -> 0.67 us  [shards(): direction = resid + (norm_next / norm_now)[:, None] * direction]
    div x2, other arithmetic: 0.01 us -> 0.67 us  [shards(): step_size = norm_now / jnp.sum(direction * image, 1)]
    mul x1 -> x2, other arithmetic: 1.13 us -> 1.73 us  [screened(): off = lax.erf(screening * squared * inverse) * inverse]
    ppermute x2, waiting for transfers between devices: 1.73 us -> 1.14 us  [operate(): return partial + lax.ppermute(partial, everyone, partner)]
    add x2, local copies, waits for them, and re-layouts: 0.07 us -> 0.66 us  [pulling_fields(): screening = lax.rsqrt(row_geometry[3][:, None] + col_geometry[3][None, :])]
  transfers between devices with their start and end apart: 4 -> 4, of which waited for: 3 -> 3; matrix products, arithmetic and copies ran while one was open for 5% -> 8% of each run, Pallas kernels for 0% -> 0%
where the time goes in v18:
time: 38.5 us; the launch traced here: 38.2 us
  other arithmetic  17.4 us (45%)
  starting transfers between devices  7.98 us (21%)
  waiting for transfers between devices  7.9 us (21%)
  local copies, waits for them, and re-layouts  2.14 us (6%)
  Pallas kernels  1.61 us (4%)
  between operations  1.14 us (3%)
    all_to_all x1, starting transfers between devices, shards(): got = lax.all_to_all(payload, everyone, 0, 0, tiled=True)  7.3 us
    all_to_all x1, waiting for transfers between devices, shards(): got = lax.all_to_all(payload, everyone, 0, 0, tiled=True)  6.76 us
    reduce_sum x6, other arithmetic, curvature(): jnp.sum(matrix[None, :, :] * col_part[:, None, :], 2)  4.22 us
    reduce_sum x6, other arithmetic, partial_image(): backward = jnp.sum(matrix[None, :, :] * row_part[:, :, None], 1)  3.85 us
    mul x2, other arithmetic, screened(): off = lax.erf(screening * squared * inverse) * inverse  1.73 us
    pallas_call x1, Pallas kernels, prep(): pl.pallas_call(prep_kernel, in_specs=[pl.BlockSpec(memory_space=smem), pl...  1.61 us
    reduce_sum x1, other arithmetic, pulling_fields(): jnp.sum(slope * vector[None, :] * separation, 1)  1.32 us
    ppermute x2, waiting for transfers between devices, operate(): return partial + lax.ppermute(partial, everyone, partner)  1.14 us
  transfers between devices with their start and end apart: 4, of which 3 were waited for; matrix products, arithmetic and copies ran while one was open for 8% of the time, Pallas kernels for 0%

profile of v18, /device:TPU:0, one launch (start us, length us, event | category | flops | bytes accessed | tf_op | source)
XLA Modules:
  0.0 38.2 jit_solution(6794843833277743098)
XLA Ops:
  0.6 1.6 %shard_map.77 = f32[32,1,384]{2,1,0:T(1,128)} custom-call(f32[4]{0:T(128)} %hard_ref.1, f32[4]{0:T(128)} %width_ref.1, f32[3,1,64]{2,1,0:T(1,128)} %bitcast.107, s32[1,64]{1,0:T(1,128)} %bitcast.128, f32[64,128]{1,0:T(8,128)} %bitcast.81, f32[4,128]{1,0:T(4,128)} %readout_ref.1), custom_call_target="tpu_custom_call" | custom-call | tf_op jit(solution)/shard_map/pallas_call | solution.py:94
  2.2 7.3 %all-to-all-start = ((f32[32,1,384]{2,1,0:T(1,128)}), f32[32,1,384]{2,1,0:T(1,128)S(1)}, u32[]{:S(2)}, u32[]{:S(2)}) async-start(f32[32,1,384]{2,1,0:T(1,128)} %shard_map.77), calls=%async_computation | async-start | bytes 98304 | tf_op jit(solution)/shard_map/all_to_all | solution.py:154
  9.6 0.5 %iota_add_fusion = s32[64]{0:T(128)} fusion(s32[]{:T(128)S(6)} %mul.1036), kind=kLoop, calls=%fused_computation.249 | loop fusion | flops 64 | bytes 260 | tf_op jit(solution)/shard_map/add | solution.py:256
  10.1 6.8 %all-to-all-done = f32[32,1,384]{2,1,0:T(1,128)S(1)} async-done(((f32[32,1,384]{2,1,0:T(1,128)}), f32[32,1,384]{2,1,0:T(1,128)S(1)}, u32[]{:S(2)}, u32[]{:S(2)}) %all-to-all-start) | async-done | bytes 49184 | tf_op jit(solution)/shard_map/all_to_all | solution.py:154
  17.8 0.5 %fusion.21 = (f32[256,256]{1,0:T(8,128)S(1)}, f32[256,256]{1,0:T(8,128)S(1)}, f32[256,256]{1,0:T(8,128)S(1)}) fusion(f32[256]{0:T(256)S(1)} %bitcast.127, f32[256]{0:T(256)S(1)} %bitcast.123, f32[256]{0:T(256)S(1)} %bitcast.124, f32[256]{0:T(256)S(1)} %bitcast.125, f32[256]{0:T(256)S(1)} %bitcast.118, f32[256]{0:T(256)S(1)} %bitcast.126, ...), kind=kLoop, calls=%fused_computation.86 | loop fusion | flops 2686976 | bytes 796672 | tf_op jit(solution)/shard_map/jit(_where)/select_n | solution.py:34
  18.4 0.5 %fusion.23 = (f32[256,256]{1,0:T(8,128)S(1)}, f32[256,256]{1,0:T(8,128)S(1)}, f32[256,256]{1,0:T(8,128)S(1)}) fusion(f32[256]{0:T(256)S(1)} %bitcast.117, f32[256]{0:T(256)S(1)} %bitcast.112, f32[256]{0:T(256)S(1)} %bitcast.113, f32[256]{0:T(256)S(1)} %bitcast.114, f32[256]{0:T(256)S(1)} %bitcast.115, f32[256]{0:T(256)S(1)} %bitcast.116, ...), kind=kLoop, calls=%fused_computation.88 | loop fusion | flops 2686976 | bytes 796672 | tf_op jit(solution)/shard_map/jit(_where)/select_n | solution.py:34
  18.9 0.6 %erf_multiply_fusion.2 = f32[512,512]{1,0:T(8,128)S(1)} fusion(f32[512]{0:T(512)S(1)} %bitcast.104, f32[512]{0:T(512)S(1)} %bitcast.105, f32[512]{0:T(512)S(1)} %bitcast.98, f32[512]{0:T(512)S(1)} %bitcast.99, f32[512]{0:T(512)S(1)} %bitcast.100, f32[512]{0:T(512)S(1)} %bitcast.101, f32[512]{0:T(512)S(1)} %bitcast.102, f32[512]{0:T(512)S(1)} %bitcast.103), kind=kLoop, calls=%fused_computation.32 | loop fusion | flops 3145728 | bytes 1064960 | tf_op jit(solution)/shard_map/mul | solution.py:31
  19.5 1.1 %erf_multiply_fusion = (f32[512,512]{1,0:T(8,128)S(1)}, f32[512,512]{1,0:T(8,128)S(1)}) fusion(f32[512]{0:T(512)S(1)} %bitcast.90, f32[512]{0:T(512)S(1)} %bitcast.91, f32[512]{0:T(512)S(1)} %bitcast.92, f32[512]{0:T(512)S(1)} %bitcast.86, f32[512]{0:T(512)S(1)} %bitcast.96, f32[512]{0:T(512)S(1)} %bitcast.87, f32[512]{0:T(512)S(1)} %bitcast.88, ...), kind=kLoop, calls=%fused_computation.30 | loop fusion | flops 6291456 | bytes 2121728 | tf_op jit(solution)/shard_map/mul | solution.py:31
  20.6 0.7 %multiply_reduce_fusion.29 = (f32[2,256]{1,0:T(2,128)S(1)}, f32[2,256]{1,0:T(2,128)S(1)}, f32[2,256]{1,0:T(2,128)S(1)}, f32[2,256]{1,0:T(2,128)S(1)}, f32[2,256]...) fusion(f32[2,256]{1,0:T(2,128)S(1)} %get-tuple-element.154, ...), kind=kLoop, calls=%fused_computation.71 | loop fusion | flops 2093056 | bytes 1597440 | tf_op jit(solution)/shard_map/reduce_sum | solution.py:224
  21.5 1.2 %multiply_reduce_fusion.9 = (f32[2,512]{1,0:T(2,128)S(1)}, f32[2,512]{1,0:T(2,128)S(1)}, f32[2,512]{1,0:T(2,128)S(1)}, f32[2,512]{1,0:T(2,128)S(1)}, f32[2,512]{1,0:T(2,128)S(1)}, /*index=5*/f32[2,512]{1,0:T(2,128)S(1)}) fusion(f32[2,512]{1,0:T(2,128)S(1)} %get-tuple-element.147, f32[512,512]{1,0:T(8,128)S(1)} %get-tuple-element.145, ...), kind=kLoop, calls=%fused_computation.9 | loop fusion | flops 6285312 | bytes 3190784 | tf_op jit(solution)/shard_map/reduce_sum | solution.py:224
  23.1 1.0 %collective-permute-done = f32[2,2048]{1,0:T(2,128)S(1)} collective-permute-done((f32[2,2048]{1,0:T(2,128)S(1)}, f32[2,2048]{1,0:T(2,128)S(1)}, u32[]{:S(2)}, u32[]{:S(2)}) %collective-permute-start) | collective-permute-done | bytes 16416 | tf_op jit(solution)/shard_map/ppermute | solution.py:232
  25.0 0.4 %multiply_reduce_fusion.21 = (f32[2,256]{1,0:T(2,128)S(1)}, f32[2,256]{1,0:T(2,128)S(1)}, f32[2,256]{1,0:T(2,128)S(1)}, f32[2,256]{1,0:T(2,128)S(1)}) fusion(f32[2,256]{1,0:T(2,128)S(1)} %get-tuple-element.142, f32[256,256]{1,0:T(8,128)S(1)} %get-tuple-element.165, f32[2,256]{1,0:T(2,128)S(1)} %get-tuple-element.141, f32[256,256]{1,0:T(8,128)S(1)} %get-tuple-element.166, ...), kind=kLoop, calls=%fused_computation.63 | loop fusion | flops 1046528 | bytes 798720 | tf_op jit(solution)/shard_map/reduce_sum | solution.py:224
  25.4 0.4 %multiply_reduce_fusion.25 = (f32[2,256]{1,0:T(2,128)S(1)}, f32[2,256]{1,0:T(2,128)S(1)}, f32[2,256]{1,0:T(2,128)S(1)}, f32[2,256]{1,0:T(2,128)S(1)}) fusion(f32[2,256]{1,0:T(2,128)S(1)} %get-tuple-element.144, f32[256,256]{1,0:T(8,128)S(1)} %get-tuple-element.168, f32[2,256]{1,0:T(2,128)S(1)} %get-tuple-element.143, f32[256,256]{1,0:T(8,128)S(1)} %get-tuple-element.169, ...), kind=kLoop, calls=%fused_computation.67 | loop fusion | flops 1046528 | bytes 798720 | tf_op jit(solution)/shard_map/reduce_sum | solution.py:224
  26.0 0.4 %multiply_reduce_fusion.7 = (f32[2,512]{1,0:T(2,128)S(1)}, f32[2,512]{1,0:T(2,128)S(1)}) fusion(f32[2,512]{1,0:T(2,128)S(1)} %get-tuple-element.139, f32[512,512]{1,0:T(8,128)S(1)} %erf_multiply_fusion.2, f32[2,512]{1,0:T(2,128)S(1)} %get-tuple-element.140), kind=kLoop, calls=%fused_computation.7 | loop fusion | flops 2095104 | bytes 1064960 | tf_op jit(solution)/shard_map/reduce_sum | solution.py:224
  26.5 0.7 %multiply_reduce_fusion.3 = (f32[2,512]{1,0:T(2,128)S(1)}, f32[2,512]{1,0:T(2,128)S(1)}, f32[2,512]{1,0:T(2,128)S(1)}, f32[2,512]{1,0:T(2,128)S(1)}) fusion(f32[2,512]{1,0:T(2,128)S(1)} %get-tuple-element.136, f32[512,512]{1,0:T(8,128)S(1)} %get-tuple-element.145, f32[2,512]{1,0:T(2,128)S(1)} %get-tuple-element.138, f32[2,512]{1,0:T(2,128)S(1)} %get-tuple-element.137, ...), kind=kLoop, calls=%fused_computation.3 | loop fusion | flops 4190208 | bytes 2125824 | tf_op jit(solution)/shard_map/reduce_sum | solution.py:224
  27.5 0.6 %slice_bitcast_fusion.3 = (f32[64]{0:T(128)}, f32[64]{0:T(128)}, f32[64]{0:T(128)}, f32[64]{0:T(128)}) fusion(f32[6,64]{1,0:T(8,128)S(1)} %constant_dynamic-slice_fusion.1), kind=kLoop, calls=%fused_computation.248 | loop fusion | bytes 2048 | tf_op jit(solution)/shard_map/add | solution.py:125
  28.7 0.7 %div.36 = f32[2]{0:T(128)S(1)} divide(f32[2]{0:T(128)} %copy-done.8, f32[2]{0:T(128)S(1)} %get-tuple-element.79) | non-fusion elementwise | flops 2 | bytes 24 | tf_op jit(solution)/shard_map/div | solution.py:259
  29.6 0.7 %div.37 = f32[2]{0:T(128)S(1)} divide(f32[2]{0:T(128)S(1)} %get-tuple-element.77, f32[2]{0:T(128)} %copy-done.8) | non-fusion elementwise | flops 2 | bytes 24 | tf_op jit(solution)/shard_map/div | solution.py:263
  30.5 1.1 %multiply_reduce_fusion.20 = f32[2,256]{1,0:T(2,128)S(1)} fusion(f32[2,256]{1,0:T(2,128)S(1)} %get-tuple-element.131, f32[256,256]{1,0:T(8,128)} %copy-done.6), kind=kLoop, calls=%fused_computation.62 | loop fusion | flops 261632 | bytes 266240 | tf_op jit(solution)/shard_map/reduce_sum | solution.py:239
  31.6 1.1 %multiply_reduce_fusion.17 = f32[2,256]{1,0:T(2,128)S(1)} fusion(f32[2,256]{1,0:T(2,128)S(1)} %get-tuple-element.130, f32[256,256]{1,0:T(8,128)} %copy-done.1), kind=kLoop, calls=%fused_computation.59 | loop fusion | flops 261632 | bytes 266240 | tf_op jit(solution)/shard_map/reduce_sum | solution.py:239
  32.7 1.2 %multiply_reduce_fusion.16 = (f32[2,256]{1,0:T(2,128)S(1)}, f32[2,256]{1,0:T(2,128)S(1)}) fusion(f32[2,256]{1,0:T(2,128)S(1)} %get-tuple-element.129, f32[256,256]{1,0:T(8,128)} %copy-done, f32[256,256]{1,0:T(8,128)S(1)} %get-tuple-element.165), kind=kLoop, calls=%fused_computation.58 | loop fusion | flops 523264 | bytes 530432 | tf_op jit(solution)/shard_map/reduce_sum | solution.py:239
  34.7 0.4 %multiply_reduce_fusion.1 = (f32[2,512]{1,0:T(2,128)S(1)}, f32[2,512]{1,0:T(2,128)S(1)}) fusion(f32[2,512]{1,0:T(2,128)S(1)} %get-tuple-element.132, f32[512,512]{1,0:T(8,128)S(1)} %get-tuple-element.146, f32[512,512]{1,0:T(8,128)S(1)} %get-tuple-element.145), kind=kLoop, calls=%fused_computation.1 | loop fusion | flops 2095104 | bytes 2109440 | tf_op jit(solution)/shard_map/reduce_sum | solution.py:239
  35.9 1.3 %fusion.9 = (f32[64]{0:T(128)S(1)}, f32[64]{0:T(128)S(1)}, f32[64]{0:T(128)S(1)}, f32[64]{0:T(128)S(1)}, f32[64]{0:T(128)S(1)}, /*index=5*/f32[64]{0:T(128)S(1)}...) fusion(f32[2048]{0:T(1024)S(1)} %bitcast.83, ...), kind=kLoop, calls=%fused_computation.45 | loop fusion | flops 6683904 | bytes 69888 | tf_op jit(solution)/shard_map/reduce_sum | solution.py:136
  37.6 0.6 %reshape_multiply_fusion = f32[3,1,1,64]{3,2,1,0:T(1,128)} fusion(f32[3,64]{1,0:T(4,128)S(1)} %fusion.42, f32[64]{0:T(128)S(1)} %fusion.59), kind=kLoop, calls=%fused_computation.240 | loop fusion | flops 192 | bytes 1792 | tf_op jit(solution)/shard_map/mul | solution.py:281
  (109 shorter events, 5.7 us)
Async XLA Ops:
  2.2 14.6 %all-to-all-start = ((f32[32,1,384]{2,1,0:T(1,128)}), f32[32,1,384]{2,1,0:T(1,128)S(1)}, u32[]{:S(2)}, u32[]{:S(2)}) async-start(f32[32,1,384]{2,1,0:T(1,128)} %shard_map.77), calls=%async_computation | async-start | bytes 98304 | tf_op jit(solution)/shard_map/all_to_all | solution.py:154
  18.3 6.7 %copy-start = (f32[256,256]{1,0:T(8,128)}, f32[256,256]{1,0:T(8,128)S(1)}, u32[]{:S(2)}) copy-start(f32[256,256]{1,0:T(8,128)S(1)} %get-tuple-element.166) | copy-start | bytes 786436
  18.3 6.7 %copy-start.1 = (f32[256,256]{1,0:T(8,128)}, f32[256,256]{1,0:T(8,128)S(1)}, u32[]{:S(2)}) copy-start(f32[256,256]{1,0:T(8,128)S(1)} %get-tuple-element.164) | copy-start | bytes 786436
  18.9 6.5 %copy-start.2 = (f32[256,256]{1,0:T(8,128)}, f32[256,256]{1,0:T(8,128)S(1)}, u32[]{:S(2)}) copy-start(f32[256,256]{1,0:T(8,128)S(1)} %get-tuple-element.168) | copy-start | bytes 786436
  18.9 6.5 %copy-start.4 = (f32[256,256]{1,0:T(8,128)}, f32[256,256]{1,0:T(8,128)S(1)}, u32[]{:S(2)}) copy-start(f32[256,256]{1,0:T(8,128)S(1)} %get-tuple-element.169) | copy-start | bytes 786436
  18.9 6.5 %copy-start.6 = (f32[256,256]{1,0:T(8,128)}, f32[256,256]{1,0:T(8,128)S(1)}, u32[]{:S(2)}) copy-start(f32[256,256]{1,0:T(8,128)S(1)} %get-tuple-element.167) | copy-start | bytes 786436
  22.8 1.2 %collective-permute-start = (f32[2,2048]{1,0:T(2,128)S(1)}, f32[2,2048]{1,0:T(2,128)S(1)}, u32[]{:S(2)}, u32[]{:S(2)}) collective-permute-start(f32[2,2048]{1,0:T(2,128)S(1)} %constant_dynamic-update-slice_fusion.14), channel_id=1, source_target_pairs={{0,1},{1,0},{2,3},{3,2},{4,5},{5,4},{6,7},{7,6},{8,9},{9,8},{10,11... | collective-permute-start | bytes 49160 | tf_op jit(solution)/shard_map/ppermute | solution.py:232
  24.5 0.5 %copy-start.8 = (f32[2]{0:T(128)}, f32[2]{0:T(128)S(1)}, u32[]{:S(2)}) copy-start(f32[2]{0:T(128)S(1)} %get-tuple-element.81) | copy-start | bytes 28
  27.2 1.2 %collective-permute-start.1 = (f32[2,2048]{1,0:T(2,128)S(1)}, f32[2,2048]{1,0:T(2,128)S(1)}, u32[]{:S(2)}, u32[]{:S(2)}) collective-permute-start(f32[2,2048]{1,0:T(2,128)S(1)} %constant_dynamic-update-slice_fusion), channel_id=1, source_target_pairs={{0,1},{1,0},{2,3},{3,2},{4,5},{5,4},{6,7},{7,6},{8,9},{9,8},{10,11... | collective-permute-start | bytes 49160 | tf_op jit(solution)/shard_map/ppermute | solution.py:232
  28.4 5.5 %copy-start.3 = (f32[256,256]{1,0:T(8,128)S(1)}, f32[256,256]{1,0:T(8,128)}, u32[]{:S(2)}) copy-start(f32[256,256]{1,0:T(8,128)} %copy-done.2) | copy-start | bytes 786436
  28.4 5.5 %copy-start.5 = (f32[256,256]{1,0:T(8,128)S(1)}, f32[256,256]{1,0:T(8,128)}, u32[]{:S(2)}) copy-start(f32[256,256]{1,0:T(8,128)} %copy-done.4) | copy-start | bytes 786436
  34.6 1.2 %copy-start.9 = (f32[64]{0:T(128)S(1)}, f32[64]{0:T(128)}, u32[]{:S(2)}) copy-start(f32[64]{0:T(128)} %get-tuple-element.156) | copy-start | bytes 772
  34.6 1.2 %copy-start.10 = (f32[64]{0:T(128)S(1)}, f32[64]{0:T(128)}, u32[]{:S(2)}) copy-start(f32[64]{0:T(128)} %get-tuple-element.157) | copy-start | bytes 772
  34.6 1.2 %copy-start.11 = (f32[64]{0:T(128)S(1)}, f32[64]{0:T(128)}, u32[]{:S(2)}) copy-start(f32[64]{0:T(128)} %get-tuple-element.158) | copy-start | bytes 772
  34.6 1.2 %copy-start.12 = (f32[64]{0:T(128)S(1)}, f32[64]{0:T(128)}, u32[]{:S(2)}) copy-start(f32[64]{0:T(128)} %get-tuple-element.159) | copy-start | bytes 772
  34.6 1.2 %copy-start.13 = (s32[64]{0:T(128)S(1)}, s32[64]{0:T(128)}, u32[]{:S(2)}) copy-start(s32[64]{0:T(128)} %iota_add_fusion) | copy-start | bytes 772
  35.5 1.7 %collective-permute-start.2 = (f32[2]{0:T(128)S(1)}, f32[2]{0:T(128)S(1)}, u32[]{:S(2)}, u32[]{:S(2)}) collective-permute-start(f32[2]{0:T(128)S(1)} %multiply_add_fusion.2), channel_id=1, source_target_pairs={{0,1},{1,0},{2,3},{3,2},{4,5},{5,4},{6,7},{7,6},{8,9},{9,8},{10,11... | collective-permute-start | bytes 32 | tf_op jit(solution)/shard_map/ppermute | solution.py:241
  37.5 0.7 %copy-start.7 = (f32[64]{0:T(128)}, f32[64]{0:T(128)S(1)}, u32[]{:S(2)}) copy-start(f32[64]{0:T(128)S(1)} %fusion.59) | copy-start | bytes 772
